TPU v7x, 512 devices: a whole 4x8x8 slice. The times are simulated.
512 devices in a mesh: band: 32 (over x, y), seq: 16 (over z, core).
Axes of the slice: x: 4, y: 8, z: 8, core: 2. Of those that a mesh axis runs over, the one named last changes fastest.
Arguments:
- posteriors: bfloat16 [32, 262144], P(None, ('band', 'seq'))
- seed_mask: int32 [262144], P(('band', 'seq')), may hold values 0 or 1
- frame_perm: int32 [512, 512], P(('band', 'seq')), may hold values from 0 to 511, each once within a row
- lengths: int32 [256], replicated, may hold values from 1 to 4096, 262144 in all
- embeddings: bfloat16 [262144, 256], P(('band', 'seq')), may hold values from -12 to 12
- partners: int32 [2048, 32], P(('band', 'seq')), may hold values from 0 to 127, as said below
- levels: int32 [2048, 32], P(('band', 'seq')), may hold values from 1 to 8, as said below
Outputs:
- spread_labels: float32 [32, 262144], P(None, ('band', 'seq'))
Inputs may be any that keep to these rules, and one draw needn't show every extreme that they name: `partners`: within each seq index s, slot k pairs the 128 tiles mutually: if tile number a names b in slot k then b names a in slot k; no tile names itself. `levels`: two tiles paired in slot k carry the same level.
All inputs are finite; a program needn't handle non-finite values. No bound on the sum of `seed_mask` on one device may be relied on, other than what follows from the above.
Results may differ from a plain program's by a relative error of at most 0.007.
Values may be sent and summed in bfloat16 or wider, within the bound.
No kernel may reach another device: no remote copies, remote signals or barrier semaphores. Data moves between devices by JAX's collectives and lax.ppermute only.
A program may use at most 64 MiB of HBM per device.

v0:
```python
import math

import jax
import jax.numpy as jnp
from jax import lax
from jax.sharding import PartitionSpec as P

RADIUS = 64
ITERS = 3


decay_len = 16.0
spread_rate = 0.9


def with_halo(cells, sides, width):
    for axis, dim in sides:
        count = lax.axis_size(axis)
        ends = count - 1
        head = lax.slice_in_dim(cells, 0, width, axis=dim)
        tail = lax.slice_in_dim(cells, cells.shape[dim] - width, cells.shape[dim], axis=dim)
        cells = jnp.concatenate(
            [
                lax.ppermute(tail, axis, [(i, (i + 1) % count) for i in range(ends)]),
                cells,
                lax.ppermute(head, axis, [((i + 1) % count, i) for i in range(ends)]),
            ],
            axis=dim,
        )
    return cells


def total_over_devices(values):
    for axis in ("seq", "band"):
        count = lax.axis_size(axis)
        spread = jnp.broadcast_to(values[None], (count,) + values.shape)
        rows = lax.all_to_all(spread, axis, split_axis=0, concat_axis=0, tiled=True)
        values = jnp.sum(rows, axis=0)
    return values


def band_gather(block):
    count = lax.axis_size("band")
    spread = jnp.broadcast_to(block[None], (count,) + block.shape)
    return lax.all_to_all(spread, "band", split_axis=0, concat_axis=0, tiled=True)


def on_device(posteriors, seed_mask, frame_perm, lengths, embeddings, partners, levels):
    channels, frames = posteriors.shape
    band_count = lax.axis_size("band")
    groups = lax.axis_size("seq")
    tile_count = frames // 128
    seeded = posteriors * seed_mask.astype(jnp.bfloat16)[None, :]
    ordered = jnp.take(seeded, frame_perm[0], axis=1).reshape(
        channels, band_count, frames // band_count
    )
    arrived = lax.all_to_all(ordered, "band", split_axis=1, concat_axis=1, tiled=True)
    labels = arrived.reshape(channels, frames).astype(jnp.float32)
    device = lax.axis_index("band") * groups + lax.axis_index("seq")
    frame_total = frames * band_count * groups
    window = 128 + 2 * RADIUS
    global_at = device * frames - RADIUS + jnp.arange(frames + 2 * RADIUS, dtype=jnp.int32)
    utt_ends = jnp.cumsum(lengths)
    owner_seg = jnp.sum((utt_ends[None, :] <= global_at[:, None]).astype(jnp.int32), axis=1)
    inside = (global_at >= 0) & (global_at < frame_total)
    tile_off = (jnp.arange(tile_count, dtype=jnp.int32) * 128)[:, None, None]
    win_pos = tile_off + jnp.arange(window, dtype=jnp.int32)[None, :, None]
    row_pos = tile_off + RADIUS + jnp.arange(128, dtype=jnp.int32)[None, None, :]
    offset = jnp.abs(win_pos - row_pos)
    linked = (
        (offset >= 1)
        & (offset <= RADIUS)
        & (owner_seg[win_pos] == owner_seg[row_pos])
        & inside[win_pos]
    )
    band_tiles = jnp.where(
        linked, jnp.exp(-offset.astype(jnp.float32) / decay_len), jnp.float32(0.0)
    ).astype(jnp.bfloat16)
    near_degree = jnp.sum(band_tiles.astype(jnp.float32), axis=1).reshape(frames)
    gathered = lax.all_gather(embeddings, "band", axis=0, tiled=True)
    embed_width = embeddings.shape[1]
    partner_rows = gathered.reshape(-1, 128, embed_width)[partners]
    own_rows = embeddings.reshape(tile_count, 128, embed_width)
    inner_prod = jnp.einsum(
        "tkje,tie->tkji", partner_rows, own_rows, preferred_element_type=jnp.float32
    )
    affinity = (
        jnp.exp(0.5 * (inner_prod / math.sqrt(embed_width)))
        * (levels.astype(jnp.float32) / 8.0)[:, :, None, None]
        / 128.0
    )
    affinity = affinity.astype(jnp.bfloat16)
    far_degree = jnp.sum(affinity.astype(jnp.float32), axis=(1, 2)).reshape(frames)
    norm_scale = 1.0 / jnp.sqrt(near_degree + far_degree)

    def squares(residual):
        return total_over_devices(jnp.sum(residual * residual, axis=1))

    solution = jnp.zeros((channels, frames), jnp.float32)
    residual = labels
    direction = labels
    first_norm = jnp.sum(residual * residual, axis=1)
    for iteration in range(ITERS):
        lifted = (norm_scale[None, :] * direction).astype(jnp.bfloat16)
        padded = with_halo(lifted, ((("band", "seq"), 1),), RADIUS)
        windows = jnp.stack(
            [padded[:, position * 128 : position * 128 + window] for position in range(tile_count)],
            axis=0,
        )
        near_term = jnp.einsum(
            "tcw,twa->cta", windows, band_tiles, preferred_element_type=jnp.float32
        ).reshape(channels, frames)
        spread = jnp.transpose(band_gather(lifted), (1, 0, 2)).reshape(channels, -1, 128)
        far_tiles = spread[:, partners]
        far_term = jnp.einsum(
            "ctkj,tkji->cti", far_tiles, affinity, preferred_element_type=jnp.float32
        ).reshape(channels, frames)
        image = direction - spread_rate * norm_scale[None, :] * (near_term + far_term)
        curve = jnp.sum(direction * image, axis=1)
        if iteration == 0:
            both = total_over_devices(jnp.stack([first_norm, curve]))
            norm_now, curve = both[0], both[1]
        else:
            curve = total_over_devices(curve)
        alpha = norm_now / curve
        solution = solution + alpha[:, None] * direction
        residual = residual - alpha[:, None] * image
        norm_next = squares(residual)
        direction = residual + (norm_next / norm_now)[:, None] * direction
        norm_now = norm_next
    return solution


def solution(mesh):
    placed = (
        P(None, ("band", "seq")),
        P(("band", "seq")),
        P(("band", "seq"), None),
        P(),
        P(("band", "seq"), None),
        P(("band", "seq"), None),
        P(("band", "seq"), None),
    )
    return jax.shard_map(
        on_device, mesh=mesh, in_specs=placed, out_specs=P(None, ("band", "seq")), check_vma=False
    )
```

profile of v0, /device:TPU:6, one launch (start us, length us, event | category | flops | bytes accessed | tf_op | source)
XLA Modules:
  0.0 399.9 jit_solution(14003725385219385086)
XLA Ops:
  9.4 1.3 reduce.19
  11.5 1.3 gather_fusion
  13.7 10.2 %all-to-all-start = ((bf16[32,2,256]{2,1,0:T(2,128)(2,1)}), bf16[32,2,256]{2,1,0:T(2,128)(2,1)S(1)}, u32[]{:S(2)}, u32[]{:S(2)}) async-start(bf16[32,2,256]{2,1,0:T(2,128)(2,1)} %reshape.782), calls=%async_computation | async-start | bytes 65536 | tf_op jit(solution)/shard_map/all_to_all | solution.py:57
  24.0 1.0 reduce-window.9
  25.7 4.5 %gather_fusion.1 = s32[1024]{0:T(1024)S(1)} fusion(s32[640]{0:T(1024)S(1)} %convert_reduce_fusion.1, s32[1024]{0:T(1024)S(1)} %broadcast_clamp_fusion), kind=kCustom, calls=%fused_computation.1 | custom fusion | bytes 12288 | tf_op jit(solution)/shard_map/gather | solution.py:73
  30.3 2.3 gather_fusion.2
  32.6 6.8 %gather_fusion.3 = pred[1024]{0:T(1024)(128)(4,1)S(1)} fusion(pred[640]{0:T(1024)(128)(4,1)S(1)} %compare_and_fusion.1, s32[1024]{0:T(1024)S(1)} %broadcast_clamp_fusion), kind=kCustom, calls=%fused_computation.3 | custom fusion | bytes 6144 | tf_op jit(solution)/shard_map/gather | solution.py:74
  40.6 76.2 %all-gather.2.cloned.1.call-done = bf16[16384,256]{1,0:T(8,128)(2,1)} async-done(((bf16[512,256]{1,0:T(8,128)(2,1)}), bf16[16384,256]{1,0:T(8,128)(2,1)}) %all-gather.2.cloned.1.call-update) | async-done | bytes 8388624 | tf_op jit(solution)/shard_map/all_gather | solution.py:80
  116.7 10.0 %gather_fusion.4 = bf16[128,128,256]{2,1,0:T(8,128)(2,1)} fusion(bf16[128,128,256]{2,1,0:T(8,128)(2,1)} %bitcast.164, s32[1024]{0:T(1024)S(1)} %pad_clamp_fusion), kind=kCustom, calls=%fused_computation.4 | custom fusion | bytes 16777728 | tf_op jit(solution)/shard_map/gather | solution.py:82
  126.7 7.7 %convert_reduce_fusion = (f32[4,128]{1,0:T(4,128)S(1)}, bf16[4,32,128,128]{3,2,1,0:T(8,128)(2,1)}) fusion(f32[4,32]{1,0:T(4,128)S(1)} %convert_multiply_fusion.3, bf16[4,32,128,256]{3,2,1,0:T(8,128)(2,1)} %bitcast.165, bf16[4,128,256,1]{2,1,3,0:T(8,128)(2,1)S(1)} %bitcast.179), kind=kOutput, calls=%fused_computation.8 | convolution fusion | flops 1086324224 | bytes 12847616 | tf_op jit(solution)/shard_map/tkje,tie->tkji/dot_general | solution.py:84
  135.0 1.1 broadcast_in_dim.46
  136.1 8.0 %all-to-all-start.1 = ((bf16[32,32,512]{2,1,0:T(8,128)(2,1)}), bf16[32,32,512]{2,1,0:T(8,128)(2,1)S(1)}, u32[]{:S(2)}, u32[]{:S(2)}) async-start(bf16[32,32,512]{2,1,0:T(8,128)(2,1)} %broadcast_in_dim.46), calls=%async_computation.1 | async-start | bytes 2097152 | tf_op jit(solution)/shard_map/all_to_all | solution.py:45
  144.2 1.9 collective-permute-start
  146.1 7.9 %collective-permute-start.1 = (bf16[32,64]{1,0:T(8,128)(2,1)S(1)}, bf16[32,64]{1,0:T(8,128)(2,1)S(1)}, u32[]{:S(2)}, u32[]{:S(2)}) collective-permute-start(bf16[32,64]{1,0:T(8,128)(2,1)S(1)} %get-tuple-element.28), channel_id=1, source_target_pairs={{1,0},{2,1},{3,2},{4,3},{5,4},{6,5},{7,6},{8,7},{9,8},{10,9},{11,1... | collective-permute-start | bytes 12296 | tf_op jit(solution)/shard_map/ppermute | solution.py:26
  154.0 13.1 %collective-permute-done = bf16[32,64]{1,0:T(8,128)(2,1)S(1)} collective-permute-done((bf16[32,64]{1,0:T(8,128)(2,1)S(1)}, bf16[32,64]{1,0:T(8,128)(2,1)S(1)}, u32[]{:S(2)}, u32[]{:S(2)}) %collective-permute-start) | collective-permute-done | bytes 4128 | tf_op jit(solution)/shard_map/ppermute | solution.py:24
  167.9 2.3 all-to-all-done.1
  173.0 2.9 fusion.3
  176.2 14.9 %all_to_all.78 = f32[16,2,32]{2,1,0:T(2,128)S(1)} all-to-all(f32[16,2,32]{2,1,0:T(2,128)S(1)} %broadcast_in_dim.47), channel_id=1, replica_groups=mesh['band'=32,'seq'=16] {'seq'}, dimensions={0} | all-to-all | bytes 8192 | tf_op jit(solution)/shard_map/all_to_all | solution.py:37
  191.2 14.9 %all_to_all.79 = f32[32,2,32]{2,1,0:T(2,128)S(1)} all-to-all(f32[32,2,32]{2,1,0:T(2,128)S(1)} %broadcast_in_dim.48), channel_id=1, replica_groups=mesh['band'=32,'seq'=16] {'band'}, dimensions={0} | all-to-all | bytes 16384 | tf_op jit(solution)/shard_map/all_to_all | solution.py:37
  206.4 10.1 %all_to_all.80 = f32[16,1,32]{2,1,0:T(1,128)S(1)} all-to-all(f32[16,1,32]{2,1,0:T(1,128)S(1)} %broadcast_in_dim.49), channel_id=1, replica_groups=mesh['band'=32,'seq'=16] {'seq'}, dimensions={0} | all-to-all | bytes 4096 | tf_op jit(solution)/shard_map/all_to_all | solution.py:37
  216.5 12.7 %all_to_all.81 = f32[32,1,32]{2,1,0:T(1,128)S(1)} all-to-all(f32[32,1,32]{2,1,0:T(1,128)S(1)} %broadcast_in_dim.50), channel_id=1, replica_groups=mesh['band'=32,'seq'=16] {'band'}, dimensions={0} | all-to-all | bytes 8192 | tf_op jit(solution)/shard_map/all_to_all | solution.py:37
  229.3 0.9 multiply_convert_fusion.2
  230.2 1.1 broadcast_in_dim.51
  231.3 5.9 %all-to-all-start.6 = ((bf16[32,32,512]{2,1,0:T(8,128)(2,1)}), bf16[32,32,512]{2,1,0:T(8,128)(2,1)S(1)}, u32[]{:S(2)}, u32[]{:S(2)}) async-start(bf16[32,32,512]{2,1,0:T(8,128)(2,1)} %broadcast_in_dim.51), calls=%async_computation.6 | async-start | bytes 2097152 | tf_op jit(solution)/shard_map/all_to_all | solution.py:45
  237.3 1.9 collective-permute-start.2
  239.2 7.9 %collective-permute-start.3 = (bf16[32,64]{1,0:T(8,128)(2,1)S(1)}, bf16[32,64]{1,0:T(8,128)(2,1)S(1)}, u32[]{:S(2)}, u32[]{:S(2)}) collective-permute-start(bf16[32,64]{1,0:T(8,128)(2,1)S(1)} %get-tuple-element.22), channel_id=1, source_target_pairs={{1,0},{2,1},{3,2},{4,3},{5,4},{6,5},{7,6},{8,7},{9,8},{10,9},{11,1... | collective-permute-start | bytes 12296 | tf_op jit(solution)/shard_map/ppermute | solution.py:26
  247.0 9.7 %collective-permute-done.2 = bf16[32,64]{1,0:T(8,128)(2,1)S(1)} collective-permute-done((bf16[32,64]{1,0:T(8,128)(2,1)S(1)}, bf16[32,64]{1,0:T(8,128)(2,1)S(1)}, u32[]{:S(2)}, u32[]{:S(2)}) %collective-permute-start.2) | collective-permute-done | bytes 4128 | tf_op jit(solution)/shard_map/ppermute | solution.py:24
  257.4 2.1 fusion.14
  259.5 3.5 all-to-all-done.6
  264.9 0.9 gather_fusion.6
  265.8 2.9 fusion.2
  269.8 11.0 %all_to_all.82 = f32[16,1,32]{2,1,0:T(1,128)S(1)} all-to-all(f32[16,1,32]{2,1,0:T(1,128)S(1)} %broadcast_in_dim.52), channel_id=1, replica_groups=mesh['band'=32,'seq'=16] {'seq'}, dimensions={0} | all-to-all | bytes 4096 | tf_op jit(solution)/shard_map/all_to_all | solution.py:37
  280.8 16.2 %all_to_all.83 = f32[32,1,32]{2,1,0:T(1,128)S(1)} all-to-all(f32[32,1,32]{2,1,0:T(1,128)S(1)} %broadcast_in_dim.53), channel_id=1, replica_groups=mesh['band'=32,'seq'=16] {'band'}, dimensions={0} | all-to-all | bytes 8192 | tf_op jit(solution)/shard_map/all_to_all | solution.py:37
  298.6 10.1 %all_to_all.84 = f32[16,1,32]{2,1,0:T(1,128)S(1)} all-to-all(f32[16,1,32]{2,1,0:T(1,128)S(1)} %broadcast_in_dim.54), channel_id=1, replica_groups=mesh['band'=32,'seq'=16] {'seq'}, dimensions={0} | all-to-all | bytes 4096 | tf_op jit(solution)/shard_map/all_to_all | solution.py:37
  308.8 12.7 %all_to_all.85 = f32[32,1,32]{2,1,0:T(1,128)S(1)} all-to-all(f32[32,1,32]{2,1,0:T(1,128)S(1)} %broadcast_in_dim.55), channel_id=1, replica_groups=mesh['band'=32,'seq'=16] {'band'}, dimensions={0} | all-to-all | bytes 8192 | tf_op jit(solution)/shard_map/all_to_all | solution.py:37
  322.1 1.6 multiply_convert_fusion.1
  323.7 1.1 broadcast_in_dim.56
  324.8 5.9 %all-to-all-start.11 = ((bf16[32,32,512]{2,1,0:T(8,128)(2,1)}), bf16[32,32,512]{2,1,0:T(8,128)(2,1)S(1)}, u32[]{:S(2)}, u32[]{:S(2)}) async-start(bf16[32,32,512]{2,1,0:T(8,128)(2,1)} %broadcast_in_dim.56), calls=%async_computation.11 | async-start | bytes 2097152 | tf_op jit(solution)/shard_map/all_to_all | solution.py:45
  330.8 1.9 collective-permute-start.4
  332.7 7.9 %collective-permute-start.5 = (bf16[32,64]{1,0:T(8,128)(2,1)S(1)}, bf16[32,64]{1,0:T(8,128)(2,1)S(1)}, u32[]{:S(2)}, u32[]{:S(2)}) collective-permute-start(bf16[32,64]{1,0:T(8,128)(2,1)S(1)} %get-tuple-element.16), channel_id=1, source_target_pairs={{1,0},{2,1},{3,2},{4,3},{5,4},{6,5},{7,6},{8,7},{9,8},{10,9},{11,1... | collective-permute-start | bytes 12296 | tf_op jit(solution)/shard_map/ppermute | solution.py:26
  340.5 9.7 %collective-permute-done.4 = bf16[32,64]{1,0:T(8,128)(2,1)S(1)} collective-permute-done((bf16[32,64]{1,0:T(8,128)(2,1)S(1)}, bf16[32,64]{1,0:T(8,128)(2,1)S(1)}, u32[]{:S(2)}, u32[]{:S(2)}) %collective-permute-start.4) | collective-permute-done | bytes 4128 | tf_op jit(solution)/shard_map/ppermute | solution.py:24
  350.9 2.1 fusion.15
  353.0 3.5 all-to-all-done.11
  359.3 2.9 fusion.1
  362.4 0.9 fusion.12
  363.4 11.0 %all_to_all.86 = f32[16,1,32]{2,1,0:T(1,128)S(1)} all-to-all(f32[16,1,32]{2,1,0:T(1,128)S(1)} %broadcast_in_dim.57), channel_id=1, replica_groups=mesh['band'=32,'seq'=16] {'seq'}, dimensions={0} | all-to-all | bytes 4096 | tf_op jit(solution)/shard_map/all_to_all | solution.py:37
  374.4 16.2 %all_to_all.87 = f32[32,1,32]{2,1,0:T(1,128)S(1)} all-to-all(f32[32,1,32]{2,1,0:T(1,128)S(1)} %broadcast_in_dim.58), channel_id=1, replica_groups=mesh['band'=32,'seq'=16] {'band'}, dimensions={0} | all-to-all | bytes 8192 | tf_op jit(solution)/shard_map/all_to_all | solution.py:37
  391.4 1.6 multiply_add_fusion
  (136 shorter events, 21.4 us)
Async XLA Ops:
  6.5 32.9 %copy-start.14 = (s32[4,32]{1,0:T(4,128)S(1)}, s32[4,32]{1,0:T(4,128)}, u32[]{:S(2)}) copy-start(s32[4,32]{1,0:T(4,128)} %param.12) | copy-start | bytes 1540
  6.5 33.7 %copy-start.15 = (s32[4,32]{1,0:T(4,128)S(1)}, s32[4,32]{1,0:T(4,128)}, u32[]{:S(2)}) copy-start(s32[4,32]{1,0:T(4,128)} %param.13) | copy-start | bytes 1540
  6.5 110.2 %all-gather.2.cloned.1.call-start = ((), (), s32[]{:S(2)}) async-start(), calls=%async_computation.14 | async-start | bytes 8650752 | tf_op jit(solution)/shard_map/all_gather | solution.py:80
  13.7 26.6 %all-to-all-start = ((bf16[32,2,256]{2,1,0:T(2,128)(2,1)}), bf16[32,2,256]{2,1,0:T(2,128)(2,1)S(1)}, u32[]{:S(2)}, u32[]{:S(2)}) async-start(bf16[32,2,256]{2,1,0:T(2,128)(2,1)} %reshape.782), calls=%async_computation | async-start | bytes 65536 | tf_op jit(solution)/shard_map/all_to_all | solution.py:57
  30.2 137.1 %copy-start.11 = (s32[4,256]{1,0:T(4,128)}, s32[4,256]{1,0:T(4,128)S(1)}, u32[]{:S(2)}) copy-start(s32[4,256]{1,0:T(4,128)S(1)} %eq.17) | copy-start | bytes 12292
  32.6 134.7 %copy-start.16 = (s32[512]{0:T(512)}, s32[512]{0:T(512)S(1)}, u32[]{:S(2)}) copy-start(s32[512]{0:T(512)S(1)} %gather_fusion.2) | copy-start | bytes 6148
  39.5 127.8 %copy-start.17 = (pred[4,256]{1,0:T(4,128)(4,1)}, pred[4,256]{1,0:T(4,128)(4,1)S(1)}, u32[]{:S(2)}) copy-start(pred[4,256]{1,0:T(4,128)(4,1)S(1)} %and.33) | copy-start | bytes 3076
  39.6 127.7 %copy-start.13 = (s32[4,128]{1,0:T(4,128)}, s32[4,128]{1,0:T(4,128)S(1)}, u32[]{:S(2)}) copy-start(s32[4,128]{1,0:T(4,128)S(1)} %iota_add_fusion.2) | copy-start | bytes 6148
  39.7 127.6 %copy-start.10 = (s32[4,256]{1,0:T(4,128)}, s32[4,256]{1,0:T(4,128)S(1)}, u32[]{:S(2)}) copy-start(s32[4,256]{1,0:T(4,128)S(1)} %iota_add_fusion.1) | copy-start | bytes 12292
  40.3 131.9 %copy-start.5 = (s32[1024]{0:T(1024)}, s32[1024]{0:T(1024)S(1)}, u32[]{:S(2)}) copy-start(s32[1024]{0:T(1024)S(1)} %pad_clamp_fusion) | copy-start | bytes 12292
  40.6 94.4 %copy-start.3 = (f32[32,512]{1,0:T(8,128)}, f32[32,512]{1,0:T(8,128)S(1)}, u32[]{:S(2)}) copy-start(f32[32,512]{1,0:T(8,128)S(1)} %copy.88) | copy-start | bytes 196612
  116.7 10.0 %copy-start.4 = (bf16[512,256]{1,0:T(8,128)(2,1)S(1)}, bf16[512,256]{1,0:T(8,128)(2,1)}, u32[]{:S(2)}) copy-start(bf16[512,256]{1,0:T(8,128)(2,1)} %param.11) | copy-start | bytes 786436
  135.0 40.9 %copy-start.6 = (f32[512]{0:T(512)}, f32[512]{0:T(512)S(1)}, u32[]{:S(2)}) copy-start(f32[512]{0:T(512)S(1)} %get-tuple-element.10) | copy-start | bytes 6148
  136.1 34.1 %all-to-all-start.1 = ((bf16[32,32,512]{2,1,0:T(8,128)(2,1)}), bf16[32,32,512]{2,1,0:T(8,128)(2,1)S(1)}, u32[]{:S(2)}, u32[]{:S(2)}) async-start(bf16[32,32,512]{2,1,0:T(8,128)(2,1)} %broadcast_in_dim.46), calls=%async_computation.1 | async-start | bytes 2097152 | tf_op jit(solution)/shard_map/all_to_all | solution.py:45
  144.2 23.0 %collective-permute-start = (bf16[32,64]{1,0:T(8,128)(2,1)S(1)}, bf16[32,64]{1,0:T(8,128)(2,1)S(1)}, u32[]{:S(2)}, u32[]{:S(2)}) collective-permute-start(bf16[32,64]{1,0:T(8,128)(2,1)S(1)} %get-tuple-element.27), channel_id=1, source_target_pairs={{0,1},{1,2},{2,3},{3,4},{4,5},{5,6},{6,7},{7,8},{8,9},{9,10},{10,1... | collective-permute-start | bytes 12296 | tf_op jit(solution)/shard_map/ppermute | solution.py:24
  146.1 21.1 %collective-permute-start.1 = (bf16[32,64]{1,0:T(8,128)(2,1)S(1)}, bf16[32,64]{1,0:T(8,128)(2,1)S(1)}, u32[]{:S(2)}, u32[]{:S(2)}) collective-permute-start(bf16[32,64]{1,0:T(8,128)(2,1)S(1)} %get-tuple-element.28), channel_id=1, source_target_pairs={{1,0},{2,1},{3,2},{4,3},{5,4},{6,5},{7,6},{8,7},{9,8},{10,9},{11,1... | collective-permute-start | bytes 12296 | tf_op jit(solution)/shard_map/ppermute | solution.py:26
  175.9 55.4 %copy-start.2 = (f32[4,128,32]{1,2,0:T(8,128)}, f32[4,128,32]{1,2,0:T(8,128)S(1)}, u32[]{:S(2)}) copy-start(f32[4,128,32]{1,2,0:T(8,128)S(1)} %fusion.3) | copy-start | bytes 196612
  206.2 25.1 %copy-start.7 = (f32[32]{0:T(128)}, f32[32]{0:T(128)S(1)}, u32[]{:S(2)}) copy-start(f32[32]{0:T(128)S(1)} %bitcast_divide_fusion) | copy-start | bytes 388
  229.2 2.1 copy-start.19
  229.3 2.0 copy-start.8
  231.3 31.7 %all-to-all-start.6 = ((bf16[32,32,512]{2,1,0:T(8,128)(2,1)}), bf16[32,32,512]{2,1,0:T(8,128)(2,1)S(1)}, u32[]{:S(2)}, u32[]{:S(2)}) async-start(bf16[32,32,512]{2,1,0:T(8,128)(2,1)} %broadcast_in_dim.51), calls=%async_computation.6 | async-start | bytes 2097152 | tf_op jit(solution)/shard_map/all_to_all | solution.py:45
  237.3 19.5 %collective-permute-start.2 = (bf16[32,64]{1,0:T(8,128)(2,1)S(1)}, bf16[32,64]{1,0:T(8,128)(2,1)S(1)}, u32[]{:S(2)}, u32[]{:S(2)}) collective-permute-start(bf16[32,64]{1,0:T(8,128)(2,1)S(1)} %get-tuple-element.21), channel_id=1, source_target_pairs={{0,1},{1,2},{2,3},{3,4},{4,5},{5,6},{6,7},{7,8},{8,9},{9,10},{10,1... | collective-permute-start | bytes 12296 | tf_op jit(solution)/shard_map/ppermute | solution.py:24
  239.2 18.1 %collective-permute-start.3 = (bf16[32,64]{1,0:T(8,128)(2,1)S(1)}, bf16[32,64]{1,0:T(8,128)(2,1)S(1)}, u32[]{:S(2)}, u32[]{:S(2)}) collective-permute-start(bf16[32,64]{1,0:T(8,128)(2,1)S(1)} %get-tuple-element.22), channel_id=1, source_target_pairs={{1,0},{2,1},{3,2},{4,3},{5,4},{6,5},{7,6},{8,7},{9,8},{10,9},{11,1... | collective-permute-start | bytes 12296 | tf_op jit(solution)/shard_map/ppermute | solution.py:26
  268.9 55.9 %copy-start = (f32[32,4,128]{0,2,1:T(8,128)}, f32[32,4,128]{0,2,1:T(8,128)S(1)}, u32[]{:S(2)}) copy-start(f32[32,4,128]{0,2,1:T(8,128)S(1)} %copy.103) | copy-start | bytes 196612
  297.7 27.1 %copy-start.9 = (f32[32]{0:T(128)}, f32[32]{0:T(128)S(1)}, u32[]{:S(2)}) copy-start(f32[32]{0:T(128)S(1)} %div.65) | copy-start | bytes 388
  321.5 3.3 copy-start.18
  322.1 2.7 copy-start.12
  324.8 31.7 %all-to-all-start.11 = ((bf16[32,32,512]{2,1,0:T(8,128)(2,1)}), bf16[32,32,512]{2,1,0:T(8,128)(2,1)S(1)}, u32[]{:S(2)}, u32[]{:S(2)}) async-start(bf16[32,32,512]{2,1,0:T(8,128)(2,1)} %broadcast_in_dim.56), calls=%async_computation.11 | async-start | bytes 2097152 | tf_op jit(solution)/shard_map/all_to_all | solution.py:45
  330.8 19.5 %collective-permute-start.4 = (bf16[32,64]{1,0:T(8,128)(2,1)S(1)}, bf16[32,64]{1,0:T(8,128)(2,1)S(1)}, u32[]{:S(2)}, u32[]{:S(2)}) collective-permute-start(bf16[32,64]{1,0:T(8,128)(2,1)S(1)} %get-tuple-element.15), channel_id=1, source_target_pairs={{0,1},{1,2},{2,3},{3,4},{4,5},{5,6},{6,7},{7,8},{8,9},{9,10},{10,1... | collective-permute-start | bytes 12296 | tf_op jit(solution)/shard_map/ppermute | solution.py:24
  332.7 18.1 %collective-permute-start.5 = (bf16[32,64]{1,0:T(8,128)(2,1)S(1)}, bf16[32,64]{1,0:T(8,128)(2,1)S(1)}, u32[]{:S(2)}, u32[]{:S(2)}) collective-permute-start(bf16[32,64]{1,0:T(8,128)(2,1)S(1)} %get-tuple-element.16), channel_id=1, source_target_pairs={{1,0},{2,1},{3,2},{4,3},{5,4},{6,5},{7,6},{8,7},{9,8},{10,9},{11,1... | collective-permute-start | bytes 12296 | tf_op jit(solution)/shard_map/ppermute | solution.py:26
  357.7 4.7 %copy-start.1 = (f32[32,4,128]{0,2,1:T(8,128)S(1)}, f32[32,4,128]{0,2,1:T(8,128)}, u32[]{:S(2)}) copy-start(f32[32,4,128]{0,2,1:T(8,128)} %copy-done) | copy-start | bytes 196612
Sparse Core Ops, SparseCore 0:
  10.5 106.1 all-gather.1
where the time goes:
time: 402 us; the launch traced here: 400 us
  blocking collectives  130 us (32%)
  waiting for transfers between devices  120 us (30%)
  starting transfers between devices  59.3 us (15%)
  local copies, waits for them, and re-layouts  39.4 us (10%)
  matrix products  21.3 us (5%)
  other arithmetic  16.1 us (4%)
  between operations  14 us (3%)
    all_to_all x10, blocking collectives, total_over_devices(): rows = lax.all_to_all(spread, axis, split_axis=0, concat_axis=0, tiled=True)  130 us
    all_gather x1, waiting for transfers between devices, on_device(): gathered = lax.all_gather(embeddings, 'band', axis=0, tiled=True)  76.2 us
    ppermute x3, waiting for transfers between devices, with_halo(): lax.ppermute(tail, axis, [(i, (i + 1) % count) for i in range(ends)])  32.5 us
    ppermute x3, starting transfers between devices, with_halo(): lax.ppermute(head, axis, [((i + 1) % count, i) for i in range(ends)])  23.6 us
    all_to_all x3, starting transfers between devices, band_gather(): lax.all_to_all(spread, 'band', split_axis=0, concat_axis=0, tiled=True)  19.7 us
    all_to_all x1, starting transfers between devices, on_device(): lax.all_to_all(ordered, 'band', split_axis=1, concat_axis=1, tiled=True)  10.2 us
    gather x1, local copies, waits for them, and re-layouts, on_device(): partner_rows = gathered.reshape(-1, 128, embed_width)[partners]  9.99 us
    all_to_all x3, waiting for transfers between devices, band_gather(): lax.all_to_all(spread, 'band', split_axis=0, concat_axis=0, tiled=True)  9.26 us
  transfers between devices with their start and end apart: 11, of which 9 were waited for; matrix products, arithmetic and copies ran while one was open for 7% of the time, Pallas kernels for 0%

commit v1 on v0

--- a/solution.py
+++ b/solution.py
@@ -116,18 +116,23 @@
             "ctkj,tkji->cti", far_tiles, affinity, preferred_element_type=jnp.float32
         ).reshape(channels, frames)
         image = direction - spread_rate * norm_scale[None, :] * (near_term + far_term)
-        curve = jnp.sum(direction * image, axis=1)
+        sums = [jnp.sum(direction * image, axis=1)]
+        last = iteration == ITERS - 1
+        if not last:
+            sums += [jnp.sum(residual * image, axis=1), jnp.sum(image * image, axis=1)]
         if iteration == 0:
-            both = total_over_devices(jnp.stack([first_norm, curve]))
-            norm_now, curve = both[0], both[1]
-        else:
-            curve = total_over_devices(curve)
+            sums.append(first_norm)
+        totals = total_over_devices(jnp.stack(sums))
+        curve = totals[0]
+        if iteration == 0:
+            norm_now = totals[-1]
         alpha = norm_now / curve
         solution = solution + alpha[:, None] * direction
-        residual = residual - alpha[:, None] * image
-        norm_next = squares(residual)
-        direction = residual + (norm_next / norm_now)[:, None] * direction
-        norm_now = norm_next
+        if not last:
+            residual = residual - alpha[:, None] * image
+            norm_next = norm_now - 2.0 * alpha * totals[1] + alpha * alpha * totals[2]
+            direction = residual + (norm_next / norm_now)[:, None] * direction
+            norm_now = norm_next
     return solution
 
 

time: 402 us -> 347 us (0.86)
  blocking collectives: 130 us -> 81.7 us
  other arithmetic: 16.1 us -> 9.32 us
    all_to_all x10 -> x6, blocking collectives: 130 us -> 81.7 us  [total_over_devices(): rows = lax.all_to_all(spread, axis, split_axis=0, concat_axis=0, tiled=True)]
where the time goes in v1:
time: 347 us; the launch traced here: 345 us
  waiting for transfers between devices  123 us (35%)
  blocking collectives  81.7 us (24%)
  starting transfers between devices  59.1 us (17%)
  local copies, waits for them, and re-layouts  40 us (12%)
  matrix products  18.3 us (5%)
  between operations  13.9 us (4%)
  other arithmetic  9.32 us (3%)
    all_to_all x6, blocking collectives, total_over_devices(): rows = lax.all_to_all(spread, axis, split_axis=0, concat_axis=0, tiled=True)  81.7 us
    all_gather x1, waiting for transfers between devices, on_device(): gathered = lax.all_gather(embeddings, 'band', axis=0, tiled=True)  76.4 us
    ppermute x3, waiting for transfers between devices, with_halo(): lax.ppermute(tail, axis, [(i, (i + 1) % count) for i in range(ends)])  32.3 us
    ppermute x3, starting transfers between devices, with_halo(): lax.ppermute(head, axis, [((i + 1) % count, i) for i in range(ends)])  23.6 us
    all_to_all x3, starting transfers between devices, band_gather(): lax.all_to_all(spread, 'band', split_axis=0, concat_axis=0, tiled=True)  19.6 us
    all_to_all x3, waiting for transfers between devices, band_gather(): lax.all_to_all(spread, 'band', split_axis=0, concat_axis=0, tiled=True)  12.2 us
    all_to_all x1, starting transfers between devices, on_device(): lax.all_to_all(ordered, 'band', split_axis=1, concat_axis=1, tiled=True)  10.2 us
    gather x1, local copies, waits for them, and re-layouts, on_device(): partner_rows = gathered.reshape(-1, 128, embed_width)[partners]  10 us
  transfers between devices with their start and end apart: 11, of which 9 were waited for; matrix products, arithmetic and copies ran while one was open for 7% of the time, Pallas kernels for 0%

profile of v1, /device:TPU:6, one launch (start us, length us, event | category | flops | bytes accessed | tf_op | source)
XLA Modules:
  0.0 345.0 jit_solution(3802023884421018203)
XLA Ops:
  6.5 0.7 all-gather.2.cloned.1.call-update
  7.3 0.7 convert_element_type.70
  7.9 0.8 broadcast_multiply_fusion
  9.4 1.3 reduce.14
  10.8 0.7 compare_select_fusion.1
  11.5 1.3 gather_fusion
  13.0 0.8 reshape.842
  13.7 10.2 %all-to-all-start = ((bf16[32,2,256]{2,1,0:T(2,128)(2,1)}), bf16[32,2,256]{2,1,0:T(2,128)(2,1)S(1)}, u32[]{:S(2)}, u32[]{:S(2)}) async-start(bf16[32,2,256]{2,1,0:T(2,128)(2,1)} %reshape.842), calls=%async_computation | async-start | bytes 65536 | tf_op jit(solution)/shard_map/all_to_all | solution.py:57
  24.0 1.0 reduce-window.9
  25.7 4.5 %gather_fusion.1 = s32[1024]{0:T(1024)S(1)} fusion(s32[640]{0:T(1024)S(1)} %convert_reduce_fusion.1, s32[1024]{0:T(1024)S(1)} %broadcast_clamp_fusion), kind=kCustom, calls=%fused_computation.1 | custom fusion | bytes 12288 | tf_op jit(solution)/shard_map/gather | solution.py:73
  30.3 2.3 gather_fusion.2
  32.6 6.8 %gather_fusion.3 = pred[1024]{0:T(1024)(128)(4,1)S(1)} fusion(pred[640]{0:T(1024)(128)(4,1)S(1)} %compare_and_fusion.1, s32[1024]{0:T(1024)S(1)} %broadcast_clamp_fusion), kind=kCustom, calls=%fused_computation.3 | custom fusion | bytes 6144 | tf_op jit(solution)/shard_map/gather | solution.py:74
  40.5 76.4 %all-gather.2.cloned.1.call-done = bf16[16384,256]{1,0:T(8,128)(2,1)} async-done(((bf16[512,256]{1,0:T(8,128)(2,1)}), bf16[16384,256]{1,0:T(8,128)(2,1)}) %all-gather.2.cloned.1.call-update) | async-done | bytes 8388624 | tf_op jit(solution)/shard_map/all_gather | solution.py:80
  116.9 10.0 %gather_fusion.4 = bf16[128,128,256]{2,1,0:T(8,128)(2,1)} fusion(bf16[128,128,256]{2,1,0:T(8,128)(2,1)} %bitcast.186, s32[1024]{0:T(1024)S(1)} %pad_clamp_fusion), kind=kCustom, calls=%fused_computation.4 | custom fusion | bytes 16777728 | tf_op jit(solution)/shard_map/gather | solution.py:82
  126.9 7.7 %convert_reduce_fusion = (f32[4,128]{1,0:T(4,128)S(1)}, bf16[4,32,128,128]{3,2,1,0:T(8,128)(2,1)}) fusion(f32[4,32]{1,0:T(4,128)S(1)} %convert_multiply_fusion.3, bf16[4,32,128,256]{3,2,1,0:T(8,128)(2,1)} %bitcast.187, bf16[4,128,256,1]{2,1,3,0:T(8,128)(2,1)S(1)} %bitcast.203), kind=kOutput, calls=%fused_computation.8 | convolution fusion | flops 1086324224 | bytes 12847616 | tf_op jit(solution)/shard_map/tkje,tie->tkji/dot_general | solution.py:84
  134.6 1.1 broadcast_in_dim.38
  135.8 8.0 %all-to-all-start.1 = ((bf16[32,32,512]{2,1,0:T(8,128)(2,1)}), bf16[32,32,512]{2,1,0:T(8,128)(2,1)S(1)}, u32[]{:S(2)}, u32[]{:S(2)}) async-start(bf16[32,32,512]{2,1,0:T(8,128)(2,1)} %broadcast_in_dim.38), calls=%async_computation.1 | async-start | bytes 2097152 | tf_op jit(solution)/shard_map/all_to_all | solution.py:45
  143.8 1.9 collective-permute-start
  145.7 7.9 %collective-permute-start.1 = (bf16[32,64]{1,0:T(8,128)(2,1)S(1)}, bf16[32,64]{1,0:T(8,128)(2,1)S(1)}, u32[]{:S(2)}, u32[]{:S(2)}) collective-permute-start(bf16[32,64]{1,0:T(8,128)(2,1)S(1)} %get-tuple-element.38), channel_id=1, source_target_pairs={{1,0},{2,1},{3,2},{4,3},{5,4},{6,5},{7,6},{8,7},{9,8},{10,9},{11,1... | collective-permute-start | bytes 12296 | tf_op jit(solution)/shard_map/ppermute | solution.py:26
  153.7 13.1 %collective-permute-done = bf16[32,64]{1,0:T(8,128)(2,1)S(1)} collective-permute-done((bf16[32,64]{1,0:T(8,128)(2,1)S(1)}, bf16[32,64]{1,0:T(8,128)(2,1)S(1)}, u32[]{:S(2)}, u32[]{:S(2)}) %collective-permute-start) | collective-permute-done | bytes 4128 | tf_op jit(solution)/shard_map/ppermute | solution.py:24
  167.5 2.4 all-to-all-done.1
  171.1 0.7 copy.86
  171.8 0.8 gather_fusion.5
  172.6 2.9 fusion.3
  176.0 14.8 %all_to_all.50 = f32[16,1,128]{2,1,0:T(1,128)S(1)} all-to-all(f32[16,1,128]{2,1,0:T(1,128)S(1)} %reshape.844), channel_id=1, replica_groups=mesh['band'=32,'seq'=16] {'seq'}, dimensions={0} | all-to-all | bytes 16384 | tf_op jit(solution)/shard_map/all_to_all | solution.py:37
  192.2 14.9 %all_to_all.51 = f32[32,1,128]{2,1,0:T(1,128)S(1)} all-to-all(f32[32,1,128]{2,1,0:T(1,128)S(1)} %reshape.846), channel_id=1, replica_groups=mesh['band'=32,'seq'=16] {'band'}, dimensions={0} | all-to-all | bytes 32768 | tf_op jit(solution)/shard_map/all_to_all | solution.py:37
  207.1 0.7 reduce.16
  208.0 1.1 broadcast_in_dim.41
  209.1 5.8 %all-to-all-start.4 = ((bf16[32,32,512]{2,1,0:T(8,128)(2,1)}), bf16[32,32,512]{2,1,0:T(8,128)(2,1)S(1)}, u32[]{:S(2)}, u32[]{:S(2)}) async-start(bf16[32,32,512]{2,1,0:T(8,128)(2,1)} %broadcast_in_dim.41), calls=%async_computation.4 | async-start | bytes 2097152 | tf_op jit(solution)/shard_map/all_to_all | solution.py:45
  215.0 1.9 collective-permute-start.2
  217.0 7.9 %collective-permute-start.3 = (bf16[32,64]{1,0:T(8,128)(2,1)S(1)}, bf16[32,64]{1,0:T(8,128)(2,1)S(1)}, u32[]{:S(2)}, u32[]{:S(2)}) collective-permute-start(bf16[32,64]{1,0:T(8,128)(2,1)S(1)} %get-tuple-element.32), channel_id=1, source_target_pairs={{1,0},{2,1},{3,2},{4,3},{5,4},{6,5},{7,6},{8,7},{9,8},{10,9},{11,1... | collective-permute-start | bytes 12296 | tf_op jit(solution)/shard_map/ppermute | solution.py:26
  224.8 9.6 %collective-permute-done.2 = bf16[32,64]{1,0:T(8,128)(2,1)S(1)} collective-permute-done((bf16[32,64]{1,0:T(8,128)(2,1)S(1)}, bf16[32,64]{1,0:T(8,128)(2,1)S(1)}, u32[]{:S(2)}, u32[]{:S(2)}) %collective-permute-start.2) | collective-permute-done | bytes 4128 | tf_op jit(solution)/shard_map/ppermute | solution.py:24
  235.5 4.9 %all-to-all-done.4 = bf16[32,32,512]{2,1,0:T(8,128)(2,1)S(1)} async-done(((bf16[32,32,512]{2,1,0:T(8,128)(2,1)}), bf16[32,32,512]{2,1,0:T(8,128)(2,1)S(1)}, u32[]{:S(2)}, u32[]{:S(2)}) %all-to-all-start.4) | async-done | bytes 1048608 | tf_op jit(solution)/shard_map/all_to_all | solution.py:45
  242.3 0.8 gather_fusion.6
  243.0 2.9 fusion.2
  246.4 10.3 %all_to_all.52 = f32[16,3,32]{2,1,0:T(4,128)S(1)} all-to-all(f32[16,3,32]{2,1,0:T(4,128)S(1)} %broadcast_in_dim.42), channel_id=1, replica_groups=mesh['band'=32,'seq'=16] {'seq'}, dimensions={0} | all-to-all | bytes 12288 | tf_op jit(solution)/shard_map/all_to_all | solution.py:37
  256.7 16.0 %all_to_all.53 = f32[32,3,32]{2,1,0:T(4,128)S(1)} all-to-all(f32[32,3,32]{2,1,0:T(4,128)S(1)} %broadcast_in_dim.43), channel_id=1, replica_groups=mesh['band'=32,'seq'=16] {'band'}, dimensions={0} | all-to-all | bytes 24576 | tf_op jit(solution)/shard_map/all_to_all | solution.py:37
  272.8 1.1 broadcast_in_dim.44
  273.9 5.8 %all-to-all-start.7 = ((bf16[32,32,512]{2,1,0:T(8,128)(2,1)}), bf16[32,32,512]{2,1,0:T(8,128)(2,1)S(1)}, u32[]{:S(2)}, u32[]{:S(2)}) async-start(bf16[32,32,512]{2,1,0:T(8,128)(2,1)} %broadcast_in_dim.44), calls=%async_computation.7 | async-start | bytes 2097152 | tf_op jit(solution)/shard_map/all_to_all | solution.py:45
  279.8 1.9 collective-permute-start.4
  281.8 7.9 %collective-permute-start.5 = (bf16[32,64]{1,0:T(8,128)(2,1)S(1)}, bf16[32,64]{1,0:T(8,128)(2,1)S(1)}, u32[]{:S(2)}, u32[]{:S(2)}) collective-permute-start(bf16[32,64]{1,0:T(8,128)(2,1)S(1)} %get-tuple-element.26), channel_id=1, source_target_pairs={{1,0},{2,1},{3,2},{4,3},{5,4},{6,5},{7,6},{8,7},{9,8},{10,9},{11,1... | collective-permute-start | bytes 12296 | tf_op jit(solution)/shard_map/ppermute | solution.py:26
  289.6 9.6 %collective-permute-done.4 = bf16[32,64]{1,0:T(8,128)(2,1)S(1)} collective-permute-done((bf16[32,64]{1,0:T(8,128)(2,1)S(1)}, bf16[32,64]{1,0:T(8,128)(2,1)S(1)}, u32[]{:S(2)}, u32[]{:S(2)}) %collective-permute-start.4) | collective-permute-done | bytes 4128 | tf_op jit(solution)/shard_map/ppermute | solution.py:24
  300.5 5.0 %all-to-all-done.7 = bf16[32,32,512]{2,1,0:T(8,128)(2,1)S(1)} async-done(((bf16[32,32,512]{2,1,0:T(8,128)(2,1)}), bf16[32,32,512]{2,1,0:T(8,128)(2,1)S(1)}, u32[]{:S(2)}, u32[]{:S(2)}) %all-to-all-start.7) | async-done | bytes 1048608 | tf_op jit(solution)/shard_map/all_to_all | solution.py:45
  307.5 0.8 gather_fusion.7
  308.2 2.9 fusion.1
  311.6 10.1 %all_to_all.54 = f32[16,1,32]{2,1,0:T(1,128)S(1)} all-to-all(f32[16,1,32]{2,1,0:T(1,128)S(1)} %broadcast_in_dim.45), channel_id=1, replica_groups=mesh['band'=32,'seq'=16] {'seq'}, dimensions={0} | all-to-all | bytes 4096 | tf_op jit(solution)/shard_map/all_to_all | solution.py:37
  321.7 15.6 %all_to_all.55 = f32[32,1,32]{2,1,0:T(1,128)S(1)} all-to-all(f32[32,1,32]{2,1,0:T(1,128)S(1)} %broadcast_in_dim.46), channel_id=1, replica_groups=mesh['band'=32,'seq'=16] {'band'}, dimensions={0} | all-to-all | bytes 8192 | tf_op jit(solution)/shard_map/all_to_all | solution.py:37
  337.4 0.7 multiply_add_fusion
  (94 shorter events, 14.2 us)
Async XLA Ops:
  6.5 32.9 %copy-start.1 = (s32[4,32]{1,0:T(4,128)S(1)}, s32[4,32]{1,0:T(4,128)}, u32[]{:S(2)}) copy-start(s32[4,32]{1,0:T(4,128)} %param.12) | copy-start | bytes 1540
  6.5 33.7 %copy-start.2 = (s32[4,32]{1,0:T(4,128)S(1)}, s32[4,32]{1,0:T(4,128)}, u32[]{:S(2)}) copy-start(s32[4,32]{1,0:T(4,128)} %param.13) | copy-start | bytes 1540
  6.5 110.4 %all-gather.2.cloned.1.call-start = ((), (), s32[]{:S(2)}) async-start(), calls=%async_computation.10 | async-start | bytes 8650752 | tf_op jit(solution)/shard_map/all_gather | solution.py:80
  13.7 26.5 %all-to-all-start = ((bf16[32,2,256]{2,1,0:T(2,128)(2,1)}), bf16[32,2,256]{2,1,0:T(2,128)(2,1)S(1)}, u32[]{:S(2)}, u32[]{:S(2)}) async-start(bf16[32,2,256]{2,1,0:T(2,128)(2,1)} %reshape.842), calls=%async_computation | async-start | bytes 65536 | tf_op jit(solution)/shard_map/all_to_all | solution.py:57
  116.9 10.0 %copy-start = (bf16[512,256]{1,0:T(8,128)(2,1)S(1)}, bf16[512,256]{1,0:T(8,128)(2,1)}, u32[]{:S(2)}) copy-start(bf16[512,256]{1,0:T(8,128)(2,1)} %param.11) | copy-start | bytes 786436
  135.8 34.1 %all-to-all-start.1 = ((bf16[32,32,512]{2,1,0:T(8,128)(2,1)}), bf16[32,32,512]{2,1,0:T(8,128)(2,1)S(1)}, u32[]{:S(2)}, u32[]{:S(2)}) async-start(bf16[32,32,512]{2,1,0:T(8,128)(2,1)} %broadcast_in_dim.38), calls=%async_computation.1 | async-start | bytes 2097152 | tf_op jit(solution)/shard_map/all_to_all | solution.py:45
  143.8 23.0 %collective-permute-start = (bf16[32,64]{1,0:T(8,128)(2,1)S(1)}, bf16[32,64]{1,0:T(8,128)(2,1)S(1)}, u32[]{:S(2)}, u32[]{:S(2)}) collective-permute-start(bf16[32,64]{1,0:T(8,128)(2,1)S(1)} %get-tuple-element.37), channel_id=1, source_target_pairs={{0,1},{1,2},{2,3},{3,4},{4,5},{5,6},{6,7},{7,8},{8,9},{9,10},{10,1... | collective-permute-start | bytes 12296 | tf_op jit(solution)/shard_map/ppermute | solution.py:24
  145.7 21.1 %collective-permute-start.1 = (bf16[32,64]{1,0:T(8,128)(2,1)S(1)}, bf16[32,64]{1,0:T(8,128)(2,1)S(1)}, u32[]{:S(2)}, u32[]{:S(2)}) collective-permute-start(bf16[32,64]{1,0:T(8,128)(2,1)S(1)} %get-tuple-element.38), channel_id=1, source_target_pairs={{1,0},{2,1},{3,2},{4,3},{5,4},{6,5},{7,6},{8,7},{9,8},{10,9},{11,1... | collective-permute-start | bytes 12296 | tf_op jit(solution)/shard_map/ppermute | solution.py:26
  209.1 31.2 %all-to-all-start.4 = ((bf16[32,32,512]{2,1,0:T(8,128)(2,1)}), bf16[32,32,512]{2,1,0:T(8,128)(2,1)S(1)}, u32[]{:S(2)}, u32[]{:S(2)}) async-start(bf16[32,32,512]{2,1,0:T(8,128)(2,1)} %broadcast_in_dim.41), calls=%async_computation.4 | async-start | bytes 2097152 | tf_op jit(solution)/shard_map/all_to_all | solution.py:45
  215.0 19.3 %collective-permute-start.2 = (bf16[32,64]{1,0:T(8,128)(2,1)S(1)}, bf16[32,64]{1,0:T(8,128)(2,1)S(1)}, u32[]{:S(2)}, u32[]{:S(2)}) collective-permute-start(bf16[32,64]{1,0:T(8,128)(2,1)S(1)} %get-tuple-element.31), channel_id=1, source_target_pairs={{0,1},{1,2},{2,3},{3,4},{4,5},{5,6},{6,7},{7,8},{8,9},{9,10},{10,1... | collective-permute-start | bytes 12296 | tf_op jit(solution)/shard_map/ppermute | solution.py:24
  217.0 17.8 %collective-permute-start.3 = (bf16[32,64]{1,0:T(8,128)(2,1)S(1)}, bf16[32,64]{1,0:T(8,128)(2,1)S(1)}, u32[]{:S(2)}, u32[]{:S(2)}) collective-permute-start(bf16[32,64]{1,0:T(8,128)(2,1)S(1)} %get-tuple-element.32), channel_id=1, source_target_pairs={{1,0},{2,1},{3,2},{4,3},{5,4},{6,5},{7,6},{8,7},{9,8},{10,9},{11,1... | collective-permute-start | bytes 12296 | tf_op jit(solution)/shard_map/ppermute | solution.py:26
  273.9 31.6 %all-to-all-start.7 = ((bf16[32,32,512]{2,1,0:T(8,128)(2,1)}), bf16[32,32,512]{2,1,0:T(8,128)(2,1)S(1)}, u32[]{:S(2)}, u32[]{:S(2)}) async-start(bf16[32,32,512]{2,1,0:T(8,128)(2,1)} %broadcast_in_dim.44), calls=%async_computation.7 | async-start | bytes 2097152 | tf_op jit(solution)/shard_map/all_to_all | solution.py:45
  279.8 19.4 %collective-permute-start.4 = (bf16[32,64]{1,0:T(8,128)(2,1)S(1)}, bf16[32,64]{1,0:T(8,128)(2,1)S(1)}, u32[]{:S(2)}, u32[]{:S(2)}) collective-permute-start(bf16[32,64]{1,0:T(8,128)(2,1)S(1)} %get-tuple-element.25), channel_id=1, source_target_pairs={{0,1},{1,2},{2,3},{3,4},{4,5},{5,6},{6,7},{7,8},{8,9},{9,10},{10,1... | collective-permute-start | bytes 12296 | tf_op jit(solution)/shard_map/ppermute | solution.py:24
  281.8 18.1 %collective-permute-start.5 = (bf16[32,64]{1,0:T(8,128)(2,1)S(1)}, bf16[32,64]{1,0:T(8,128)(2,1)S(1)}, u32[]{:S(2)}, u32[]{:S(2)}) collective-permute-start(bf16[32,64]{1,0:T(8,128)(2,1)S(1)} %get-tuple-element.26), channel_id=1, source_target_pairs={{1,0},{2,1},{3,2},{4,3},{5,4},{6,5},{7,6},{8,7},{9,8},{10,9},{11,1... | collective-permute-start | bytes 12296 | tf_op jit(solution)/shard_map/ppermute | solution.py:26
Sparse Core Ops, SparseCore 0:
  10.5 106.3 all-gather.1

commit v2 on v1

--- a/solution.py
+++ b/solution.py
@@ -77,8 +77,15 @@
         linked, jnp.exp(-offset.astype(jnp.float32) / decay_len), jnp.float32(0.0)
     ).astype(jnp.bfloat16)
     near_degree = jnp.sum(band_tiles.astype(jnp.float32), axis=1).reshape(frames)
-    gathered = lax.all_gather(embeddings, "band", axis=0, tiled=True)
     embed_width = embeddings.shape[1]
+    split_rows = (tile_count - 1) * 128
+    gathered = jnp.concatenate(
+        [
+            lax.all_gather(embeddings[:split_rows], "band", axis=0, tiled=False),
+            band_gather(embeddings[split_rows:]),
+        ],
+        axis=1,
+    )
     partner_rows = gathered.reshape(-1, 128, embed_width)[partners]
     own_rows = embeddings.reshape(tile_count, 128, embed_width)
     inner_prod = jnp.einsum(

time: 347 us -> 371 us (1.069)
  other arithmetic: 9.32 us -> 22.5 us
  waiting for transfers between devices: 123 us -> 114 us
  starting transfers between devices: 59.1 us -> 67.9 us
  local copies, waits for them, and re-layouts: 40 us -> 44.3 us
    all_gather x1, waiting for transfers between devices: 76.4 us -> 24.2 us  [on_device(): lax.all_gather(embeddings[:split_rows], 'band', axis=0, tiled=False)]
    all_to_all x3 -> x4, waiting for transfers between devices: 12.2 us -> 48.2 us  [band_gather(): lax.all_to_all(spread, 'band', split_axis=0, concat_axis=0, tiled=True)]
    all_to_all x1, waiting for transfers between devices: 0.01 us -> 7.18 us  [on_device(): lax.all_to_all(ordered, 'band', split_axis=1, concat_axis=1, tiled=True)]
    concatenate x0 -> x1, other arithmetic: none -> 6.8 us  [on_device(): jnp.concatenate([lax.all_gather(embeddings[:split_rows], 'band', axis=0,...]
    all_to_all x3 -> x4, starting transfers between devices: 19.6 us -> 25.2 us  [band_gather(): lax.all_to_all(spread, 'band', split_axis=0, concat_axis=0, tiled=True)]
  transfers between devices with their start and end apart: 11 -> 12, of which waited for: 9 -> 10; matrix products, arithmetic and copies ran while one was open for 7% -> 8% of each run, Pallas kernels for 0% -> 0%
where the time goes in v2:
time: 371 us; the launch traced here: 368 us
  waiting for transfers between devices  114 us (31%)
  blocking collectives  85 us (23%)
  starting transfers between devices  67.9 us (18%)
  local copies, waits for them, and re-layouts  44.3 us (12%)
  other arithmetic  22.5 us (6%)
  matrix products  20.7 us (6%)
  between operations  14 us (4%)
    all_to_all x6, blocking collectives, total_over_devices(): rows = lax.all_to_all(spread, axis, split_axis=0, concat_axis=0, tiled=True)  85 us
    all_to_all x4, waiting for transfers between devices, band_gather(): lax.all_to_all(spread, 'band', split_axis=0, concat_axis=0, tiled=True)  48.2 us
    ppermute x3, waiting for transfers between devices, with_halo(): lax.ppermute(tail, axis, [(i, (i + 1) % count) for i in range(ends)])  32.9 us
    ppermute x3, starting transfers between devices, with_halo(): lax.ppermute(head, axis, [((i + 1) % count, i) for i in range(ends)])  26.8 us
    all_to_all x4, starting transfers between devices, band_gather(): lax.all_to_all(spread, 'band', split_axis=0, concat_axis=0, tiled=True)  25.2 us
    all_gather x1, waiting for transfers between devices, on_device(): lax.all_gather(embeddings[:split_rows], 'band', axis=0, tiled=False)  24.2 us
    all_to_all x1, starting transfers between devices, on_device(): lax.all_to_all(ordered, 'band', split_axis=1, concat_axis=1, tiled=True)  10.2 us
    gather x1, local copies, waits for them, and re-layouts, on_device(): partner_rows = gathered.reshape(-1, 128, embed_width)[partners]  9.99 us
  transfers between devices with their start and end apart: 12, of which 10 were waited for; matrix products, arithmetic and copies ran while one was open for 8% of the time, Pallas kernels for 0%

profile of v2, /device:TPU:6, one launch (start us, length us, event | category | flops | bytes accessed | tf_op | source)
XLA Modules:
  0.0 368.0 jit_solution(16369834909836987338)
XLA Ops:
  6.5 1.7 slice.96
  10.3 1.3 reduce.14
  12.4 1.3 gather_fusion
  14.7 10.2 %all-to-all-start = ((bf16[32,2,256]{2,1,0:T(2,128)(2,1)}), bf16[32,2,256]{2,1,0:T(2,128)(2,1)S(1)}, u32[]{:S(2)}, u32[]{:S(2)}) async-start(bf16[32,2,256]{2,1,0:T(2,128)(2,1)} %reshape.844), calls=%async_computation | async-start | bytes 65536 | tf_op jit(solution)/shard_map/all_to_all | solution.py:57
  25.8 7.2 %all-to-all-done = bf16[32,2,256]{2,1,0:T(2,128)(2,1)S(1)} async-done(((bf16[32,2,256]{2,1,0:T(2,128)(2,1)}), bf16[32,2,256]{2,1,0:T(2,128)(2,1)S(1)}, u32[]{:S(2)}, u32[]{:S(2)}) %all-to-all-start) | async-done | bytes 32800 | tf_op jit(solution)/shard_map/all_to_all | solution.py:57
  33.0 1.6 broadcast_in_dim.39
  34.6 5.9 %all-to-all-start.1 = ((bf16[32,128,256]{2,1,0:T(8,128)(2,1)}), bf16[32,128,256]{2,1,0:T(8,128)(2,1)S(1)}, u32[]{:S(2)}, u32[]{:S(2)}) async-start(bf16[32,128,256]{2,1,0:T(8,128)(2,1)} %broadcast_in_dim.39), calls=%async_computation.1 | async-start | bytes 4194304 | tf_op jit(solution)/shard_map/all_to_all | solution.py:45
  40.5 1.0 reduce-window.9
  42.1 4.5 %gather_fusion.1 = s32[1024]{0:T(1024)S(1)} fusion(s32[640]{0:T(1024)S(1)} %convert_reduce_fusion.1, s32[1024]{0:T(1024)S(1)} %broadcast_clamp_fusion), kind=kCustom, calls=%fused_computation.1 | custom fusion | bytes 12288 | tf_op jit(solution)/shard_map/gather | solution.py:73
  46.8 2.3 gather_fusion.2
  49.1 6.8 %gather_fusion.3 = pred[1024]{0:T(1024)(128)(4,1)S(1)} fusion(pred[640]{0:T(1024)(128)(4,1)S(1)} %compare_and_fusion.1, s32[1024]{0:T(1024)S(1)} %broadcast_clamp_fusion), kind=kCustom, calls=%fused_computation.3 | custom fusion | bytes 6144 | tf_op jit(solution)/shard_map/gather | solution.py:74
  57.0 40.9 %all-to-all-done.1 = bf16[32,128,256]{2,1,0:T(8,128)(2,1)S(1)} async-done(((bf16[32,128,256]{2,1,0:T(8,128)(2,1)}), bf16[32,128,256]{2,1,0:T(8,128)(2,1)S(1)}, u32[]{:S(2)}, u32[]{:S(2)}) %all-to-all-start.1) | async-done | bytes 2097184 | tf_op jit(solution)/shard_map/all_to_all | solution.py:45
  97.9 24.2 %all-gather.3.cloned.1.call-done = bf16[12288,256]{1,0:T(8,128)(2,1)} async-done(((bf16[384,256]{1,0:T(8,128)(2,1)}), bf16[12288,256]{1,0:T(8,128)(2,1)}) %all-gather.3.cloned.1.call-update) | async-done | bytes 6291472 | tf_op jit(solution)/shard_map/all_gather | solution.py:84
  122.1 6.8 %pad_maximum_fusion = bf16[32,512,256]{2,1,0:T(8,128)(2,1)} fusion(bf16[32,128,256]{2,1,0:T(8,128)(2,1)S(1)} %all-to-all-done.1, bf16[32,384,256]{2,1,0:T(8,128)(2,1)} %bitcast.189), kind=kLoop, calls=%fused_computation.8 | loop fusion | flops 16777216 | bytes 16777216 | tf_op jit(solution)/shard_map/concatenate | solution.py:82
  128.9 10.0 %gather_fusion.4 = bf16[128,128,256]{2,1,0:T(8,128)(2,1)} fusion(bf16[128,128,256]{2,1,0:T(8,128)(2,1)} %bitcast.187, s32[1024]{0:T(1024)S(1)} %pad_clamp_fusion), kind=kCustom, calls=%fused_computation.4 | custom fusion | bytes 16777728 | tf_op jit(solution)/shard_map/gather | solution.py:89
  138.9 7.7 %convert_reduce_fusion = (f32[4,128]{1,0:T(4,128)S(1)}, bf16[4,32,128,128]{3,2,1,0:T(8,128)(2,1)}) fusion(f32[4,32]{1,0:T(4,128)S(1)} %convert_multiply_fusion.3, bf16[4,32,128,256]{3,2,1,0:T(8,128)(2,1)} %bitcast.188, bf16[4,128,256,1]{2,1,3,0:T(8,128)(2,1)S(1)} %bitcast.205), kind=kOutput, calls=%fused_computation.9 | convolution fusion | flops 1086324224 | bytes 12847616 | tf_op jit(solution)/shard_map/tkje,tie->tkji/dot_general | solution.py:91
  146.6 1.1 broadcast_in_dim.41
  147.7 7.6 %all-to-all-start.2 = ((bf16[32,32,512]{2,1,0:T(8,128)(2,1)}), bf16[32,32,512]{2,1,0:T(8,128)(2,1)S(1)}, u32[]{:S(2)}, u32[]{:S(2)}) async-start(bf16[32,32,512]{2,1,0:T(8,128)(2,1)} %broadcast_in_dim.41), calls=%async_computation.2 | async-start | bytes 2097152 | tf_op jit(solution)/shard_map/all_to_all | solution.py:45
  155.4 1.9 collective-permute-start
  157.3 10.8 %collective-permute-start.1 = (bf16[32,64]{1,0:T(8,128)(2,1)S(1)}, bf16[32,64]{1,0:T(8,128)(2,1)S(1)}, u32[]{:S(2)}, u32[]{:S(2)}) collective-permute-start(bf16[32,64]{1,0:T(8,128)(2,1)S(1)} %get-tuple-element.38), channel_id=1, source_target_pairs={{1,0},{2,1},{3,2},{4,3},{5,4},{6,5},{7,6},{8,7},{9,8},{10,9},{11,1... | collective-permute-start | bytes 12296 | tf_op jit(solution)/shard_map/ppermute | solution.py:26
  168.3 14.0 %collective-permute-done = bf16[32,64]{1,0:T(8,128)(2,1)S(1)} collective-permute-done((bf16[32,64]{1,0:T(8,128)(2,1)S(1)}, bf16[32,64]{1,0:T(8,128)(2,1)S(1)}, u32[]{:S(2)}, u32[]{:S(2)}) %collective-permute-start) | collective-permute-done | bytes 4128 | tf_op jit(solution)/shard_map/ppermute | solution.py:24
  185.7 2.9 fusion.3
  189.0 15.6 %all_to_all.55 = f32[16,1,128]{2,1,0:T(1,128)S(1)} all-to-all(f32[16,1,128]{2,1,0:T(1,128)S(1)} %reshape.846), channel_id=1, replica_groups=mesh['band'=32,'seq'=16] {'seq'}, dimensions={0} | all-to-all | bytes 16384 | tf_op jit(solution)/shard_map/all_to_all | solution.py:37
  206.0 15.0 %all_to_all.56 = f32[32,1,128]{2,1,0:T(1,128)S(1)} all-to-all(f32[32,1,128]{2,1,0:T(1,128)S(1)} %reshape.848), channel_id=1, replica_groups=mesh['band'=32,'seq'=16] {'band'}, dimensions={0} | all-to-all | bytes 32768 | tf_op jit(solution)/shard_map/all_to_all | solution.py:37
  222.5 1.1 broadcast_in_dim.44
  223.6 5.8 %all-to-all-start.5 = ((bf16[32,32,512]{2,1,0:T(8,128)(2,1)}), bf16[32,32,512]{2,1,0:T(8,128)(2,1)S(1)}, u32[]{:S(2)}, u32[]{:S(2)}) async-start(bf16[32,32,512]{2,1,0:T(8,128)(2,1)} %broadcast_in_dim.44), calls=%async_computation.5 | async-start | bytes 2097152 | tf_op jit(solution)/shard_map/all_to_all | solution.py:45
  229.5 1.9 collective-permute-start.2
  231.5 7.9 %collective-permute-start.3 = (bf16[32,64]{1,0:T(8,128)(2,1)S(1)}, bf16[32,64]{1,0:T(8,128)(2,1)S(1)}, u32[]{:S(2)}, u32[]{:S(2)}) collective-permute-start(bf16[32,64]{1,0:T(8,128)(2,1)S(1)} %get-tuple-element.32), channel_id=1, source_target_pairs={{1,0},{2,1},{3,2},{4,3},{5,4},{6,5},{7,6},{8,7},{9,8},{10,9},{11,1... | collective-permute-start | bytes 12296 | tf_op jit(solution)/shard_map/ppermute | solution.py:26
  239.3 9.6 %collective-permute-done.2 = bf16[32,64]{1,0:T(8,128)(2,1)S(1)} collective-permute-done((bf16[32,64]{1,0:T(8,128)(2,1)S(1)}, bf16[32,64]{1,0:T(8,128)(2,1)S(1)}, u32[]{:S(2)}, u32[]{:S(2)}) %collective-permute-start.2) | collective-permute-done | bytes 4128 | tf_op jit(solution)/shard_map/ppermute | solution.py:24
  249.4 1.4 fusion.14
  250.9 4.0 %all-to-all-done.5 = bf16[32,32,512]{2,1,0:T(8,128)(2,1)S(1)} async-done(((bf16[32,32,512]{2,1,0:T(8,128)(2,1)}), bf16[32,32,512]{2,1,0:T(8,128)(2,1)S(1)}, u32[]{:S(2)}, u32[]{:S(2)}) %all-to-all-start.5) | async-done | bytes 1048608 | tf_op jit(solution)/shard_map/all_to_all | solution.py:45
  257.7 2.9 fusion.2
  261.7 10.7 %all_to_all.57 = f32[16,3,32]{2,1,0:T(4,128)S(1)} all-to-all(f32[16,3,32]{2,1,0:T(4,128)S(1)} %broadcast_in_dim.45), channel_id=1, replica_groups=mesh['band'=32,'seq'=16] {'seq'}, dimensions={0} | all-to-all | bytes 12288 | tf_op jit(solution)/shard_map/all_to_all | solution.py:37
  272.4 16.5 %all_to_all.58 = f32[32,3,32]{2,1,0:T(4,128)S(1)} all-to-all(f32[32,3,32]{2,1,0:T(4,128)S(1)} %broadcast_in_dim.46), channel_id=1, replica_groups=mesh['band'=32,'seq'=16] {'band'}, dimensions={0} | all-to-all | bytes 24576 | tf_op jit(solution)/shard_map/all_to_all | solution.py:37
  289.0 1.1 fusion.73
  290.1 1.6 multiply_convert_fusion.1
  291.7 1.1 broadcast_in_dim.47
  292.8 5.8 %all-to-all-start.8 = ((bf16[32,32,512]{2,1,0:T(8,128)(2,1)}), bf16[32,32,512]{2,1,0:T(8,128)(2,1)S(1)}, u32[]{:S(2)}, u32[]{:S(2)}) async-start(bf16[32,32,512]{2,1,0:T(8,128)(2,1)} %broadcast_in_dim.47), calls=%async_computation.8 | async-start | bytes 2097152 | tf_op jit(solution)/shard_map/all_to_all | solution.py:45
  298.7 1.9 collective-permute-start.4
  300.7 8.1 %collective-permute-start.5 = (bf16[32,64]{1,0:T(8,128)(2,1)S(1)}, bf16[32,64]{1,0:T(8,128)(2,1)S(1)}, u32[]{:S(2)}, u32[]{:S(2)}) collective-permute-start(bf16[32,64]{1,0:T(8,128)(2,1)S(1)} %get-tuple-element.26), channel_id=1, source_target_pairs={{1,0},{2,1},{3,2},{4,3},{5,4},{6,5},{7,6},{8,7},{9,8},{10,9},{11,1... | collective-permute-start | bytes 12296 | tf_op jit(solution)/shard_map/ppermute | solution.py:26
  308.7 9.4 %collective-permute-done.4 = bf16[32,64]{1,0:T(8,128)(2,1)S(1)} collective-permute-done((bf16[32,64]{1,0:T(8,128)(2,1)S(1)}, bf16[32,64]{1,0:T(8,128)(2,1)S(1)}, u32[]{:S(2)}, u32[]{:S(2)}) %collective-permute-start.4) | collective-permute-done | bytes 4128 | tf_op jit(solution)/shard_map/ppermute | solution.py:24
  318.8 2.2 fusion.15
  321.0 3.4 all-to-all-done.8
  327.3 2.9 fusion.1
  330.4 1.2 fusion.12
  331.6 11.1 %all_to_all.59 = f32[16,1,32]{2,1,0:T(1,128)S(1)} all-to-all(f32[16,1,32]{2,1,0:T(1,128)S(1)} %broadcast_in_dim.48), channel_id=1, replica_groups=mesh['band'=32,'seq'=16] {'seq'}, dimensions={0} | all-to-all | bytes 4096 | tf_op jit(solution)/shard_map/all_to_all | solution.py:37
  342.7 16.2 %all_to_all.60 = f32[32,1,32]{2,1,0:T(1,128)S(1)} all-to-all(f32[32,1,32]{2,1,0:T(1,128)S(1)} %broadcast_in_dim.49), channel_id=1, replica_groups=mesh['band'=32,'seq'=16] {'band'}, dimensions={0} | all-to-all | bytes 8192 | tf_op jit(solution)/shard_map/all_to_all | solution.py:37
  359.6 1.6 multiply_add_fusion
  (134 shorter events, 22.2 us)
Async XLA Ops:
  6.5 49.4 %copy-start.16 = (s32[4,32]{1,0:T(4,128)S(1)}, s32[4,32]{1,0:T(4,128)}, u32[]{:S(2)}) copy-start(s32[4,32]{1,0:T(4,128)} %param.12) | copy-start | bytes 1540
  6.5 50.2 %copy-start.17 = (s32[4,32]{1,0:T(4,128)S(1)}, s32[4,32]{1,0:T(4,128)}, u32[]{:S(2)}) copy-start(s32[4,32]{1,0:T(4,128)} %param.13) | copy-start | bytes 1540
  6.5 115.6 %all-gather.3.cloned.1.call-start = ((), (), s32[]{:S(2)}) async-start(), calls=%async_computation.11 | async-start | bytes 6488064 | tf_op jit(solution)/shard_map/all_gather | solution.py:84
  14.7 18.3 %all-to-all-start = ((bf16[32,2,256]{2,1,0:T(2,128)(2,1)}), bf16[32,2,256]{2,1,0:T(2,128)(2,1)S(1)}, u32[]{:S(2)}, u32[]{:S(2)}) async-start(bf16[32,2,256]{2,1,0:T(2,128)(2,1)} %reshape.844), calls=%async_computation | async-start | bytes 65536 | tf_op jit(solution)/shard_map/all_to_all | solution.py:57
  34.6 63.3 %all-to-all-start.1 = ((bf16[32,128,256]{2,1,0:T(8,128)(2,1)}), bf16[32,128,256]{2,1,0:T(8,128)(2,1)S(1)}, u32[]{:S(2)}, u32[]{:S(2)}) async-start(bf16[32,128,256]{2,1,0:T(8,128)(2,1)} %broadcast_in_dim.39), calls=%async_computation.1 | async-start | bytes 4194304 | tf_op jit(solution)/shard_map/all_to_all | solution.py:45
  46.7 202.7 %copy-start.14 = (s32[4,256]{1,0:T(4,128)}, s32[4,256]{1,0:T(4,128)S(1)}, u32[]{:S(2)}) copy-start(s32[4,256]{1,0:T(4,128)S(1)} %eq.17) | copy-start | bytes 12292
  49.1 200.3 %copy-start.18 = (s32[512]{0:T(512)}, s32[512]{0:T(512)S(1)}, u32[]{:S(2)}) copy-start(s32[512]{0:T(512)S(1)} %gather_fusion.2) | copy-start | bytes 6148
  55.9 193.5 %copy-start.19 = (pred[4,256]{1,0:T(4,128)(4,1)}, pred[4,256]{1,0:T(4,128)(4,1)S(1)}, u32[]{:S(2)}) copy-start(pred[4,256]{1,0:T(4,128)(4,1)S(1)} %and.33) | copy-start | bytes 3076
  56.0 128.9 %copy-start.4 = (s32[1024]{0:T(1024)}, s32[1024]{0:T(1024)S(1)}, u32[]{:S(2)}) copy-start(s32[1024]{0:T(1024)S(1)} %pad_clamp_fusion) | copy-start | bytes 12292
  56.1 193.3 %copy-start.15 = (s32[4,128]{1,0:T(4,128)}, s32[4,128]{1,0:T(4,128)S(1)}, u32[]{:S(2)}) copy-start(s32[4,128]{1,0:T(4,128)S(1)} %iota_add_fusion.2) | copy-start | bytes 6148
  56.2 193.2 %copy-start.13 = (s32[4,256]{1,0:T(4,128)}, s32[4,256]{1,0:T(4,128)S(1)}, u32[]{:S(2)}) copy-start(s32[4,256]{1,0:T(4,128)S(1)} %iota_add_fusion.1) | copy-start | bytes 12292
  57.0 165.4 %copy-start.2 = (f32[32,512]{1,0:T(8,128)}, f32[32,512]{1,0:T(8,128)S(1)}, u32[]{:S(2)}) copy-start(f32[32,512]{1,0:T(8,128)S(1)} %copy.84) | copy-start | bytes 196612
  128.9 10.0 %copy-start.3 = (bf16[512,256]{1,0:T(8,128)(2,1)S(1)}, bf16[512,256]{1,0:T(8,128)(2,1)}, u32[]{:S(2)}) copy-start(bf16[512,256]{1,0:T(8,128)(2,1)} %param.11) | copy-start | bytes 786436
  146.6 75.9 %copy-start.5 = (f32[512]{0:T(512)}, f32[512]{0:T(512)S(1)}, u32[]{:S(2)}) copy-start(f32[512]{0:T(512)S(1)} %get-tuple-element.16) | copy-start | bytes 6148
  146.6 75.9 %copy-start.6 = (f32[512]{0:T(512)}, f32[512]{0:T(512)S(1)}, u32[]{:S(2)}) copy-start(f32[512]{0:T(512)S(1)} %get-tuple-element.17) | copy-start | bytes 6148
  147.7 35.3 %all-to-all-start.2 = ((bf16[32,32,512]{2,1,0:T(8,128)(2,1)}), bf16[32,32,512]{2,1,0:T(8,128)(2,1)S(1)}, u32[]{:S(2)}, u32[]{:S(2)}) async-start(bf16[32,32,512]{2,1,0:T(8,128)(2,1)} %broadcast_in_dim.41), calls=%async_computation.2 | async-start | bytes 2097152 | tf_op jit(solution)/shard_map/all_to_all | solution.py:45
  155.4 26.8 %collective-permute-start = (bf16[32,64]{1,0:T(8,128)(2,1)S(1)}, bf16[32,64]{1,0:T(8,128)(2,1)S(1)}, u32[]{:S(2)}, u32[]{:S(2)}) collective-permute-start(bf16[32,64]{1,0:T(8,128)(2,1)S(1)} %get-tuple-element.37), channel_id=1, source_target_pairs={{0,1},{1,2},{2,3},{3,4},{4,5},{5,6},{6,7},{7,8},{8,9},{9,10},{10,1... | collective-permute-start | bytes 12296 | tf_op jit(solution)/shard_map/ppermute | solution.py:24
  157.3 24.9 %collective-permute-start.1 = (bf16[32,64]{1,0:T(8,128)(2,1)S(1)}, bf16[32,64]{1,0:T(8,128)(2,1)S(1)}, u32[]{:S(2)}, u32[]{:S(2)}) collective-permute-start(bf16[32,64]{1,0:T(8,128)(2,1)S(1)} %get-tuple-element.38), channel_id=1, source_target_pairs={{1,0},{2,1},{3,2},{4,3},{5,4},{6,5},{7,6},{8,7},{9,8},{10,9},{11,1... | collective-permute-start | bytes 12296 | tf_op jit(solution)/shard_map/ppermute | solution.py:26
  188.6 35.0 %copy-start.1 = (f32[4,128,32]{1,2,0:T(8,128)}, f32[4,128,32]{1,2,0:T(8,128)S(1)}, u32[]{:S(2)}) copy-start(f32[4,128,32]{1,2,0:T(8,128)S(1)} %fusion.3) | copy-start | bytes 196612
  222.4 32.4 %copy-start.7 = (f32[32]{0:T(128)}, f32[32]{0:T(128)S(1)}, u32[]{:S(2)}) copy-start(f32[32]{0:T(128)S(1)} %get-tuple-element.18) | copy-start | bytes 388
  222.4 32.4 %copy-start.9 = (f32[32]{0:T(128)}, f32[32]{0:T(128)S(1)}, u32[]{:S(2)}) copy-start(f32[32]{0:T(128)S(1)} %get-tuple-element.20) | copy-start | bytes 388
  223.6 31.2 %all-to-all-start.5 = ((bf16[32,32,512]{2,1,0:T(8,128)(2,1)}), bf16[32,32,512]{2,1,0:T(8,128)(2,1)S(1)}, u32[]{:S(2)}, u32[]{:S(2)}) async-start(bf16[32,32,512]{2,1,0:T(8,128)(2,1)} %broadcast_in_dim.44), calls=%async_computation.5 | async-start | bytes 2097152 | tf_op jit(solution)/shard_map/all_to_all | solution.py:45
  229.5 19.3 %collective-permute-start.2 = (bf16[32,64]{1,0:T(8,128)(2,1)S(1)}, bf16[32,64]{1,0:T(8,128)(2,1)S(1)}, u32[]{:S(2)}, u32[]{:S(2)}) collective-permute-start(bf16[32,64]{1,0:T(8,128)(2,1)S(1)} %get-tuple-element.31), channel_id=1, source_target_pairs={{0,1},{1,2},{2,3},{3,4},{4,5},{5,6},{6,7},{7,8},{8,9},{9,10},{10,1... | collective-permute-start | bytes 12296 | tf_op jit(solution)/shard_map/ppermute | solution.py:24
  231.5 17.8 %collective-permute-start.3 = (bf16[32,64]{1,0:T(8,128)(2,1)S(1)}, bf16[32,64]{1,0:T(8,128)(2,1)S(1)}, u32[]{:S(2)}, u32[]{:S(2)}) collective-permute-start(bf16[32,64]{1,0:T(8,128)(2,1)S(1)} %get-tuple-element.32), channel_id=1, source_target_pairs={{1,0},{2,1},{3,2},{4,3},{5,4},{6,5},{7,6},{8,7},{9,8},{10,9},{11,1... | collective-permute-start | bytes 12296 | tf_op jit(solution)/shard_map/ppermute | solution.py:26
  256.8 33.3 %copy-start.8 = (f32[32]{0:T(128)S(1)}, f32[32]{0:T(128)}, u32[]{:S(2)}) copy-start(f32[32]{0:T(128)} %copy-done.7) | copy-start | bytes 388
  256.8 33.3 %copy-start.10 = (f32[32]{0:T(128)S(1)}, f32[32]{0:T(128)}, u32[]{:S(2)}) copy-start(f32[32]{0:T(128)} %copy-done.9) | copy-start | bytes 388
  260.8 32.1 %copy-start = (f32[32,4,128]{0,2,1:T(8,128)}, f32[32,4,128]{0,2,1:T(8,128)S(1)}, u32[]{:S(2)}) copy-start(f32[32,4,128]{0,2,1:T(8,128)S(1)} %copy.97) | copy-start | bytes 196612
  290.1 2.7 copy-start.11
  290.1 2.7 copy-start.12
  292.8 31.6 %all-to-all-start.8 = ((bf16[32,32,512]{2,1,0:T(8,128)(2,1)}), bf16[32,32,512]{2,1,0:T(8,128)(2,1)S(1)}, u32[]{:S(2)}, u32[]{:S(2)}) async-start(bf16[32,32,512]{2,1,0:T(8,128)(2,1)} %broadcast_in_dim.47), calls=%async_computation.8 | async-start | bytes 2097152 | tf_op jit(solution)/shard_map/all_to_all | solution.py:45
  298.7 19.4 %collective-permute-start.4 = (bf16[32,64]{1,0:T(8,128)(2,1)S(1)}, bf16[32,64]{1,0:T(8,128)(2,1)S(1)}, u32[]{:S(2)}, u32[]{:S(2)}) collective-permute-start(bf16[32,64]{1,0:T(8,128)(2,1)S(1)} %get-tuple-element.25), channel_id=1, source_target_pairs={{0,1},{1,2},{2,3},{3,4},{4,5},{5,6},{6,7},{7,8},{8,9},{9,10},{10,1... | collective-permute-start | bytes 12296 | tf_op jit(solution)/shard_map/ppermute | solution.py:24
  300.7 18.1 %collective-permute-start.5 = (bf16[32,64]{1,0:T(8,128)(2,1)S(1)}, bf16[32,64]{1,0:T(8,128)(2,1)S(1)}, u32[]{:S(2)}, u32[]{:S(2)}) collective-permute-start(bf16[32,64]{1,0:T(8,128)(2,1)S(1)} %get-tuple-element.26), channel_id=1, source_target_pairs={{1,0},{2,1},{3,2},{4,3},{5,4},{6,5},{7,6},{8,7},{9,8},{10,9},{11,1... | collective-permute-start | bytes 12296 | tf_op jit(solution)/shard_map/ppermute | solution.py:26
Sparse Core Ops, SparseCore 0:
  10.5 111.5 all-gather.2

commit v3 on v1

--- a/solution.py
+++ b/solution.py
@@ -78,6 +78,8 @@
     ).astype(jnp.bfloat16)
     near_degree = jnp.sum(band_tiles.astype(jnp.float32), axis=1).reshape(frames)
     gathered = lax.all_gather(embeddings, "band", axis=0, tiled=True)
+    labels_band = band_gather(arrived.reshape(channels, frames))
+    labels_band, gathered = lax.optimization_barrier((labels_band, gathered))
     embed_width = embeddings.shape[1]
     partner_rows = gathered.reshape(-1, 128, embed_width)[partners]
     own_rows = embeddings.reshape(tile_count, 128, embed_width)
@@ -100,6 +102,7 @@
     residual = labels
     direction = labels
     first_norm = jnp.sum(residual * residual, axis=1)
+    scale_band = band_gather(norm_scale)
     for iteration in range(ITERS):
         lifted = (norm_scale[None, :] * direction).astype(jnp.bfloat16)
         padded = with_halo(lifted, ((("band", "seq"), 1),), RADIUS)
@@ -110,7 +113,11 @@
         near_term = jnp.einsum(
             "tcw,twa->cta", windows, band_tiles, preferred_element_type=jnp.float32
         ).reshape(channels, frames)
-        spread = jnp.transpose(band_gather(lifted), (1, 0, 2)).reshape(channels, -1, 128)
+        if iteration == 0:
+            lifted_band = (scale_band[:, None, :] * labels_band.astype(jnp.float32)).astype(jnp.bfloat16)
+        else:
+            lifted_band = band_gather(lifted)
+        spread = jnp.transpose(lifted_band, (1, 0, 2)).reshape(channels, -1, 128)
         far_tiles = spread[:, partners]
         far_term = jnp.einsum(
             "ctkj,tkji->cti", far_tiles, affinity, preferred_element_type=jnp.float32

time: 347 us -> 343 us (0.988)
  waiting for transfers between devices: 123 us -> 116 us
  starting transfers between devices: 59.1 us -> 64.3 us
  blocking collectives: 81.7 us -> 77.6 us
    all_to_all x3 -> x4, waiting for transfers between devices: 12.2 us -> 34.7 us  [band_gather(): lax.all_to_all(spread, 'band', split_axis=0, concat_axis=0, tiled=True)]
    all_gather x1, waiting for transfers between devices: 76.4 us -> 54.2 us  [on_device(): gathered = lax.all_gather(embeddings, 'band', axis=0, tiled=True)]
    ppermute x3, waiting for transfers between devices: 32.3 us -> 19 us  [with_halo(): lax.ppermute(tail, axis, [(i, (i + 1) % count) for i in range(ends)])]
    all_to_all x1, waiting for transfers between devices: 0.01 us -> 6.65 us  [on_device(): lax.all_to_all(ordered, 'band', split_axis=1, concat_axis=1, tiled=True)]
    all_to_all x3 -> x4, starting transfers between devices: 19.6 us -> 24.5 us  [band_gather(): lax.all_to_all(spread, 'band', split_axis=0, concat_axis=0, tiled=True)]
    all_to_all x6, blocking collectives: 81.7 us -> 77.6 us  [total_over_devices(): rows = lax.all_to_all(spread, axis, split_axis=0, concat_axis=0, tiled=True)]
  transfers between devices with their start and end apart: 11 -> 12, of which waited for: 9 -> 10; matrix products, arithmetic and copies ran while one was open for 7% -> 8% of each run, Pallas kernels for 0% -> 0%
where the time goes in v3:
time: 343 us; the launch traced here: 341 us
  waiting for transfers between devices  116 us (34%)
  blocking collectives  77.6 us (23%)
  starting transfers between devices  64.3 us (19%)
  local copies, waits for them, and re-layouts  40.7 us (12%)
  matrix products  18.2 us (5%)
  between operations  13.9 us (4%)
  other arithmetic  9.58 us (3%)
    all_to_all x6, blocking collectives, total_over_devices(): rows = lax.all_to_all(spread, axis, split_axis=0, concat_axis=0, tiled=True)  77.6 us
    all_gather x1, waiting for transfers between devices, on_device(): gathered = lax.all_gather(embeddings, 'band', axis=0, tiled=True)  54.2 us
    all_to_all x4, waiting for transfers between devices, band_gather(): lax.all_to_all(spread, 'band', split_axis=0, concat_axis=0, tiled=True)  34.7 us
    all_to_all x4, starting transfers between devices, band_gather(): lax.all_to_all(spread, 'band', split_axis=0, concat_axis=0, tiled=True)  24.5 us
    ppermute x3, starting transfers between devices, with_halo(): lax.ppermute(head, axis, [((i + 1) % count, i) for i in range(ends)])  23.8 us
    ppermute x3, waiting for transfers between devices, with_halo(): lax.ppermute(tail, axis, [(i, (i + 1) % count) for i in range(ends)])  19 us
    all_to_all x1, starting transfers between devices, on_device(): lax.all_to_all(ordered, 'band', split_axis=1, concat_axis=1, tiled=True)  10.2 us
    gather x1, local copies, waits for them, and re-layouts, on_device(): partner_rows = gathered.reshape(-1, 128, embed_width)[partners]  9.99 us
  transfers between devices with their start and end apart: 12, of which 10 were waited for; matrix products, arithmetic and copies ran while one was open for 8% of the time, Pallas kernels for 0%

profile of v3, /device:TPU:6, one launch (start us, length us, event | category | flops | bytes accessed | tf_op | source)
XLA Modules:
  0.0 340.6 jit_solution(14593774616092935248)
XLA Ops:
  6.5 0.7 all-gather.2.cloned.1.call-update
  7.3 0.7 convert_element_type.66
  7.9 0.8 broadcast_multiply_fusion
  9.4 1.3 reduce.14
  10.8 0.7 compare_select_fusion.1
  11.5 1.3 gather_fusion
  13.0 0.8 reshape.829
  13.7 10.2 %all-to-all-start = ((bf16[32,2,256]{2,1,0:T(2,128)(2,1)}), bf16[32,2,256]{2,1,0:T(2,128)(2,1)S(1)}, u32[]{:S(2)}, u32[]{:S(2)}) async-start(bf16[32,2,256]{2,1,0:T(2,128)(2,1)} %reshape.829), calls=%async_computation | async-start | bytes 65536 | tf_op jit(solution)/shard_map/all_to_all | solution.py:57
  24.0 1.0 reduce-window.9
  25.4 6.7 %all-to-all-done = bf16[32,2,256]{2,1,0:T(2,128)(2,1)S(1)} async-done(((bf16[32,2,256]{2,1,0:T(2,128)(2,1)}), bf16[32,2,256]{2,1,0:T(2,128)(2,1)S(1)}, u32[]{:S(2)}, u32[]{:S(2)}) %all-to-all-start) | async-done | bytes 32800 | tf_op jit(solution)/shard_map/all_to_all | solution.py:57
  32.2 1.2 broadcast_in_dim.40
  33.4 5.8 %all-to-all-start.1 = ((bf16[32,32,512]{2,1,0:T(8,128)(2,1)}), bf16[32,32,512]{2,1,0:T(8,128)(2,1)S(1)}, u32[]{:S(2)}, u32[]{:S(2)}) async-start(bf16[32,32,512]{2,1,0:T(8,128)(2,1)} %broadcast_in_dim.40), calls=%async_computation.1 | async-start | bytes 2097152 | tf_op jit(solution)/shard_map/all_to_all | solution.py:45
  39.5 4.5 %gather_fusion.1 = s32[1024]{0:T(1024)S(1)} fusion(s32[640]{0:T(1024)S(1)} %convert_reduce_fusion.1, s32[1024]{0:T(1024)S(1)} %broadcast_clamp_fusion), kind=kCustom, calls=%fused_computation.1 | custom fusion | bytes 12288 | tf_op jit(solution)/shard_map/gather | solution.py:73
  44.2 2.3 gather_fusion.2
  46.5 6.8 %gather_fusion.3 = pred[1024]{0:T(1024)(128)(4,1)S(1)} fusion(pred[640]{0:T(1024)(128)(4,1)S(1)} %compare_and_fusion.1, s32[1024]{0:T(1024)S(1)} %broadcast_clamp_fusion), kind=kCustom, calls=%fused_computation.3 | custom fusion | bytes 6144 | tf_op jit(solution)/shard_map/gather | solution.py:74
  54.2 17.5 %all-to-all-done.1 = bf16[32,32,512]{2,1,0:T(8,128)(2,1)S(1)} async-done(((bf16[32,32,512]{2,1,0:T(8,128)(2,1)}), bf16[32,32,512]{2,1,0:T(8,128)(2,1)S(1)}, u32[]{:S(2)}, u32[]{:S(2)}) %all-to-all-start.1) | async-done | bytes 1048608 | tf_op jit(solution)/shard_map/all_to_all | solution.py:45
  71.7 54.2 %all-gather.2.cloned.1.call-done = bf16[16384,256]{1,0:T(8,128)(2,1)} async-done(((bf16[512,256]{1,0:T(8,128)(2,1)}), bf16[16384,256]{1,0:T(8,128)(2,1)}) %all-gather.2.cloned.1.call-update) | async-done | bytes 8388624 | tf_op jit(solution)/shard_map/all_gather | solution.py:80
  125.8 10.0 %gather_fusion.4 = bf16[128,128,256]{2,1,0:T(8,128)(2,1)} fusion(bf16[128,128,256]{2,1,0:T(8,128)(2,1)} %bitcast.181, s32[1024]{0:T(1024)S(1)} %pad_clamp_fusion), kind=kCustom, calls=%fused_computation.4 | custom fusion | bytes 16777728 | tf_op jit(solution)/shard_map/gather | solution.py:84
  135.8 7.7 %convert_reduce_fusion = (f32[4,128]{1,0:T(4,128)S(1)}, bf16[4,32,128,128]{3,2,1,0:T(8,128)(2,1)}) fusion(f32[4,32]{1,0:T(4,128)S(1)} %convert_multiply_fusion.6, bf16[4,32,128,256]{3,2,1,0:T(8,128)(2,1)} %bitcast.182, bf16[4,128,256,1]{2,1,3,0:T(8,128)(2,1)S(1)} %bitcast.198), kind=kOutput, calls=%fused_computation.8 | convolution fusion | flops 1086324224 | bytes 12847616 | tf_op jit(solution)/shard_map/tkje,tie->tkji/dot_general | solution.py:86
  143.6 1.9 collective-permute-start
  145.5 7.9 %collective-permute-start.1 = (bf16[32,64]{1,0:T(8,128)(2,1)S(1)}, bf16[32,64]{1,0:T(8,128)(2,1)S(1)}, u32[]{:S(2)}, u32[]{:S(2)}) collective-permute-start(bf16[32,64]{1,0:T(8,128)(2,1)S(1)} %get-tuple-element.42), channel_id=1, source_target_pairs={{1,0},{2,1},{3,2},{4,3},{5,4},{6,5},{7,6},{8,7},{9,8},{10,9},{11,1... | collective-permute-start | bytes 12296 | tf_op jit(solution)/shard_map/ppermute | solution.py:26
  154.0 7.1 %all-to-all-start.2 = ((f32[32,1,512]{2,1,0:T(1,128)}), f32[32,1,512]{2,1,0:T(1,128)S(1)}, u32[]{:S(2)}, u32[]{:S(2)}) async-start(f32[32,1,512]{2,1,0:T(1,128)} %mul.397), calls=%async_computation.2 | async-start | bytes 131072 | tf_op jit(solution)/shard_map/all_to_all | solution.py:45
  161.9 7.3 %all-to-all-done.2 = f32[32,1,512]{2,1,0:T(1,128)S(1)} async-done(((f32[32,1,512]{2,1,0:T(1,128)}), f32[32,1,512]{2,1,0:T(1,128)S(1)}, u32[]{:S(2)}, u32[]{:S(2)}) %all-to-all-start.2) | async-done | bytes 65568 | tf_op jit(solution)/shard_map/all_to_all | solution.py:45
  171.5 0.8 gather_fusion.5
  172.2 2.9 fusion.3
  175.6 12.8 %all_to_all.56 = f32[16,1,128]{2,1,0:T(1,128)S(1)} all-to-all(f32[16,1,128]{2,1,0:T(1,128)S(1)} %reshape.831), channel_id=1, replica_groups=mesh['band'=32,'seq'=16] {'seq'}, dimensions={0} | all-to-all | bytes 16384 | tf_op jit(solution)/shard_map/all_to_all | solution.py:37
  189.8 12.9 %all_to_all.57 = f32[32,1,128]{2,1,0:T(1,128)S(1)} all-to-all(f32[32,1,128]{2,1,0:T(1,128)S(1)} %reshape.833), channel_id=1, replica_groups=mesh['band'=32,'seq'=16] {'band'}, dimensions={0} | all-to-all | bytes 32768 | tf_op jit(solution)/shard_map/all_to_all | solution.py:37
  203.6 1.1 broadcast_in_dim.44
  204.7 5.8 %all-to-all-start.5 = ((bf16[32,32,512]{2,1,0:T(8,128)(2,1)}), bf16[32,32,512]{2,1,0:T(8,128)(2,1)S(1)}, u32[]{:S(2)}, u32[]{:S(2)}) async-start(bf16[32,32,512]{2,1,0:T(8,128)(2,1)} %broadcast_in_dim.44), calls=%async_computation.5 | async-start | bytes 2097152 | tf_op jit(solution)/shard_map/all_to_all | solution.py:45
  210.6 1.9 collective-permute-start.2
  212.5 7.9 %collective-permute-start.3 = (bf16[32,64]{1,0:T(8,128)(2,1)S(1)}, bf16[32,64]{1,0:T(8,128)(2,1)S(1)}, u32[]{:S(2)}, u32[]{:S(2)}) collective-permute-start(bf16[32,64]{1,0:T(8,128)(2,1)S(1)} %get-tuple-element.36), channel_id=1, source_target_pairs={{1,0},{2,1},{3,2},{4,3},{5,4},{6,5},{7,6},{8,7},{9,8},{10,9},{11,1... | collective-permute-start | bytes 12296 | tf_op jit(solution)/shard_map/ppermute | solution.py:26
  220.4 9.6 %collective-permute-done.2 = bf16[32,64]{1,0:T(8,128)(2,1)S(1)} collective-permute-done((bf16[32,64]{1,0:T(8,128)(2,1)S(1)}, bf16[32,64]{1,0:T(8,128)(2,1)S(1)}, u32[]{:S(2)}, u32[]{:S(2)}) %collective-permute-start.2) | collective-permute-done | bytes 4128 | tf_op jit(solution)/shard_map/ppermute | solution.py:24
  231.2 4.9 %all-to-all-done.5 = bf16[32,32,512]{2,1,0:T(8,128)(2,1)S(1)} async-done(((bf16[32,32,512]{2,1,0:T(8,128)(2,1)}), bf16[32,32,512]{2,1,0:T(8,128)(2,1)S(1)}, u32[]{:S(2)}, u32[]{:S(2)}) %all-to-all-start.5) | async-done | bytes 1048608 | tf_op jit(solution)/shard_map/all_to_all | solution.py:45
  238.0 0.8 gather_fusion.6
  238.8 2.9 fusion.2
  242.1 10.3 %all_to_all.58 = f32[16,3,32]{2,1,0:T(4,128)S(1)} all-to-all(f32[16,3,32]{2,1,0:T(4,128)S(1)} %broadcast_in_dim.45), channel_id=1, replica_groups=mesh['band'=32,'seq'=16] {'seq'}, dimensions={0} | all-to-all | bytes 12288 | tf_op jit(solution)/shard_map/all_to_all | solution.py:37
  252.4 15.9 %all_to_all.59 = f32[32,3,32]{2,1,0:T(4,128)S(1)} all-to-all(f32[32,3,32]{2,1,0:T(4,128)S(1)} %broadcast_in_dim.46), channel_id=1, replica_groups=mesh['band'=32,'seq'=16] {'band'}, dimensions={0} | all-to-all | bytes 24576 | tf_op jit(solution)/shard_map/all_to_all | solution.py:37
  268.5 1.1 broadcast_in_dim.47
  269.6 5.8 %all-to-all-start.8 = ((bf16[32,32,512]{2,1,0:T(8,128)(2,1)}), bf16[32,32,512]{2,1,0:T(8,128)(2,1)S(1)}, u32[]{:S(2)}, u32[]{:S(2)}) async-start(bf16[32,32,512]{2,1,0:T(8,128)(2,1)} %broadcast_in_dim.47), calls=%async_computation.8 | async-start | bytes 2097152 | tf_op jit(solution)/shard_map/all_to_all | solution.py:45
  275.5 1.9 collective-permute-start.4
  277.4 8.1 %collective-permute-start.5 = (bf16[32,64]{1,0:T(8,128)(2,1)S(1)}, bf16[32,64]{1,0:T(8,128)(2,1)S(1)}, u32[]{:S(2)}, u32[]{:S(2)}) collective-permute-start(bf16[32,64]{1,0:T(8,128)(2,1)S(1)} %get-tuple-element.30), channel_id=1, source_target_pairs={{1,0},{2,1},{3,2},{4,3},{5,4},{6,5},{7,6},{8,7},{9,8},{10,9},{11,1... | collective-permute-start | bytes 12296 | tf_op jit(solution)/shard_map/ppermute | solution.py:26
  285.5 9.4 %collective-permute-done.4 = bf16[32,64]{1,0:T(8,128)(2,1)S(1)} collective-permute-done((bf16[32,64]{1,0:T(8,128)(2,1)S(1)}, bf16[32,64]{1,0:T(8,128)(2,1)S(1)}, u32[]{:S(2)}, u32[]{:S(2)}) %collective-permute-start.4) | collective-permute-done | bytes 4128 | tf_op jit(solution)/shard_map/ppermute | solution.py:24
  296.2 5.0 %all-to-all-done.8 = bf16[32,32,512]{2,1,0:T(8,128)(2,1)S(1)} async-done(((bf16[32,32,512]{2,1,0:T(8,128)(2,1)}), bf16[32,32,512]{2,1,0:T(8,128)(2,1)S(1)}, u32[]{:S(2)}, u32[]{:S(2)}) %all-to-all-start.8) | async-done | bytes 1048608 | tf_op jit(solution)/shard_map/all_to_all | solution.py:45
  303.2 0.8 gather_fusion.7
  303.9 2.9 fusion.1
  307.3 10.1 %all_to_all.60 = f32[16,1,32]{2,1,0:T(1,128)S(1)} all-to-all(f32[16,1,32]{2,1,0:T(1,128)S(1)} %broadcast_in_dim.48), channel_id=1, replica_groups=mesh['band'=32,'seq'=16] {'seq'}, dimensions={0} | all-to-all | bytes 4096 | tf_op jit(solution)/shard_map/all_to_all | solution.py:37
  317.4 15.6 %all_to_all.61 = f32[32,1,32]{2,1,0:T(1,128)S(1)} all-to-all(f32[32,1,32]{2,1,0:T(1,128)S(1)} %broadcast_in_dim.49), channel_id=1, replica_groups=mesh['band'=32,'seq'=16] {'band'}, dimensions={0} | all-to-all | bytes 8192 | tf_op jit(solution)/shard_map/all_to_all | solution.py:37
  333.1 0.7 fusion.19
  (99 shorter events, 16.6 us)
Async XLA Ops:
  6.5 46.8 %copy-start.1 = (s32[4,32]{1,0:T(4,128)S(1)}, s32[4,32]{1,0:T(4,128)}, u32[]{:S(2)}) copy-start(s32[4,32]{1,0:T(4,128)} %param.12) | copy-start | bytes 1540
  6.5 47.6 %copy-start.2 = (s32[4,32]{1,0:T(4,128)S(1)}, s32[4,32]{1,0:T(4,128)}, u32[]{:S(2)}) copy-start(s32[4,32]{1,0:T(4,128)} %param.13) | copy-start | bytes 1540
  6.5 119.3 %all-gather.2.cloned.1.call-start = ((), (), s32[]{:S(2)}) async-start(), calls=%async_computation.11 | async-start | bytes 8650752 | tf_op jit(solution)/shard_map/all_gather | solution.py:80
  13.7 18.3 %all-to-all-start = ((bf16[32,2,256]{2,1,0:T(2,128)(2,1)}), bf16[32,2,256]{2,1,0:T(2,128)(2,1)S(1)}, u32[]{:S(2)}, u32[]{:S(2)}) async-start(bf16[32,2,256]{2,1,0:T(2,128)(2,1)} %reshape.829), calls=%async_computation | async-start | bytes 65536 | tf_op jit(solution)/shard_map/all_to_all | solution.py:57
  33.4 38.2 %all-to-all-start.1 = ((bf16[32,32,512]{2,1,0:T(8,128)(2,1)}), bf16[32,32,512]{2,1,0:T(8,128)(2,1)S(1)}, u32[]{:S(2)}, u32[]{:S(2)}) async-start(bf16[32,32,512]{2,1,0:T(8,128)(2,1)} %broadcast_in_dim.40), calls=%async_computation.1 | async-start | bytes 2097152 | tf_op jit(solution)/shard_map/all_to_all | solution.py:45
  125.8 10.0 %copy-start = (bf16[512,256]{1,0:T(8,128)(2,1)S(1)}, bf16[512,256]{1,0:T(8,128)(2,1)}, u32[]{:S(2)}) copy-start(bf16[512,256]{1,0:T(8,128)(2,1)} %param.11) | copy-start | bytes 786436
  143.6 17.6 %collective-permute-start = (bf16[32,64]{1,0:T(8,128)(2,1)S(1)}, bf16[32,64]{1,0:T(8,128)(2,1)S(1)}, u32[]{:S(2)}, u32[]{:S(2)}) collective-permute-start(bf16[32,64]{1,0:T(8,128)(2,1)S(1)} %get-tuple-element.41), channel_id=1, source_target_pairs={{0,1},{1,2},{2,3},{3,4},{4,5},{5,6},{6,7},{7,8},{8,9},{9,10},{10,1... | collective-permute-start | bytes 12296 | tf_op jit(solution)/shard_map/ppermute | solution.py:24
  145.5 15.7 %collective-permute-start.1 = (bf16[32,64]{1,0:T(8,128)(2,1)S(1)}, bf16[32,64]{1,0:T(8,128)(2,1)S(1)}, u32[]{:S(2)}, u32[]{:S(2)}) collective-permute-start(bf16[32,64]{1,0:T(8,128)(2,1)S(1)} %get-tuple-element.42), channel_id=1, source_target_pairs={{1,0},{2,1},{3,2},{4,3},{5,4},{6,5},{7,6},{8,7},{9,8},{10,9},{11,1... | collective-permute-start | bytes 12296 | tf_op jit(solution)/shard_map/ppermute | solution.py:26
  154.0 15.2 %all-to-all-start.2 = ((f32[32,1,512]{2,1,0:T(1,128)}), f32[32,1,512]{2,1,0:T(1,128)S(1)}, u32[]{:S(2)}, u32[]{:S(2)}) async-start(f32[32,1,512]{2,1,0:T(1,128)} %mul.397), calls=%async_computation.2 | async-start | bytes 131072 | tf_op jit(solution)/shard_map/all_to_all | solution.py:45
  204.7 31.3 %all-to-all-start.5 = ((bf16[32,32,512]{2,1,0:T(8,128)(2,1)}), bf16[32,32,512]{2,1,0:T(8,128)(2,1)S(1)}, u32[]{:S(2)}, u32[]{:S(2)}) async-start(bf16[32,32,512]{2,1,0:T(8,128)(2,1)} %broadcast_in_dim.44), calls=%async_computation.5 | async-start | bytes 2097152 | tf_op jit(solution)/shard_map/all_to_all | solution.py:45
  210.6 19.4 %collective-permute-start.2 = (bf16[32,64]{1,0:T(8,128)(2,1)S(1)}, bf16[32,64]{1,0:T(8,128)(2,1)S(1)}, u32[]{:S(2)}, u32[]{:S(2)}) collective-permute-start(bf16[32,64]{1,0:T(8,128)(2,1)S(1)} %get-tuple-element.35), channel_id=1, source_target_pairs={{0,1},{1,2},{2,3},{3,4},{4,5},{5,6},{6,7},{7,8},{8,9},{9,10},{10,1... | collective-permute-start | bytes 12296 | tf_op jit(solution)/shard_map/ppermute | solution.py:24
  212.5 17.9 %collective-permute-start.3 = (bf16[32,64]{1,0:T(8,128)(2,1)S(1)}, bf16[32,64]{1,0:T(8,128)(2,1)S(1)}, u32[]{:S(2)}, u32[]{:S(2)}) collective-permute-start(bf16[32,64]{1,0:T(8,128)(2,1)S(1)} %get-tuple-element.36), channel_id=1, source_target_pairs={{1,0},{2,1},{3,2},{4,3},{5,4},{6,5},{7,6},{8,7},{9,8},{10,9},{11,1... | collective-permute-start | bytes 12296 | tf_op jit(solution)/shard_map/ppermute | solution.py:26
  269.6 31.6 %all-to-all-start.8 = ((bf16[32,32,512]{2,1,0:T(8,128)(2,1)}), bf16[32,32,512]{2,1,0:T(8,128)(2,1)S(1)}, u32[]{:S(2)}, u32[]{:S(2)}) async-start(bf16[32,32,512]{2,1,0:T(8,128)(2,1)} %broadcast_in_dim.47), calls=%async_computation.8 | async-start | bytes 2097152 | tf_op jit(solution)/shard_map/all_to_all | solution.py:45
  275.5 19.4 %collective-permute-start.4 = (bf16[32,64]{1,0:T(8,128)(2,1)S(1)}, bf16[32,64]{1,0:T(8,128)(2,1)S(1)}, u32[]{:S(2)}, u32[]{:S(2)}) collective-permute-start(bf16[32,64]{1,0:T(8,128)(2,1)S(1)} %get-tuple-element.29), channel_id=1, source_target_pairs={{0,1},{1,2},{2,3},{3,4},{4,5},{5,6},{6,7},{7,8},{8,9},{9,10},{10,1... | collective-permute-start | bytes 12296 | tf_op jit(solution)/shard_map/ppermute | solution.py:24
  277.4 18.1 %collective-permute-start.5 = (bf16[32,64]{1,0:T(8,128)(2,1)S(1)}, bf16[32,64]{1,0:T(8,128)(2,1)S(1)}, u32[]{:S(2)}, u32[]{:S(2)}) collective-permute-start(bf16[32,64]{1,0:T(8,128)(2,1)S(1)} %get-tuple-element.30), channel_id=1, source_target_pairs={{1,0},{2,1},{3,2},{4,3},{5,4},{6,5},{7,6},{8,7},{9,8},{10,9},{11,1... | collective-permute-start | bytes 12296 | tf_op jit(solution)/shard_map/ppermute | solution.py:26
Sparse Core Ops, SparseCore 0:
  10.5 115.2 all-gather.1

commit v4 on v3

--- a/solution.py
+++ b/solution.py
@@ -31,12 +31,8 @@
 
 
 def total_over_devices(values):
-    for axis in ("seq", "band"):
-        count = lax.axis_size(axis)
-        spread = jnp.broadcast_to(values[None], (count,) + values.shape)
-        rows = lax.all_to_all(spread, axis, split_axis=0, concat_axis=0, tiled=True)
-        values = jnp.sum(rows, axis=0)
-    return values
+    values = lax.optimization_barrier(lax.psum(values, "seq"))
+    return lax.psum(values, "band")
 
 
 def band_gather(block):

time: 343 us -> 530 us (1.55); the launches traced: 341 us -> 520 us
  blocking collectives: 77.6 us -> 257 us
  starting transfers between devices: 64.3 us -> 86.3 us
  waiting for transfers between devices: 116 us -> 96.8 us
    psum x0 -> x6, blocking collectives: none -> 257 us  [the longest x3 184 us: total_over_devices(): return lax.psum(values, 'band')]
    all_to_all x6 -> x0, blocking collectives: 77.6 us -> none  [total_over_devices(): rows = lax.all_to_all(spread, axis, split_axis=0, concat_axis=0, tiled=True)]
    all_to_all x4, starting transfers between devices: 24.5 us -> 46.5 us  [band_gather(): lax.all_to_all(spread, 'band', split_axis=0, concat_axis=0, tiled=True)]
    ppermute x3, waiting for transfers between devices: 19 us -> 0.01 us  [with_halo(): lax.ppermute(tail, axis, [(i, (i + 1) % count) for i in range(ends)])]
  transfers between devices with their start and end apart: 12 -> 12, of which waited for: 10 -> 8; matrix products, arithmetic and copies ran while one was open for 8% -> 5% of each run, Pallas kernels for 0% -> 0%
where the time goes in v4:
time: 530 us; the launch traced here: 520 us
  blocking collectives  257 us (48%)
  waiting for transfers between devices  96.8 us (18%)
  starting transfers between devices  86.3 us (16%)
  local copies, waits for them, and re-layouts  39.8 us (8%)
  matrix products  18.2 us (3%)
  between operations  13.8 us (3%)
  other arithmetic  8.04 us (2%)
    psum x3, blocking collectives, total_over_devices(): return lax.psum(values, 'band')  184 us
    psum x3, blocking collectives, total_over_devices(): values = lax.optimization_barrier(lax.psum(values, 'seq'))  73.4 us
    all_gather x1, waiting for transfers between devices, on_device(): gathered = lax.all_gather(embeddings, 'band', axis=0, tiled=True)  54.2 us
    all_to_all x4, starting transfers between devices, band_gather(): lax.all_to_all(spread, 'band', split_axis=0, concat_axis=0, tiled=True)  46.5 us
    all_to_all x4, waiting for transfers between devices, band_gather(): lax.all_to_all(spread, 'band', split_axis=0, concat_axis=0, tiled=True)  32.4 us
    ppermute x3, starting transfers between devices, with_halo(): lax.ppermute(head, axis, [((i + 1) % count, i) for i in range(ends)])  23.8 us
  transfers between devices with their start and end apart: 12, of which 8 were waited for; matrix products, arithmetic and copies ran while one was open for 5% of the time, Pallas kernels for 0%

profile of v4, /device:TPU:6, one launch (start us, length us, event | category | flops | bytes accessed | tf_op | source)
XLA Modules:
  0.0 520.4 jit_solution(2625239210406155558)
XLA Ops:
  6.5 0.7 all-gather.2.cloned.1.call-update
  7.3 0.7 convert_element_type.66
  7.9 0.8 broadcast_multiply_fusion
  9.4 1.3 reduce.12
  10.8 0.7 compare_select_fusion.1
  11.5 1.3 gather_fusion
  13.0 0.8 reshape.817
  13.7 10.2 %all-to-all-start = ((bf16[32,2,256]{2,1,0:T(2,128)(2,1)}), bf16[32,2,256]{2,1,0:T(2,128)(2,1)S(1)}, u32[]{:S(2)}, u32[]{:S(2)}) async-start(bf16[32,2,256]{2,1,0:T(2,128)(2,1)} %reshape.817), calls=%async_computation | async-start | bytes 65536 | tf_op jit(solution)/shard_map/all_to_all | solution.py:53
  24.0 1.0 reduce-window.9
  25.4 6.7 %all-to-all-done = bf16[32,2,256]{2,1,0:T(2,128)(2,1)S(1)} async-done(((bf16[32,2,256]{2,1,0:T(2,128)(2,1)}), bf16[32,2,256]{2,1,0:T(2,128)(2,1)S(1)}, u32[]{:S(2)}, u32[]{:S(2)}) %all-to-all-start) | async-done | bytes 32800 | tf_op jit(solution)/shard_map/all_to_all | solution.py:53
  32.2 1.2 broadcast_in_dim.28
  33.4 5.8 %all-to-all-start.1 = ((bf16[32,32,512]{2,1,0:T(8,128)(2,1)}), bf16[32,32,512]{2,1,0:T(8,128)(2,1)S(1)}, u32[]{:S(2)}, u32[]{:S(2)}) async-start(bf16[32,32,512]{2,1,0:T(8,128)(2,1)} %broadcast_in_dim.28), calls=%async_computation.1 | async-start | bytes 2097152 | tf_op jit(solution)/shard_map/all_to_all | solution.py:41
  39.5 4.5 gather_fusion.1
  44.2 2.3 gather_fusion.2
  46.5 6.8 %gather_fusion.3 = pred[1024]{0:T(1024)(128)(4,1)S(1)} fusion(pred[640]{0:T(1024)(128)(4,1)S(1)} %compare_and_fusion.1, s32[1024]{0:T(1024)S(1)} %broadcast_clamp_fusion), kind=kCustom, calls=%fused_computation.3 | custom fusion | bytes 6144 | tf_op jit(solution)/shard_map/gather | solution.py:70
  54.2 17.5 %all-to-all-done.1 = bf16[32,32,512]{2,1,0:T(8,128)(2,1)S(1)} async-done(((bf16[32,32,512]{2,1,0:T(8,128)(2,1)}), bf16[32,32,512]{2,1,0:T(8,128)(2,1)S(1)}, u32[]{:S(2)}, u32[]{:S(2)}) %all-to-all-start.1) | async-done | bytes 1048608 | tf_op jit(solution)/shard_map/all_to_all | solution.py:41
  71.7 54.2 %all-gather.2.cloned.1.call-done = bf16[16384,256]{1,0:T(8,128)(2,1)} async-done(((bf16[512,256]{1,0:T(8,128)(2,1)}), bf16[16384,256]{1,0:T(8,128)(2,1)}) %all-gather.2.cloned.1.call-update) | async-done | bytes 8388624 | tf_op jit(solution)/shard_map/all_gather | solution.py:76
  125.8 10.0 %gather_fusion.4 = bf16[128,128,256]{2,1,0:T(8,128)(2,1)} fusion(bf16[128,128,256]{2,1,0:T(8,128)(2,1)} %bitcast.181, s32[1024]{0:T(1024)S(1)} %pad_clamp_fusion), kind=kCustom, calls=%fused_computation.4 | custom fusion | bytes 16777728 | tf_op jit(solution)/shard_map/gather | solution.py:80
  135.8 7.7 %convert_reduce_fusion = (f32[4,128]{1,0:T(4,128)S(1)}, bf16[4,32,128,128]{3,2,1,0:T(8,128)(2,1)}) fusion(f32[4,32]{1,0:T(4,128)S(1)} %convert_multiply_fusion.6, bf16[4,32,128,256]{3,2,1,0:T(8,128)(2,1)} %bitcast.182, bf16[4,128,256,1]{2,1,3,0:T(8,128)(2,1)S(1)} %bitcast.198), kind=kOutput, calls=%fused_computation.8 | convolution fusion | flops 1086324224 | bytes 12847616 | tf_op jit(solution)/shard_map/tkje,tie->tkji/dot_general | solution.py:82
  143.6 1.9 collective-permute-start
  145.5 7.9 %collective-permute-start.1 = (bf16[32,64]{1,0:T(8,128)(2,1)S(1)}, bf16[32,64]{1,0:T(8,128)(2,1)S(1)}, u32[]{:S(2)}, u32[]{:S(2)}) collective-permute-start(bf16[32,64]{1,0:T(8,128)(2,1)S(1)} %get-tuple-element.42), channel_id=1, source_target_pairs={{1,0},{2,1},{3,2},{4,3},{5,4},{6,5},{7,6},{8,7},{9,8},{10,9},{11,1... | collective-permute-start | bytes 12296 | tf_op jit(solution)/shard_map/ppermute | solution.py:26
  154.0 7.1 %all-to-all-start.2 = ((f32[32,1,512]{2,1,0:T(1,128)}), f32[32,1,512]{2,1,0:T(1,128)S(1)}, u32[]{:S(2)}, u32[]{:S(2)}) async-start(f32[32,1,512]{2,1,0:T(1,128)} %mul.397), calls=%async_computation.2 | async-start | bytes 131072 | tf_op jit(solution)/shard_map/all_to_all | solution.py:41
  161.9 7.3 %all-to-all-done.2 = f32[32,1,512]{2,1,0:T(1,128)S(1)} async-done(((f32[32,1,512]{2,1,0:T(1,128)}), f32[32,1,512]{2,1,0:T(1,128)S(1)}, u32[]{:S(2)}, u32[]{:S(2)}) %all-to-all-start.2) | async-done | bytes 65568 | tf_op jit(solution)/shard_map/all_to_all | solution.py:41
  171.5 0.8 gather_fusion.5
  172.2 2.9 fusion.3
  175.5 23.5 %psum.42 = f32[4,32]{1,0:T(4,128)S(1)} all-reduce(f32[4,32]{1,0:T(4,128)S(1)} %pad_maximum_fusion.6), channel_id=1, replica_groups=mesh['band'=32,'seq'=16] {'seq'}, use_global_device_ids=true, to_apply=%region_8.9 | all-reduce | flops 128 | bytes 1024 | tf_op jit(solution)/shard_map/psum | solution.py:34
  199.1 60.8 %psum.43 = f32[4,32]{1,0:T(4,128)S(1)} all-reduce(f32[4,32]{1,0:T(4,128)S(1)} %psum.42), channel_id=1, replica_groups=mesh['band'=32,'seq'=16] {'band'}, use_global_device_ids=true, to_apply=%region_9.10 | all-reduce | flops 128 | bytes 1024 | tf_op jit(solution)/shard_map/psum | solution.py:35
  260.0 1.1 broadcast_in_dim.30
  261.0 17.3 %all-to-all-start.3 = ((bf16[32,32,512]{2,1,0:T(8,128)(2,1)}), bf16[32,32,512]{2,1,0:T(8,128)(2,1)S(1)}, u32[]{:S(2)}, u32[]{:S(2)}) async-start(bf16[32,32,512]{2,1,0:T(8,128)(2,1)} %broadcast_in_dim.30), calls=%async_computation.3 | async-start | bytes 2097152 | tf_op jit(solution)/shard_map/all_to_all | solution.py:41
  278.4 1.9 collective-permute-start.2
  280.4 7.9 %collective-permute-start.3 = (bf16[32,64]{1,0:T(8,128)(2,1)S(1)}, bf16[32,64]{1,0:T(8,128)(2,1)S(1)}, u32[]{:S(2)}, u32[]{:S(2)}) collective-permute-start(bf16[32,64]{1,0:T(8,128)(2,1)S(1)} %get-tuple-element.36), channel_id=1, source_target_pairs={{1,0},{2,1},{3,2},{4,3},{5,4},{6,5},{7,6},{8,7},{9,8},{10,9},{11,1... | collective-permute-start | bytes 12296 | tf_op jit(solution)/shard_map/ppermute | solution.py:26
  288.2 1.5 collective-permute-done.3
  290.5 3.8 all-to-all-done.3
  296.2 0.8 gather_fusion.6
  297.0 2.9 fusion.2
  300.3 24.9 %psum.44 = f32[3,32]{1,0:T(4,128)S(1)} all-reduce(f32[3,32]{1,0:T(4,128)S(1)} %pad_maximum_fusion.7), channel_id=1, replica_groups=mesh['band'=32,'seq'=16] {'seq'}, use_global_device_ids=true, to_apply=%region_13.14 | all-reduce | flops 96 | bytes 768 | tf_op jit(solution)/shard_map/psum | solution.py:34
  325.2 61.6 %psum.45 = f32[3,32]{1,0:T(4,128)S(1)} all-reduce(f32[3,32]{1,0:T(4,128)S(1)} %psum.44), channel_id=1, replica_groups=mesh['band'=32,'seq'=16] {'band'}, use_global_device_ids=true, to_apply=%region_14.15 | all-reduce | flops 96 | bytes 768 | tf_op jit(solution)/shard_map/psum | solution.py:35
  386.9 1.1 broadcast_in_dim.31
  388.0 16.3 %all-to-all-start.4 = ((bf16[32,32,512]{2,1,0:T(8,128)(2,1)}), bf16[32,32,512]{2,1,0:T(8,128)(2,1)S(1)}, u32[]{:S(2)}, u32[]{:S(2)}) async-start(bf16[32,32,512]{2,1,0:T(8,128)(2,1)} %broadcast_in_dim.31), calls=%async_computation.4 | async-start | bytes 2097152 | tf_op jit(solution)/shard_map/all_to_all | solution.py:41
  404.4 1.9 collective-permute-start.4
  406.3 8.1 %collective-permute-start.5 = (bf16[32,64]{1,0:T(8,128)(2,1)S(1)}, bf16[32,64]{1,0:T(8,128)(2,1)S(1)}, u32[]{:S(2)}, u32[]{:S(2)}) collective-permute-start(bf16[32,64]{1,0:T(8,128)(2,1)S(1)} %get-tuple-element.30), channel_id=1, source_target_pairs={{1,0},{2,1},{3,2},{4,3},{5,4},{6,5},{7,6},{8,7},{9,8},{10,9},{11,1... | collective-permute-start | bytes 12296 | tf_op jit(solution)/shard_map/ppermute | solution.py:26
  414.4 1.3 collective-permute-done.5
  416.4 3.8 all-to-all-done.4
  422.2 0.8 gather_fusion.7
  422.9 2.9 fusion.1
  426.3 24.9 %psum.46 = f32[1,32]{1,0:T(1,128)S(1)} all-reduce(f32[1,32]{1,0:T(1,128)S(1)} %bitcast.213), channel_id=1, replica_groups=mesh['band'=32,'seq'=16] {'seq'}, use_global_device_ids=true, to_apply=%region_16.17 | all-reduce | flops 32 | bytes 256 | tf_op jit(solution)/shard_map/psum | solution.py:34
  451.2 61.6 %psum.47 = f32[32]{0:T(128)S(1)} all-reduce(f32[32]{0:T(128)S(1)} %bitcast.214), channel_id=1, replica_groups=mesh['band'=32,'seq'=16] {'band'}, use_global_device_ids=true, to_apply=%region_17.18 | all-reduce | flops 32 | bytes 256 | tf_op jit(solution)/shard_map/psum | solution.py:35
  512.8 0.7 fusion.19
  (80 shorter events, 13.0 us)
Async XLA Ops:
  6.5 46.8 %copy-start.1 = (s32[4,32]{1,0:T(4,128)S(1)}, s32[4,32]{1,0:T(4,128)}, u32[]{:S(2)}) copy-start(s32[4,32]{1,0:T(4,128)} %param.12) | copy-start | bytes 1540
  6.5 47.6 %copy-start.2 = (s32[4,32]{1,0:T(4,128)S(1)}, s32[4,32]{1,0:T(4,128)}, u32[]{:S(2)}) copy-start(s32[4,32]{1,0:T(4,128)} %param.13) | copy-start | bytes 1540
  6.5 119.3 %all-gather.2.cloned.1.call-start = ((), (), s32[]{:S(2)}) async-start(), calls=%async_computation.5 | async-start | bytes 8650752 | tf_op jit(solution)/shard_map/all_gather | solution.py:76
  13.7 18.3 %all-to-all-start = ((bf16[32,2,256]{2,1,0:T(2,128)(2,1)}), bf16[32,2,256]{2,1,0:T(2,128)(2,1)S(1)}, u32[]{:S(2)}, u32[]{:S(2)}) async-start(bf16[32,2,256]{2,1,0:T(2,128)(2,1)} %reshape.817), calls=%async_computation | async-start | bytes 65536 | tf_op jit(solution)/shard_map/all_to_all | solution.py:53
  33.4 38.2 %all-to-all-start.1 = ((bf16[32,32,512]{2,1,0:T(8,128)(2,1)}), bf16[32,32,512]{2,1,0:T(8,128)(2,1)S(1)}, u32[]{:S(2)}, u32[]{:S(2)}) async-start(bf16[32,32,512]{2,1,0:T(8,128)(2,1)} %broadcast_in_dim.28), calls=%async_computation.1 | async-start | bytes 2097152 | tf_op jit(solution)/shard_map/all_to_all | solution.py:41
  125.8 10.0 %copy-start = (bf16[512,256]{1,0:T(8,128)(2,1)S(1)}, bf16[512,256]{1,0:T(8,128)(2,1)}, u32[]{:S(2)}) copy-start(bf16[512,256]{1,0:T(8,128)(2,1)} %param.11) | copy-start | bytes 786436
  143.6 17.6 %collective-permute-start = (bf16[32,64]{1,0:T(8,128)(2,1)S(1)}, bf16[32,64]{1,0:T(8,128)(2,1)S(1)}, u32[]{:S(2)}, u32[]{:S(2)}) collective-permute-start(bf16[32,64]{1,0:T(8,128)(2,1)S(1)} %get-tuple-element.41), channel_id=1, source_target_pairs={{0,1},{1,2},{2,3},{3,4},{4,5},{5,6},{6,7},{7,8},{8,9},{9,10},{10,1... | collective-permute-start | bytes 12296 | tf_op jit(solution)/shard_map/ppermute | solution.py:24
  145.5 15.7 %collective-permute-start.1 = (bf16[32,64]{1,0:T(8,128)(2,1)S(1)}, bf16[32,64]{1,0:T(8,128)(2,1)S(1)}, u32[]{:S(2)}, u32[]{:S(2)}) collective-permute-start(bf16[32,64]{1,0:T(8,128)(2,1)S(1)} %get-tuple-element.42), channel_id=1, source_target_pairs={{1,0},{2,1},{3,2},{4,3},{5,4},{6,5},{7,6},{8,7},{9,8},{10,9},{11,1... | collective-permute-start | bytes 12296 | tf_op jit(solution)/shard_map/ppermute | solution.py:26
  154.0 15.2 %all-to-all-start.2 = ((f32[32,1,512]{2,1,0:T(1,128)}), f32[32,1,512]{2,1,0:T(1,128)S(1)}, u32[]{:S(2)}, u32[]{:S(2)}) async-start(f32[32,1,512]{2,1,0:T(1,128)} %mul.397), calls=%async_computation.2 | async-start | bytes 131072 | tf_op jit(solution)/shard_map/all_to_all | solution.py:41
  261.0 33.2 %all-to-all-start.3 = ((bf16[32,32,512]{2,1,0:T(8,128)(2,1)}), bf16[32,32,512]{2,1,0:T(8,128)(2,1)S(1)}, u32[]{:S(2)}, u32[]{:S(2)}) async-start(bf16[32,32,512]{2,1,0:T(8,128)(2,1)} %broadcast_in_dim.30), calls=%async_computation.3 | async-start | bytes 2097152 | tf_op jit(solution)/shard_map/all_to_all | solution.py:41
  278.4 9.8 %collective-permute-start.2 = (bf16[32,64]{1,0:T(8,128)(2,1)S(1)}, bf16[32,64]{1,0:T(8,128)(2,1)S(1)}, u32[]{:S(2)}, u32[]{:S(2)}) collective-permute-start(bf16[32,64]{1,0:T(8,128)(2,1)S(1)} %get-tuple-element.35), channel_id=1, source_target_pairs={{0,1},{1,2},{2,3},{3,4},{4,5},{5,6},{6,7},{7,8},{8,9},{9,10},{10,1... | collective-permute-start | bytes 12296 | tf_op jit(solution)/shard_map/ppermute | solution.py:24
  280.4 9.4 %collective-permute-start.3 = (bf16[32,64]{1,0:T(8,128)(2,1)S(1)}, bf16[32,64]{1,0:T(8,128)(2,1)S(1)}, u32[]{:S(2)}, u32[]{:S(2)}) collective-permute-start(bf16[32,64]{1,0:T(8,128)(2,1)S(1)} %get-tuple-element.36), channel_id=1, source_target_pairs={{1,0},{2,1},{3,2},{4,3},{5,4},{6,5},{7,6},{8,7},{9,8},{10,9},{11,1... | collective-permute-start | bytes 12296 | tf_op jit(solution)/shard_map/ppermute | solution.py:26
  388.0 32.2 %all-to-all-start.4 = ((bf16[32,32,512]{2,1,0:T(8,128)(2,1)}), bf16[32,32,512]{2,1,0:T(8,128)(2,1)S(1)}, u32[]{:S(2)}, u32[]{:S(2)}) async-start(bf16[32,32,512]{2,1,0:T(8,128)(2,1)} %broadcast_in_dim.31), calls=%async_computation.4 | async-start | bytes 2097152 | tf_op jit(solution)/shard_map/all_to_all | solution.py:41
  404.4 10.0 %collective-permute-start.4 = (bf16[32,64]{1,0:T(8,128)(2,1)S(1)}, bf16[32,64]{1,0:T(8,128)(2,1)S(1)}, u32[]{:S(2)}, u32[]{:S(2)}) collective-permute-start(bf16[32,64]{1,0:T(8,128)(2,1)S(1)} %get-tuple-element.29), channel_id=1, source_target_pairs={{0,1},{1,2},{2,3},{3,4},{4,5},{5,6},{6,7},{7,8},{8,9},{9,10},{10,1... | collective-permute-start | bytes 12296 | tf_op jit(solution)/shard_map/ppermute | solution.py:24
  406.3 9.4 %collective-permute-start.5 = (bf16[32,64]{1,0:T(8,128)(2,1)S(1)}, bf16[32,64]{1,0:T(8,128)(2,1)S(1)}, u32[]{:S(2)}, u32[]{:S(2)}) collective-permute-start(bf16[32,64]{1,0:T(8,128)(2,1)S(1)} %get-tuple-element.30), channel_id=1, source_target_pairs={{1,0},{2,1},{3,2},{4,3},{5,4},{6,5},{7,6},{8,7},{9,8},{10,9},{11,1... | collective-permute-start | bytes 12296 | tf_op jit(solution)/shard_map/ppermute | solution.py:26
Sparse Core Ops, SparseCore 0:
  10.5 115.2 all-gather.1

commit v5 on v3

--- a/solution.py
+++ b/solution.py
@@ -3,6 +3,8 @@
 import jax
 import jax.numpy as jnp
 from jax import lax
+from jax.experimental import pallas as pl
+from jax.experimental.pallas import tpu as pltpu
 from jax.sharding import PartitionSpec as P
 
 RADIUS = 64
@@ -43,6 +45,61 @@
     count = lax.axis_size("band")
     spread = jnp.broadcast_to(block[None], (count,) + block.shape)
     return lax.all_to_all(spread, "band", split_axis=0, concat_axis=0, tiled=True)
+
+
+SLOT_BLOCK = 8
+
+
+def affinity_kernel(part_ref, lev_ref, own_ref, *refs):
+    partner_refs = refs[:SLOT_BLOCK]
+    aff_ref, deg_ref = refs[SLOT_BLOCK], refs[SLOT_BLOCK + 1]
+    tile = pl.program_id(0)
+    block = pl.program_id(1)
+    own = own_ref[0]
+    total = jnp.zeros((1, own.shape[0]), jnp.float32)
+    for slot in range(SLOT_BLOCK):
+        rows = partner_refs[slot][0]
+        inner = lax.dot_general(
+            rows, own, (((1,), (1,)), ((), ())), preferred_element_type=jnp.float32
+        )
+        level = lev_ref[tile, block * SLOT_BLOCK + slot].astype(jnp.float32)
+        weight = (
+            jnp.exp(0.5 * (inner / math.sqrt(own.shape[1]))) * (level / 8.0) / 128.0
+        ).astype(jnp.bfloat16)
+        aff_ref[0, slot] = weight
+        total = total + jnp.sum(weight.astype(jnp.float32), axis=0, keepdims=True)
+    deg_ref[0, 0] = total
+
+
+def affinity_blocks(own_rows, group_rows, partners, levels):
+    tiles, width, embed = own_rows.shape
+    slots = partners.shape[1]
+    blocks = slots // SLOT_BLOCK
+
+    def partner_spec(slot):
+        return pl.BlockSpec(
+            (1, width, embed), lambda t, b, part, lev: (part[t, b * SLOT_BLOCK + slot], 0, 0)
+        )
+
+    grid_spec = pltpu.PrefetchScalarGridSpec(
+        num_scalar_prefetch=2,
+        grid=(tiles, blocks),
+        in_specs=[pl.BlockSpec((1, width, embed), lambda t, b, part, lev: (t, 0, 0))]
+        + [partner_spec(slot) for slot in range(SLOT_BLOCK)],
+        out_specs=[
+            pl.BlockSpec((1, SLOT_BLOCK, width, width), lambda t, b, part, lev: (t, b, 0, 0)),
+            pl.BlockSpec((1, 1, 1, width), lambda t, b, part, lev: (t, b, 0, 0)),
+        ],
+    )
+    affinity, degree = pl.pallas_call(
+        affinity_kernel,
+        grid_spec=grid_spec,
+        out_shape=[
+            jax.ShapeDtypeStruct((tiles, slots, width, width), jnp.bfloat16),
+            jax.ShapeDtypeStruct((tiles, blocks, 1, width), jnp.float32),
+        ],
+    )(partners, levels, own_rows, *([group_rows] * SLOT_BLOCK))
+    return affinity, jnp.sum(degree[:, :, 0, :], axis=1).reshape(-1)
 
 
 def on_device(posteriors, seed_mask, frame_perm, lengths, embeddings, partners, levels):
@@ -81,18 +138,10 @@
     labels_band = band_gather(arrived.reshape(channels, frames))
     labels_band, gathered = lax.optimization_barrier((labels_band, gathered))
     embed_width = embeddings.shape[1]
-    partner_rows = gathered.reshape(-1, 128, embed_width)[partners]
     own_rows = embeddings.reshape(tile_count, 128, embed_width)
-    inner_prod = jnp.einsum(
-        "tkje,tie->tkji", partner_rows, own_rows, preferred_element_type=jnp.float32
-    )
-    affinity = (
-        jnp.exp(0.5 * (inner_prod / math.sqrt(embed_width)))
-        * (levels.astype(jnp.float32) / 8.0)[:, :, None, None]
-        / 128.0
-    )
-    affinity = affinity.astype(jnp.bfloat16)
-    far_degree = jnp.sum(affinity.astype(jnp.float32), axis=(1, 2)).reshape(frames)
+    affinity, far_degree = affinity_blocks(
+        own_rows, gathered.reshape(-1, 128, embed_width), partners, levels
+    )
     norm_scale = 1.0 / jnp.sqrt(near_degree + far_degree)
 
     def squares(residual):

time: 343 us -> 343 us (level)
  Pallas kernels: 0 us -> 13.7 us
  local copies, waits for them, and re-layouts: 40.7 us -> 31.3 us
  matrix products: 18.2 us -> 12.3 us
    pallas_call x0 -> x1, Pallas kernels: none -> 13.7 us  [affinity_blocks(): pl.pallas_call(affinity_kernel, grid_spec=grid_spec, out_shape=[jax.Shape...]
    gather x1 -> x0, local copies, waits for them, and re-layouts: 9.99 us -> none  [on_device(): partner_rows = gathered.reshape(-1, 128, embed_width)[partners]]
    dot_general x1 -> x0, matrix products: 7.66 us -> none  [on_device(): jnp.einsum('tkje,tie->tkji', partner_rows, own_rows, preferred_element_ty...]
where the time goes in v5:
time: 343 us; the launch traced here: 340 us
  waiting for transfers between devices  113 us (33%)
  blocking collectives  79.6 us (23%)
  starting transfers between devices  64.3 us (19%)
  local copies, waits for them, and re-layouts  31.3 us (9%)
  between operations  14.3 us (4%)
  Pallas kernels  13.7 us (4%)
  matrix products  12.3 us (4%)
  other arithmetic  12 us (3%)
    all_to_all x6, blocking collectives, total_over_devices(): rows = lax.all_to_all(spread, axis, split_axis=0, concat_axis=0, tiled=True)  79.6 us
    all_gather x1, waiting for transfers between devices, on_device(): gathered = lax.all_gather(embeddings, 'band', axis=0, tiled=True)  52.3 us
    all_to_all x4, waiting for transfers between devices, band_gather(): lax.all_to_all(spread, 'band', split_axis=0, concat_axis=0, tiled=True)  32.8 us
    all_to_all x4, starting transfers between devices, band_gather(): lax.all_to_all(spread, 'band', split_axis=0, concat_axis=0, tiled=True)  24.5 us
    ppermute x3, starting transfers between devices, with_halo(): lax.ppermute(head, axis, [((i + 1) % count, i) for i in range(ends)])  23.8 us
    ppermute x3, waiting for transfers between devices, with_halo(): lax.ppermute(tail, axis, [(i, (i + 1) % count) for i in range(ends)])  19 us
    pallas_call x1, Pallas kernels, affinity_blocks(): pl.pallas_call(affinity_kernel, grid_spec=grid_spec, out_shape=[jax.Shape...  13.7 us
    all_to_all x1, starting transfers between devices, on_device(): lax.all_to_all(ordered, 'band', split_axis=1, concat_axis=1, tiled=True)  10.2 us
  transfers between devices with their start and end apart: 12, of which 10 were waited for; matrix products, arithmetic and copies ran while one was open for 8% of the time, Pallas kernels for 0%

profile of v5, /device:TPU:6, one launch (start us, length us, event | category | flops | bytes accessed | tf_op | source)
XLA Modules:
  0.0 340.2 jit_solution(2803571941454159363)
XLA Ops:
  7.9 0.8 broadcast_multiply_fusion
  9.3 1.3 reduce.15
  11.5 1.3 gather_fusion
  13.0 0.8 reshape.817
  13.7 10.2 %all-to-all-start = ((bf16[32,2,256]{2,1,0:T(2,128)(2,1)}), bf16[32,2,256]{2,1,0:T(2,128)(2,1)S(1)}, u32[]{:S(2)}, u32[]{:S(2)}) async-start(bf16[32,2,256]{2,1,0:T(2,128)(2,1)} %reshape.817), calls=%async_computation | async-start | bytes 65536 | tf_op jit(solution)/shard_map/all_to_all | solution.py:114
  24.0 1.0 reduce-window.9
  25.3 6.7 %all-to-all-done = bf16[32,2,256]{2,1,0:T(2,128)(2,1)S(1)} async-done(((bf16[32,2,256]{2,1,0:T(2,128)(2,1)}), bf16[32,2,256]{2,1,0:T(2,128)(2,1)S(1)}, u32[]{:S(2)}, u32[]{:S(2)}) %all-to-all-start) | async-done | bytes 32800 | tf_op jit(solution)/shard_map/all_to_all | solution.py:114
  32.2 1.2 broadcast_in_dim.40
  33.4 5.8 %all-to-all-start.1 = ((bf16[32,32,512]{2,1,0:T(8,128)(2,1)}), bf16[32,32,512]{2,1,0:T(8,128)(2,1)S(1)}, u32[]{:S(2)}, u32[]{:S(2)}) async-start(bf16[32,32,512]{2,1,0:T(8,128)(2,1)} %broadcast_in_dim.40), calls=%async_computation.1 | async-start | bytes 2097152 | tf_op jit(solution)/shard_map/all_to_all | solution.py:47
  39.6 4.5 %gather_fusion.1 = s32[1024]{0:T(1024)S(1)} fusion(s32[640]{0:T(1024)S(1)} %convert_reduce_fusion, s32[1024]{0:T(1024)S(1)} %broadcast_clamp_fusion), kind=kCustom, calls=%fused_computation.1 | custom fusion | bytes 12288 | tf_op jit(solution)/shard_map/gather | solution.py:130
  44.2 2.3 gather_fusion.2
  46.6 6.8 %gather_fusion.3 = pred[1024]{0:T(1024)(128)(4,1)S(1)} fusion(pred[640]{0:T(1024)(128)(4,1)S(1)} %compare_and_fusion.1, s32[1024]{0:T(1024)S(1)} %broadcast_clamp_fusion), kind=kCustom, calls=%fused_computation.3 | custom fusion | bytes 6144 | tf_op jit(solution)/shard_map/gather | solution.py:131
  54.2 17.4 %all-to-all-done.1 = bf16[32,32,512]{2,1,0:T(8,128)(2,1)S(1)} async-done(((bf16[32,32,512]{2,1,0:T(8,128)(2,1)}), bf16[32,32,512]{2,1,0:T(8,128)(2,1)S(1)}, u32[]{:S(2)}, u32[]{:S(2)}) %all-to-all-start.1) | async-done | bytes 1048608 | tf_op jit(solution)/shard_map/all_to_all | solution.py:47
  71.6 52.3 %all-gather.2.cloned.1.call-done = bf16[16384,256]{1,0:T(8,128)(2,1)} async-done(((bf16[512,256]{1,0:T(8,128)(2,1)}), bf16[16384,256]{1,0:T(8,128)(2,1)}) %all-gather.2.cloned.1.call-update) | async-done | bytes 8388624 | tf_op jit(solution)/shard_map/all_gather | solution.py:137
  123.9 13.7 %shard_map.73 = (bf16[4,32,128,128]{3,2,1,0:T(8,128)(2,1)}, f32[4,4,1,128]{3,2,1,0:T(1,128)}) custom-call(s32[4,32]{1,0:T(4,128)} %part_ref.1, s32[4,32]{1,0:T(4,128)} %lev_ref.1, bf16[4,128,256]{2,1,0:T(8,128)(2,1)} %bitcast.194, bf16[128,128,256]{2,1,0:T(8,128)(2,1)} %bitcast.174, bf16[128,128,256]{2,1,0:T(8,128)(2,1)} %bitcast.175, ...), custom_call_target="tpu_custom_call" | custom-call | tf_op jit(solution)/shard_map/pallas_call | solution.py:94
  137.6 0.7 reduce_sum.150
  138.5 1.9 collective-permute-start
  140.4 7.9 %collective-permute-start.1 = (bf16[32,64]{1,0:T(8,128)(2,1)S(1)}, bf16[32,64]{1,0:T(8,128)(2,1)S(1)}, u32[]{:S(2)}, u32[]{:S(2)}) collective-permute-start(bf16[32,64]{1,0:T(8,128)(2,1)S(1)} %get-tuple-element.46), channel_id=1, source_target_pairs={{1,0},{2,1},{3,2},{4,3},{5,4},{6,5},{7,6},{8,7},{9,8},{10,9},{11,1... | collective-permute-start | bytes 12296 | tf_op jit(solution)/shard_map/ppermute | solution.py:28
  148.9 7.1 %all-to-all-start.2 = ((f32[32,1,512]{2,1,0:T(1,128)}), f32[32,1,512]{2,1,0:T(1,128)S(1)}, u32[]{:S(2)}, u32[]{:S(2)}) async-start(f32[32,1,512]{2,1,0:T(1,128)} %mul.379), calls=%async_computation.2 | async-start | bytes 131072 | tf_op jit(solution)/shard_map/all_to_all | solution.py:47
  156.8 7.3 %all-to-all-done.2 = f32[32,1,512]{2,1,0:T(1,128)S(1)} async-done(((f32[32,1,512]{2,1,0:T(1,128)}), f32[32,1,512]{2,1,0:T(1,128)S(1)}, u32[]{:S(2)}, u32[]{:S(2)}) %all-to-all-start.2) | async-done | bytes 65568 | tf_op jit(solution)/shard_map/all_to_all | solution.py:47
  166.4 0.8 gather_fusion.4
  167.2 2.9 fusion.3
  170.6 12.9 %all_to_all.56 = f32[16,1,128]{2,1,0:T(1,128)S(1)} all-to-all(f32[16,1,128]{2,1,0:T(1,128)S(1)} %reshape.819), channel_id=1, replica_groups=mesh['band'=32,'seq'=16] {'seq'}, dimensions={0} | all-to-all | bytes 16384 | tf_op jit(solution)/shard_map/all_to_all | solution.py:39
  184.9 12.9 %all_to_all.57 = f32[32,1,128]{2,1,0:T(1,128)S(1)} all-to-all(f32[32,1,128]{2,1,0:T(1,128)S(1)} %reshape.821), channel_id=1, replica_groups=mesh['band'=32,'seq'=16] {'band'}, dimensions={0} | all-to-all | bytes 32768 | tf_op jit(solution)/shard_map/all_to_all | solution.py:39
  199.3 1.1 broadcast_in_dim.44
  200.4 5.8 %all-to-all-start.5 = ((bf16[32,32,512]{2,1,0:T(8,128)(2,1)}), bf16[32,32,512]{2,1,0:T(8,128)(2,1)S(1)}, u32[]{:S(2)}, u32[]{:S(2)}) async-start(bf16[32,32,512]{2,1,0:T(8,128)(2,1)} %broadcast_in_dim.44), calls=%async_computation.5 | async-start | bytes 2097152 | tf_op jit(solution)/shard_map/all_to_all | solution.py:47
  206.3 1.9 collective-permute-start.2
  208.2 8.0 %collective-permute-start.3 = (bf16[32,64]{1,0:T(8,128)(2,1)S(1)}, bf16[32,64]{1,0:T(8,128)(2,1)S(1)}, u32[]{:S(2)}, u32[]{:S(2)}) collective-permute-start(bf16[32,64]{1,0:T(8,128)(2,1)S(1)} %get-tuple-element.40), channel_id=1, source_target_pairs={{1,0},{2,1},{3,2},{4,3},{5,4},{6,5},{7,6},{8,7},{9,8},{10,9},{11,1... | collective-permute-start | bytes 12296 | tf_op jit(solution)/shard_map/ppermute | solution.py:28
  216.3 9.4 %collective-permute-done.2 = bf16[32,64]{1,0:T(8,128)(2,1)S(1)} collective-permute-done((bf16[32,64]{1,0:T(8,128)(2,1)S(1)}, bf16[32,64]{1,0:T(8,128)(2,1)S(1)}, u32[]{:S(2)}, u32[]{:S(2)}) %collective-permute-start.2) | collective-permute-done | bytes 4128 | tf_op jit(solution)/shard_map/ppermute | solution.py:26
  226.3 1.4 fusion.15
  227.8 4.0 %all-to-all-done.5 = bf16[32,32,512]{2,1,0:T(8,128)(2,1)S(1)} async-done(((bf16[32,32,512]{2,1,0:T(8,128)(2,1)}), bf16[32,32,512]{2,1,0:T(8,128)(2,1)S(1)}, u32[]{:S(2)}, u32[]{:S(2)}) %all-to-all-start.5) | async-done | bytes 1048608 | tf_op jit(solution)/shard_map/all_to_all | solution.py:47
  233.8 1.0 gather_fusion.5
  234.9 2.9 fusion.2
  238.2 10.6 %all_to_all.58 = f32[16,3,32]{2,1,0:T(4,128)S(1)} all-to-all(f32[16,3,32]{2,1,0:T(4,128)S(1)} %broadcast_in_dim.45), channel_id=1, replica_groups=mesh['band'=32,'seq'=16] {'seq'}, dimensions={0} | all-to-all | bytes 12288 | tf_op jit(solution)/shard_map/all_to_all | solution.py:39
  248.9 16.5 %all_to_all.59 = f32[32,3,32]{2,1,0:T(4,128)S(1)} all-to-all(f32[32,3,32]{2,1,0:T(4,128)S(1)} %broadcast_in_dim.46), channel_id=1, replica_groups=mesh['band'=32,'seq'=16] {'band'}, dimensions={0} | all-to-all | bytes 24576 | tf_op jit(solution)/shard_map/all_to_all | solution.py:39
  266.0 0.7 multiply_convert_fusion.1
  266.7 1.1 broadcast_in_dim.47
  267.8 5.8 %all-to-all-start.8 = ((bf16[32,32,512]{2,1,0:T(8,128)(2,1)}), bf16[32,32,512]{2,1,0:T(8,128)(2,1)S(1)}, u32[]{:S(2)}, u32[]{:S(2)}) async-start(bf16[32,32,512]{2,1,0:T(8,128)(2,1)} %broadcast_in_dim.47), calls=%async_computation.8 | async-start | bytes 2097152 | tf_op jit(solution)/shard_map/all_to_all | solution.py:47
  273.7 1.9 collective-permute-start.4
  275.6 7.9 %collective-permute-start.5 = (bf16[32,64]{1,0:T(8,128)(2,1)S(1)}, bf16[32,64]{1,0:T(8,128)(2,1)S(1)}, u32[]{:S(2)}, u32[]{:S(2)}) collective-permute-start(bf16[32,64]{1,0:T(8,128)(2,1)S(1)} %get-tuple-element.34), channel_id=1, source_target_pairs={{1,0},{2,1},{3,2},{4,3},{5,4},{6,5},{7,6},{8,7},{9,8},{10,9},{11,1... | collective-permute-start | bytes 12296 | tf_op jit(solution)/shard_map/ppermute | solution.py:28
  283.5 9.6 %collective-permute-done.4 = bf16[32,64]{1,0:T(8,128)(2,1)S(1)} collective-permute-done((bf16[32,64]{1,0:T(8,128)(2,1)S(1)}, bf16[32,64]{1,0:T(8,128)(2,1)S(1)}, u32[]{:S(2)}, u32[]{:S(2)}) %collective-permute-start.4) | collective-permute-done | bytes 4128 | tf_op jit(solution)/shard_map/ppermute | solution.py:26
  293.9 1.4 fusion.16
  295.3 4.1 %all-to-all-done.8 = bf16[32,32,512]{2,1,0:T(8,128)(2,1)S(1)} async-done(((bf16[32,32,512]{2,1,0:T(8,128)(2,1)}), bf16[32,32,512]{2,1,0:T(8,128)(2,1)S(1)}, u32[]{:S(2)}, u32[]{:S(2)}) %all-to-all-start.8) | async-done | bytes 1048608 | tf_op jit(solution)/shard_map/all_to_all | solution.py:47
  301.5 1.0 gather_fusion.6
  302.5 2.9 fusion.1
  305.9 10.4 %all_to_all.60 = f32[16,1,32]{2,1,0:T(1,128)S(1)} all-to-all(f32[16,1,32]{2,1,0:T(1,128)S(1)} %broadcast_in_dim.48), channel_id=1, replica_groups=mesh['band'=32,'seq'=16] {'seq'}, dimensions={0} | all-to-all | bytes 4096 | tf_op jit(solution)/shard_map/all_to_all | solution.py:39
  316.3 16.3 %all_to_all.61 = f32[32,1,32]{2,1,0:T(1,128)S(1)} all-to-all(f32[32,1,32]{2,1,0:T(1,128)S(1)} %broadcast_in_dim.49), channel_id=1, replica_groups=mesh['band'=32,'seq'=16] {'band'}, dimensions={0} | all-to-all | bytes 8192 | tf_op jit(solution)/shard_map/all_to_all | solution.py:39
  332.6 0.7 fusion.19
  (168 shorter events, 18.6 us)
Async XLA Ops:
  6.5 117.4 %all-gather.2.cloned.1.call-start = ((), (), s32[]{:S(2)}) async-start(), calls=%async_computation.11 | async-start | bytes 8650752 | tf_op jit(solution)/shard_map/all_gather | solution.py:137
  13.7 18.3 %all-to-all-start = ((bf16[32,2,256]{2,1,0:T(2,128)(2,1)}), bf16[32,2,256]{2,1,0:T(2,128)(2,1)S(1)}, u32[]{:S(2)}, u32[]{:S(2)}) async-start(bf16[32,2,256]{2,1,0:T(2,128)(2,1)} %reshape.817), calls=%async_computation | async-start | bytes 65536 | tf_op jit(solution)/shard_map/all_to_all | solution.py:114
  32.2 167.0 %copy-start.5 = (bf16[32,512]{1,0:T(8,128)(2,1)}, bf16[32,512]{1,0:T(8,128)(2,1)S(1)}, u32[]{:S(2)}) copy-start(bf16[32,512]{1,0:T(8,128)(2,1)S(1)} %copy.72) | copy-start | bytes 98308
  33.4 38.2 %all-to-all-start.1 = ((bf16[32,32,512]{2,1,0:T(8,128)(2,1)}), bf16[32,32,512]{2,1,0:T(8,128)(2,1)S(1)}, u32[]{:S(2)}, u32[]{:S(2)}) async-start(bf16[32,32,512]{2,1,0:T(8,128)(2,1)} %broadcast_in_dim.40), calls=%async_computation.1 | async-start | bytes 2097152 | tf_op jit(solution)/shard_map/all_to_all | solution.py:47
  39.2 14.2 %copy-start.23 = (s32[4,32]{1,0:T(4,128)S(1)}, s32[4,32]{1,0:T(4,128)}, u32[]{:S(2)}) copy-start(s32[4,32]{1,0:T(4,128)} %part_ref.1) | copy-start | bytes 1540
  44.1 182.1 %copy-start.28 = (s32[4,256]{1,0:T(4,128)}, s32[4,256]{1,0:T(4,128)S(1)}, u32[]{:S(2)}) copy-start(s32[4,256]{1,0:T(4,128)S(1)} %eq.17) | copy-start | bytes 12292
  46.5 179.7 %copy-start.33 = (s32[512]{0:T(512)}, s32[512]{0:T(512)S(1)}, u32[]{:S(2)}) copy-start(s32[512]{0:T(512)S(1)} %gather_fusion.2) | copy-start | bytes 6148
  53.4 172.9 %copy-start.35 = (pred[4,256]{1,0:T(4,128)(4,1)}, pred[4,256]{1,0:T(4,128)(4,1)S(1)}, u32[]{:S(2)}) copy-start(pred[4,256]{1,0:T(4,128)(4,1)S(1)} %and.33) | copy-start | bytes 3076
  53.5 112.9 %copy-start.14 = (s32[1024]{0:T(1024)}, s32[1024]{0:T(1024)S(1)}, u32[]{:S(2)}) copy-start(s32[1024]{0:T(1024)S(1)} %pad_clamp_fusion) | copy-start | bytes 12292
  53.6 172.7 %copy-start.31 = (s32[4,128]{1,0:T(4,128)}, s32[4,128]{1,0:T(4,128)S(1)}, u32[]{:S(2)}) copy-start(s32[4,128]{1,0:T(4,128)S(1)} %iota_add_fusion.2) | copy-start | bytes 6148
  53.7 172.7 %copy-start.26 = (s32[4,256]{1,0:T(4,128)}, s32[4,256]{1,0:T(4,128)S(1)}, u32[]{:S(2)}) copy-start(s32[4,256]{1,0:T(4,128)S(1)} %iota_add_fusion.1) | copy-start | bytes 12292
  138.4 60.9 %copy-start.9 = (f32[512]{0:T(512)}, f32[512]{0:T(512)S(1)}, u32[]{:S(2)}) copy-start(f32[512]{0:T(512)S(1)} %get-tuple-element.25) | copy-start | bytes 6148
  138.4 60.9 %copy-start.11 = (f32[512]{0:T(512)}, f32[512]{0:T(512)S(1)}, u32[]{:S(2)}) copy-start(f32[512]{0:T(512)S(1)} %get-tuple-element.24) | copy-start | bytes 6148
  138.5 17.7 %collective-permute-start = (bf16[32,64]{1,0:T(8,128)(2,1)S(1)}, bf16[32,64]{1,0:T(8,128)(2,1)S(1)}, u32[]{:S(2)}, u32[]{:S(2)}) collective-permute-start(bf16[32,64]{1,0:T(8,128)(2,1)S(1)} %get-tuple-element.45), channel_id=1, source_target_pairs={{0,1},{1,2},{2,3},{3,4},{4,5},{5,6},{6,7},{7,8},{8,9},{9,10},{10,1... | collective-permute-start | bytes 12296 | tf_op jit(solution)/shard_map/ppermute | solution.py:26
  140.4 15.7 %collective-permute-start.1 = (bf16[32,64]{1,0:T(8,128)(2,1)S(1)}, bf16[32,64]{1,0:T(8,128)(2,1)S(1)}, u32[]{:S(2)}, u32[]{:S(2)}) collective-permute-start(bf16[32,64]{1,0:T(8,128)(2,1)S(1)} %get-tuple-element.46), channel_id=1, source_target_pairs={{1,0},{2,1},{3,2},{4,3},{5,4},{6,5},{7,6},{8,7},{9,8},{10,9},{11,1... | collective-permute-start | bytes 12296 | tf_op jit(solution)/shard_map/ppermute | solution.py:28
  148.9 15.2 %all-to-all-start.2 = ((f32[32,1,512]{2,1,0:T(1,128)}), f32[32,1,512]{2,1,0:T(1,128)S(1)}, u32[]{:S(2)}, u32[]{:S(2)}) async-start(f32[32,1,512]{2,1,0:T(1,128)} %mul.379), calls=%async_computation.2 | async-start | bytes 131072 | tf_op jit(solution)/shard_map/all_to_all | solution.py:47
  170.1 30.3 %copy-start.2 = (f32[4,128,32]{1,2,0:T(8,128)}, f32[4,128,32]{1,2,0:T(8,128)S(1)}, u32[]{:S(2)}) copy-start(f32[4,128,32]{1,2,0:T(8,128)S(1)} %fusion.3) | copy-start | bytes 196612
  199.2 32.5 %copy-start.15 = (f32[32]{0:T(128)}, f32[32]{0:T(128)S(1)}, u32[]{:S(2)}) copy-start(f32[32]{0:T(128)S(1)} %get-tuple-element.26) | copy-start | bytes 388
  199.2 32.5 %copy-start.18 = (f32[32]{0:T(128)}, f32[32]{0:T(128)S(1)}, u32[]{:S(2)}) copy-start(f32[32]{0:T(128)S(1)} %get-tuple-element.28) | copy-start | bytes 388
  200.4 31.3 %all-to-all-start.5 = ((bf16[32,32,512]{2,1,0:T(8,128)(2,1)}), bf16[32,32,512]{2,1,0:T(8,128)(2,1)S(1)}, u32[]{:S(2)}, u32[]{:S(2)}) async-start(bf16[32,32,512]{2,1,0:T(8,128)(2,1)} %broadcast_in_dim.44), calls=%async_computation.5 | async-start | bytes 2097152 | tf_op jit(solution)/shard_map/all_to_all | solution.py:47
  206.3 19.4 %collective-permute-start.2 = (bf16[32,64]{1,0:T(8,128)(2,1)S(1)}, bf16[32,64]{1,0:T(8,128)(2,1)S(1)}, u32[]{:S(2)}, u32[]{:S(2)}) collective-permute-start(bf16[32,64]{1,0:T(8,128)(2,1)S(1)} %get-tuple-element.39), channel_id=1, source_target_pairs={{0,1},{1,2},{2,3},{3,4},{4,5},{5,6},{6,7},{7,8},{8,9},{9,10},{10,1... | collective-permute-start | bytes 12296 | tf_op jit(solution)/shard_map/ppermute | solution.py:26
  208.2 17.9 %collective-permute-start.3 = (bf16[32,64]{1,0:T(8,128)(2,1)S(1)}, bf16[32,64]{1,0:T(8,128)(2,1)S(1)}, u32[]{:S(2)}, u32[]{:S(2)}) collective-permute-start(bf16[32,64]{1,0:T(8,128)(2,1)S(1)} %get-tuple-element.40), channel_id=1, source_target_pairs={{1,0},{2,1},{3,2},{4,3},{5,4},{6,5},{7,6},{8,7},{9,8},{10,9},{11,1... | collective-permute-start | bytes 12296 | tf_op jit(solution)/shard_map/ppermute | solution.py:28
  233.7 4.2 %copy-start.16 = (f32[32]{0:T(128)S(1)}, f32[32]{0:T(128)}, u32[]{:S(2)}) copy-start(f32[32]{0:T(128)} %copy-done.15) | copy-start | bytes 388
  233.7 4.2 %copy-start.19 = (f32[32]{0:T(128)S(1)}, f32[32]{0:T(128)}, u32[]{:S(2)}) copy-start(f32[32]{0:T(128)} %copy-done.18) | copy-start | bytes 388
  233.7 31.7 %copy-start.30 = (f32[32]{0:T(128)S(1)}, f32[32]{0:T(128)}, u32[]{:S(2)}) copy-start(f32[32]{0:T(128)} %get-tuple-element.27) | copy-start | bytes 388
  233.8 32.2 %copy-start.3 = (f32[4,128,32]{1,2,0:T(8,128)S(1)}, f32[4,128,32]{1,2,0:T(8,128)}, u32[]{:S(2)}) copy-start(f32[4,128,32]{1,2,0:T(8,128)} %copy-done.2) | copy-start | bytes 196612
  233.8 32.2 %copy-start.6 = (bf16[32,512]{1,0:T(8,128)(2,1)S(1)}, bf16[32,512]{1,0:T(8,128)(2,1)}, u32[]{:S(2)}) copy-start(bf16[32,512]{1,0:T(8,128)(2,1)} %copy-done.5) | copy-start | bytes 98308
  233.8 32.2 %copy-start.10 = (f32[512]{0:T(512)S(1)}, f32[512]{0:T(512)}, u32[]{:S(2)}) copy-start(f32[512]{0:T(512)} %copy-done.9) | copy-start | bytes 6148
  233.8 32.2 %copy-start.12 = (f32[512]{0:T(512)S(1)}, f32[512]{0:T(512)}, u32[]{:S(2)}) copy-start(f32[512]{0:T(512)} %copy-done.11) | copy-start | bytes 6148
  234.8 59.0 %copy-start.27 = (s32[4,256]{1,0:T(4,128)S(1)}, s32[4,256]{1,0:T(4,128)}, u32[]{:S(2)}) copy-start(s32[4,256]{1,0:T(4,128)} %copy-done.26) | copy-start | bytes 12292
  234.8 59.0 %copy-start.29 = (s32[4,256]{1,0:T(4,128)S(1)}, s32[4,256]{1,0:T(4,128)}, u32[]{:S(2)}) copy-start(s32[4,256]{1,0:T(4,128)} %copy-done.28) | copy-start | bytes 12292
  234.8 59.0 %copy-start.32 = (s32[4,128]{1,0:T(4,128)S(1)}, s32[4,128]{1,0:T(4,128)}, u32[]{:S(2)}) copy-start(s32[4,128]{1,0:T(4,128)} %copy-done.31) | copy-start | bytes 6148
  234.8 59.0 %copy-start.34 = (s32[512]{0:T(512)S(1)}, s32[512]{0:T(512)}, u32[]{:S(2)}) copy-start(s32[512]{0:T(512)} %copy-done.33) | copy-start | bytes 6148
  234.8 59.0 %copy-start.36 = (pred[4,256]{1,0:T(4,128)(4,1)S(1)}, pred[4,256]{1,0:T(4,128)(4,1)}, u32[]{:S(2)}) copy-start(pred[4,256]{1,0:T(4,128)(4,1)} %copy-done.35) | copy-start | bytes 3076
  238.0 29.9 %copy-start = (f32[32,4,128]{0,2,1:T(8,128)}, f32[32,4,128]{0,2,1:T(8,128)S(1)}, u32[]{:S(2)}) copy-start(f32[32,4,128]{0,2,1:T(8,128)S(1)} %copy.82) | copy-start | bytes 196612
  266.0 27.2 %copy-start.21 = (f32[32]{0:T(128)}, f32[32]{0:T(128)S(1)}, u32[]{:S(2)}) copy-start(f32[32]{0:T(128)S(1)} %get-tuple-element.23) | copy-start | bytes 388
  267.8 31.6 %all-to-all-start.8 = ((bf16[32,32,512]{2,1,0:T(8,128)(2,1)}), bf16[32,32,512]{2,1,0:T(8,128)(2,1)S(1)}, u32[]{:S(2)}, u32[]{:S(2)}) async-start(bf16[32,32,512]{2,1,0:T(8,128)(2,1)} %broadcast_in_dim.47), calls=%async_computation.8 | async-start | bytes 2097152 | tf_op jit(solution)/shard_map/all_to_all | solution.py:47
  273.7 19.4 %collective-permute-start.4 = (bf16[32,64]{1,0:T(8,128)(2,1)S(1)}, bf16[32,64]{1,0:T(8,128)(2,1)S(1)}, u32[]{:S(2)}, u32[]{:S(2)}) collective-permute-start(bf16[32,64]{1,0:T(8,128)(2,1)S(1)} %get-tuple-element.33), channel_id=1, source_target_pairs={{0,1},{1,2},{2,3},{3,4},{4,5},{5,6},{6,7},{7,8},{8,9},{9,10},{10,1... | collective-permute-start | bytes 12296 | tf_op jit(solution)/shard_map/ppermute | solution.py:26
  275.6 18.1 %collective-permute-start.5 = (bf16[32,64]{1,0:T(8,128)(2,1)S(1)}, bf16[32,64]{1,0:T(8,128)(2,1)S(1)}, u32[]{:S(2)}, u32[]{:S(2)}) collective-permute-start(bf16[32,64]{1,0:T(8,128)(2,1)S(1)} %get-tuple-element.34), channel_id=1, source_target_pairs={{1,0},{2,1},{3,2},{4,3},{5,4},{6,5},{7,6},{8,7},{9,8},{10,9},{11,1... | collective-permute-start | bytes 12296 | tf_op jit(solution)/shard_map/ppermute | solution.py:28
  301.4 4.2 %copy-start.1 = (f32[32,4,128]{0,2,1:T(8,128)S(1)}, f32[32,4,128]{0,2,1:T(8,128)}, u32[]{:S(2)}) copy-start(f32[32,4,128]{0,2,1:T(8,128)} %copy-done) | copy-start | bytes 196612
  301.4 4.2 %copy-start.17 = (f32[32]{0:T(128)S(1)}, f32[32]{0:T(128)}, u32[]{:S(2)}) copy-start(f32[32]{0:T(128)} %copy-done.15) | copy-start | bytes 388
  301.4 4.2 %copy-start.20 = (f32[32]{0:T(128)S(1)}, f32[32]{0:T(128)}, u32[]{:S(2)}) copy-start(f32[32]{0:T(128)} %copy-done.18) | copy-start | bytes 388
  301.4 4.2 %copy-start.22 = (f32[32]{0:T(128)S(1)}, f32[32]{0:T(128)}, u32[]{:S(2)}) copy-start(f32[32]{0:T(128)} %copy-done.21) | copy-start | bytes 388
  301.4 31.2 %copy-start.37 = (f32[32]{0:T(128)S(1)}, f32[32]{0:T(128)}, u32[]{:S(2)}) copy-start(f32[32]{0:T(128)} %get-tuple-element.22) | copy-start | bytes 388
  301.4 31.2 %copy-start.4 = (f32[4,128,32]{1,2,0:T(8,128)S(1)}, f32[4,128,32]{1,2,0:T(8,128)}, u32[]{:S(2)}) copy-start(f32[4,128,32]{1,2,0:T(8,128)} %copy-done.2) | copy-start | bytes 196612
  301.4 31.2 %copy-start.7 = (bf16[32,512]{1,0:T(8,128)(2,1)S(1)}, bf16[32,512]{1,0:T(8,128)(2,1)}, u32[]{:S(2)}) copy-start(bf16[32,512]{1,0:T(8,128)(2,1)} %copy-done.5) | copy-start | bytes 98308
  301.4 31.2 %copy-start.8 = (f32[32,512]{1,0:T(8,128)S(1)}, f32[32,512]{1,0:T(8,128)}, u32[]{:S(2)}) copy-start(f32[32,512]{1,0:T(8,128)} %get-tuple-element.20) | copy-start | bytes 196612
  301.4 31.2 %copy-start.13 = (f32[512]{0:T(512)S(1)}, f32[512]{0:T(512)}, u32[]{:S(2)}) copy-start(f32[512]{0:T(512)} %copy-done.11) | copy-start | bytes 6148
  (2 other events, 6.1 us)
Sparse Core Ops, SparseCore 0:
  10.5 113.3 all-gather.1

commit v6 on v3

--- a/solution.py
+++ b/solution.py
@@ -54,8 +54,10 @@
     ordered = jnp.take(seeded, frame_perm[0], axis=1).reshape(
         channels, band_count, frames // band_count
     )
-    arrived = lax.all_to_all(ordered, "band", split_axis=1, concat_axis=1, tiled=True)
-    labels = arrived.reshape(channels, frames).astype(jnp.float32)
+    from_bands = band_gather(ordered)
+    labels_band = jnp.transpose(from_bands, (2, 1, 0, 3)).reshape(band_count, channels, frames)
+    arrived = lax.dynamic_index_in_dim(labels_band, lax.axis_index("band"), axis=0, keepdims=False)
+    labels = arrived.astype(jnp.float32)
     device = lax.axis_index("band") * groups + lax.axis_index("seq")
     frame_total = frames * band_count * groups
     window = 128 + 2 * RADIUS
@@ -78,7 +80,6 @@
     ).astype(jnp.bfloat16)
     near_degree = jnp.sum(band_tiles.astype(jnp.float32), axis=1).reshape(frames)
     gathered = lax.all_gather(embeddings, "band", axis=0, tiled=True)
-    labels_band = band_gather(arrived.reshape(channels, frames))
     labels_band, gathered = lax.optimization_barrier((labels_band, gathered))
     embed_width = embeddings.shape[1]
     partner_rows = gathered.reshape(-1, 128, embed_width)[partners]

time: 343 us -> 354 us (1.032)
  blocking collectives: 77.6 us -> 48.8 us
  local copies, waits for them, and re-layouts: 40.7 us -> 61.2 us
  starting transfers between devices: 64.3 us -> 72.1 us
  waiting for transfers between devices: 116 us -> 123 us
  other arithmetic: 9.58 us -> 14.5 us
    all_to_all x6 -> x4, blocking collectives: 77.6 us -> 48.8 us  [total_over_devices(): rows = lax.all_to_all(spread, axis, split_axis=0, concat_axis=0, tiled=True)]
    unnamed x15 -> x21, local copies, waits for them, and re-layouts: 1.8 us -> 17.5 us
    all_to_all x1 -> x2, waiting for transfers between devices: 6.65 us -> 15.7 us  [total_over_devices(): rows = lax.all_to_all(spread, axis, split_axis=0, concat_axis=0, tiled=True)]
    convert_element_type x0 -> x1, other arithmetic: none -> 5.8 us  [on_device(): (scale_band[:, None, :] * labels_band.astype(jnp.float32)).astype(jnp.bfl...]
    all_to_all x4, starting transfers between devices: 24.5 us -> 29 us  [band_gather(): lax.all_to_all(spread, 'band', split_axis=0, concat_axis=0, tiled=True)]
    transpose x0 -> x2, local copies, waits for them, and re-layouts: none -> 4.08 us  [on_device(): jnp.transpose(from_bands, (2, 1, 0, 3))]
    all_to_all x1 -> x2, starting transfers between devices: 10.2 us -> 13.6 us  [total_over_devices(): rows = lax.all_to_all(spread, axis, split_axis=0, concat_axis=0, tiled=True)]
  transfers between devices with their start and end apart: 12 -> 13, of which waited for: 10 -> 11; matrix products, arithmetic and copies ran while one was open for 8% -> 12% of each run, Pallas kernels for 0% -> 0%
where the time goes in v6:
time: 354 us; the launch traced here: 352 us
  waiting for transfers between devices  123 us (35%)
  starting transfers between devices  72.1 us (20%)
  local copies, waits for them, and re-layouts  61.2 us (17%)
  blocking collectives  48.8 us (14%)
  matrix products  18.2 us (5%)
  other arithmetic  14.5 us (4%)
  between operations  13.9 us (4%)
    all_gather x1, waiting for transfers between devices, on_device(): gathered = lax.all_gather(embeddings, 'band', axis=0, tiled=True)  51.3 us
    all_to_all x4, blocking collectives, total_over_devices(): rows = lax.all_to_all(spread, axis, split_axis=0, concat_axis=0, tiled=True)  48.8 us
    all_to_all x4, waiting for transfers between devices, band_gather(): lax.all_to_all(spread, 'band', split_axis=0, concat_axis=0, tiled=True)  35.5 us
    all_to_all x4, starting transfers between devices, band_gather(): lax.all_to_all(spread, 'band', split_axis=0, concat_axis=0, tiled=True)  29 us
    ppermute x3, starting transfers between devices, with_halo(): lax.ppermute(head, axis, [((i + 1) % count, i) for i in range(ends)])  23.8 us
    ppermute x3, waiting for transfers between devices, with_halo(): lax.ppermute(tail, axis, [(i, (i + 1) % count) for i in range(ends)])  18.9 us
    unnamed x21, local copies, waits for them, and re-layouts  17.5 us
    all_to_all x2, waiting for transfers between devices, total_over_devices(): rows = lax.all_to_all(spread, axis, split_axis=0, concat_axis=0, tiled=True)  15.7 us
  transfers between devices with their start and end apart: 13, of which 11 were waited for; matrix products, arithmetic and copies ran while one was open for 12% of the time, Pallas kernels for 0%

profile of v6, /device:TPU:6, one launch (start us, length us, event | category | flops | bytes accessed | tf_op | source)
XLA Modules:
  0.0 351.9 jit_solution(5399426587774320832)
XLA Ops:
  7.9 0.8 broadcast_multiply_fusion
  9.3 1.3 reduce.7
  11.5 1.3 gather_fusion
  13.0 2.9 broadcast_bitcast_fusion
  15.9 7.5 %reshape.659 = bf16[32,2,8192]{2,1,0:T(2,128)(2,1)} reshape(bf16[32,32,16,32]{3,2,1,0:T(8,128)(2,1)} %broadcast_bitcast_fusion) | data formatting | bytes 2097152
  23.4 10.2 %all-to-all-start = ((bf16[32,2,8192]{2,1,0:T(2,128)(2,1)}), bf16[32,2,8192]{2,1,0:T(2,128)(2,1)S(1)}, u32[]{:S(2)}, u32[]{:S(2)}) async-start(bf16[32,2,8192]{2,1,0:T(2,128)(2,1)} %reshape.659), calls=%async_computation | async-start | bytes 2097152 | tf_op jit(solution)/shard_map/all_to_all | solution.py:45
  34.6 4.5 %gather_fusion.1 = s32[1024]{0:T(1024)S(1)} fusion(s32[640]{0:T(1024)S(1)} %convert_reduce_fusion.1, s32[1024]{0:T(1024)S(1)} %broadcast_clamp_fusion), kind=kCustom, calls=%fused_computation.1 | custom fusion | bytes 12288 | tf_op jit(solution)/shard_map/gather | solution.py:75
  39.3 2.3 gather_fusion.2
  41.6 6.8 %gather_fusion.3 = pred[1024]{0:T(1024)(128)(4,1)S(1)} fusion(pred[640]{0:T(1024)(128)(4,1)S(1)} %compare_and_fusion.1, s32[1024]{0:T(1024)S(1)} %broadcast_clamp_fusion), kind=kCustom, calls=%fused_computation.3 | custom fusion | bytes 6144 | tf_op jit(solution)/shard_map/gather | solution.py:76
  49.3 18.0 %all-to-all-done = bf16[32,2,8192]{2,1,0:T(2,128)(2,1)S(1)} async-done(((bf16[32,2,8192]{2,1,0:T(2,128)(2,1)}), bf16[32,2,8192]{2,1,0:T(2,128)(2,1)S(1)}, u32[]{:S(2)}, u32[]{:S(2)}) %all-to-all-start) | async-done | bytes 1048608 | tf_op jit(solution)/shard_map/all_to_all | solution.py:45
  67.3 3.6 %reshape.660 = bf16[32,32,16,32]{3,2,1,0:T(8,128)(2,1)} reshape(bf16[32,2,8192]{2,1,0:T(2,128)(2,1)S(1)} %all-to-all-done) | data formatting | bytes 2097152
  70.9 2.9 bitcast_bitcast_fusion
  73.8 1.2 copy.75
  75.0 1.9 copy-done
  77.0 51.3 %all-gather.2.cloned.1.call-done = bf16[16384,256]{1,0:T(8,128)(2,1)} async-done(((bf16[512,256]{1,0:T(8,128)(2,1)}), bf16[16384,256]{1,0:T(8,128)(2,1)}) %all-gather.2.cloned.1.call-update) | async-done | bytes 8388624 | tf_op jit(solution)/shard_map/all_gather | solution.py:82
  128.2 10.0 %gather_fusion.4 = bf16[128,128,256]{2,1,0:T(8,128)(2,1)} fusion(bf16[128,128,256]{2,1,0:T(8,128)(2,1)} %bitcast.272, s32[1024]{0:T(1024)S(1)} %pad_clamp_fusion), kind=kCustom, calls=%fused_computation.4 | custom fusion | bytes 16777728 | tf_op jit(solution)/shard_map/gather | solution.py:85
  138.2 7.7 %convert_reduce_fusion = (f32[4,128]{1,0:T(4,128)S(1)}, bf16[4,32,128,128]{3,2,1,0:T(8,128)(2,1)}) fusion(f32[4,32]{1,0:T(4,128)S(1)} %convert_multiply_fusion.1, bf16[4,32,128,256]{3,2,1,0:T(8,128)(2,1)} %bitcast.273, bf16[4,128,256,1]{2,1,3,0:T(8,128)(2,1)S(1)} %bitcast.282), kind=kOutput, calls=%fused_computation.9 | convolution fusion | flops 1086324224 | bytes 12847616 | tf_op jit(solution)/shard_map/tkje,tie->tkji/dot_general | solution.py:87
  146.0 1.9 collective-permute-start
  147.9 7.9 %collective-permute-start.1 = (bf16[32,64]{1,0:T(8,128)(2,1)S(1)}, bf16[32,64]{1,0:T(8,128)(2,1)S(1)}, u32[]{:S(2)}, u32[]{:S(2)}) collective-permute-start(bf16[32,64]{1,0:T(8,128)(2,1)S(1)} %get-tuple-element.42), channel_id=1, source_target_pairs={{1,0},{2,1},{3,2},{4,3},{5,4},{6,5},{7,6},{8,7},{9,8},{10,9},{11,1... | collective-permute-start | bytes 12296 | tf_op jit(solution)/shard_map/ppermute | solution.py:26
  156.4 7.1 %all-to-all-start.1 = ((f32[32,1,512]{2,1,0:T(1,128)}), f32[32,1,512]{2,1,0:T(1,128)S(1)}, u32[]{:S(2)}, u32[]{:S(2)}) async-start(f32[32,1,512]{2,1,0:T(1,128)} %mul.350), calls=%async_computation.1 | async-start | bytes 131072 | tf_op jit(solution)/shard_map/all_to_all | solution.py:45
  164.3 7.4 %all-to-all-done.1 = f32[32,1,512]{2,1,0:T(1,128)S(1)} async-done(((f32[32,1,512]{2,1,0:T(1,128)}), f32[32,1,512]{2,1,0:T(1,128)S(1)}, u32[]{:S(2)}, u32[]{:S(2)}) %all-to-all-start.1) | async-done | bytes 65568 | tf_op jit(solution)/shard_map/all_to_all | solution.py:45
  171.7 5.8 %multiply_convert_fusion = bf16[32,32,512]{1,2,0:T(8,128)(2,1)} fusion(bf16[32,32,512]{1,2,0:T(8,128)(2,1)} %bitcast.270, f32[32,512]{1,0:T(8,128)S(1)} %bitcast.281), kind=kLoop, calls=%fused_computation.8 | loop fusion | flops 1572864 | bytes 2162688 | tf_op jit(solution)/shard_map/convert_element_type | solution.py:118
  177.5 3.6 %copy.78 = bf16[32,128,128]{2,0,1:T(8,128)(2,1)S(1)} copy(bf16[32,128,128]{0,2,1:T(8,128)(2,1)} %bitcast.271) | data formatting | bytes 2097152 | tf_op jit(solution)/shard_map/reshape | solution.py:121
  181.0 0.8 gather_fusion.5
  181.8 2.9 fusion.3
  185.0 12.8 %all_to_all.51 = f32[16,1,128]{2,1,0:T(1,128)S(1)} all-to-all(f32[16,1,128]{2,1,0:T(1,128)S(1)} %reshape.661), channel_id=1, replica_groups=mesh['band'=32,'seq'=16] {'seq'}, dimensions={0} | all-to-all | bytes 16384 | tf_op jit(solution)/shard_map/all_to_all | solution.py:37
  199.8 5.7 %all-to-all-start.3 = ((f32[32,1,128]{2,1,0:T(1,128)}), f32[32,1,128]{2,1,0:T(1,128)S(1)}, u32[]{:S(2)}, u32[]{:S(2)}) async-start(f32[32,1,128]{2,1,0:T(1,128)} %reshape.663), calls=%async_computation.3 | async-start | bytes 32768 | tf_op jit(solution)/shard_map/all_to_all | solution.py:37
  205.6 7.7 %all-to-all-done.3 = f32[32,1,128]{2,1,0:T(1,128)S(1)} async-done(((f32[32,1,128]{2,1,0:T(1,128)}), f32[32,1,128]{2,1,0:T(1,128)S(1)}, u32[]{:S(2)}, u32[]{:S(2)}) %all-to-all-start.3) | async-done | bytes 16416 | tf_op jit(solution)/shard_map/all_to_all | solution.py:37
  214.2 1.1 broadcast_in_dim.46
  215.3 5.9 %all-to-all-start.4 = ((bf16[32,32,512]{2,1,0:T(8,128)(2,1)}), bf16[32,32,512]{2,1,0:T(8,128)(2,1)S(1)}, u32[]{:S(2)}, u32[]{:S(2)}) async-start(bf16[32,32,512]{2,1,0:T(8,128)(2,1)} %broadcast_in_dim.46), calls=%async_computation.4 | async-start | bytes 2097152 | tf_op jit(solution)/shard_map/all_to_all | solution.py:45
  221.3 1.9 collective-permute-start.2
  223.2 7.9 %collective-permute-start.3 = (bf16[32,64]{1,0:T(8,128)(2,1)S(1)}, bf16[32,64]{1,0:T(8,128)(2,1)S(1)}, u32[]{:S(2)}, u32[]{:S(2)}) collective-permute-start(bf16[32,64]{1,0:T(8,128)(2,1)S(1)} %get-tuple-element.36), channel_id=1, source_target_pairs={{1,0},{2,1},{3,2},{4,3},{5,4},{6,5},{7,6},{8,7},{9,8},{10,9},{11,1... | collective-permute-start | bytes 12296 | tf_op jit(solution)/shard_map/ppermute | solution.py:26
  231.1 9.6 %collective-permute-done.2 = bf16[32,64]{1,0:T(8,128)(2,1)S(1)} collective-permute-done((bf16[32,64]{1,0:T(8,128)(2,1)S(1)}, bf16[32,64]{1,0:T(8,128)(2,1)S(1)}, u32[]{:S(2)}, u32[]{:S(2)}) %collective-permute-start.2) | collective-permute-done | bytes 4128 | tf_op jit(solution)/shard_map/ppermute | solution.py:24
  241.9 5.0 %all-to-all-done.4 = bf16[32,32,512]{2,1,0:T(8,128)(2,1)S(1)} async-done(((bf16[32,32,512]{2,1,0:T(8,128)(2,1)}), bf16[32,32,512]{2,1,0:T(8,128)(2,1)S(1)}, u32[]{:S(2)}, u32[]{:S(2)}) %all-to-all-start.4) | async-done | bytes 1048608 | tf_op jit(solution)/shard_map/all_to_all | solution.py:45
  248.9 0.8 gather_fusion.6
  249.7 2.9 fusion.2
  252.9 10.3 %all_to_all.52 = f32[16,3,32]{2,1,0:T(4,128)S(1)} all-to-all(f32[16,3,32]{2,1,0:T(4,128)S(1)} %broadcast_in_dim.47), channel_id=1, replica_groups=mesh['band'=32,'seq'=16] {'seq'}, dimensions={0} | all-to-all | bytes 12288 | tf_op jit(solution)/shard_map/all_to_all | solution.py:37
  263.8 7.9 %all-to-all-start.6 = ((f32[32,3,32]{2,1,0:T(4,128)}), f32[32,3,32]{2,1,0:T(4,128)S(1)}, u32[]{:S(2)}, u32[]{:S(2)}) async-start(f32[32,3,32]{2,1,0:T(4,128)} %broadcast_in_dim.48), calls=%async_computation.6 | async-start | bytes 131072 | tf_op jit(solution)/shard_map/all_to_all | solution.py:37
  271.8 8.0 %all-to-all-done.6 = f32[32,3,32]{2,1,0:T(4,128)S(1)} async-done(((f32[32,3,32]{2,1,0:T(4,128)}), f32[32,3,32]{2,1,0:T(4,128)S(1)}, u32[]{:S(2)}, u32[]{:S(2)}) %all-to-all-start.6) | async-done | bytes 12320 | tf_op jit(solution)/shard_map/all_to_all | solution.py:37
  280.0 1.1 broadcast_in_dim.50
  281.1 5.8 %all-to-all-start.7 = ((bf16[32,32,512]{2,1,0:T(8,128)(2,1)}), bf16[32,32,512]{2,1,0:T(8,128)(2,1)S(1)}, u32[]{:S(2)}, u32[]{:S(2)}) async-start(bf16[32,32,512]{2,1,0:T(8,128)(2,1)} %broadcast_in_dim.50), calls=%async_computation.7 | async-start | bytes 2097152 | tf_op jit(solution)/shard_map/all_to_all | solution.py:45
  287.1 1.9 collective-permute-start.4
  289.0 8.1 %collective-permute-start.5 = (bf16[32,64]{1,0:T(8,128)(2,1)S(1)}, bf16[32,64]{1,0:T(8,128)(2,1)S(1)}, u32[]{:S(2)}, u32[]{:S(2)}) collective-permute-start(bf16[32,64]{1,0:T(8,128)(2,1)S(1)} %get-tuple-element.30), channel_id=1, source_target_pairs={{1,0},{2,1},{3,2},{4,3},{5,4},{6,5},{7,6},{8,7},{9,8},{10,9},{11,1... | collective-permute-start | bytes 12296 | tf_op jit(solution)/shard_map/ppermute | solution.py:26
  297.1 9.3 %collective-permute-done.4 = bf16[32,64]{1,0:T(8,128)(2,1)S(1)} collective-permute-done((bf16[32,64]{1,0:T(8,128)(2,1)S(1)}, bf16[32,64]{1,0:T(8,128)(2,1)S(1)}, u32[]{:S(2)}, u32[]{:S(2)}) %collective-permute-start.4) | collective-permute-done | bytes 4128 | tf_op jit(solution)/shard_map/ppermute | solution.py:24
  307.7 5.0 %all-to-all-done.7 = bf16[32,32,512]{2,1,0:T(8,128)(2,1)S(1)} async-done(((bf16[32,32,512]{2,1,0:T(8,128)(2,1)}), bf16[32,32,512]{2,1,0:T(8,128)(2,1)S(1)}, u32[]{:S(2)}, u32[]{:S(2)}) %all-to-all-start.7) | async-done | bytes 1048608 | tf_op jit(solution)/shard_map/all_to_all | solution.py:45
  315.4 2.9 fusion.1
  318.5 10.1 %all_to_all.53 = f32[16,1,32]{2,1,0:T(1,128)S(1)} all-to-all(f32[16,1,32]{2,1,0:T(1,128)S(1)} %broadcast_in_dim.51), channel_id=1, replica_groups=mesh['band'=32,'seq'=16] {'seq'}, dimensions={0} | all-to-all | bytes 4096 | tf_op jit(solution)/shard_map/all_to_all | solution.py:37
  328.6 15.6 %all_to_all.54 = f32[32,1,32]{2,1,0:T(1,128)S(1)} all-to-all(f32[32,1,32]{2,1,0:T(1,128)S(1)} %broadcast_in_dim.52), channel_id=1, replica_groups=mesh['band'=32,'seq'=16] {'band'}, dimensions={0} | all-to-all | bytes 8192 | tf_op jit(solution)/shard_map/all_to_all | solution.py:37
  (105 shorter events, 19.2 us)
Async XLA Ops:
  6.5 27.1 %copy-start.4 = (s32[256]{0:T(256)S(1)}, s32[256]{0:T(256)}, u32[]{:S(2)}) copy-start(s32[256]{0:T(256)} %param.10) | copy-start | bytes 3076
  6.5 121.7 %all-gather.2.cloned.1.call-start = ((), (), s32[]{:S(2)}) async-start(), calls=%async_computation.10 | async-start | bytes 8650752 | tf_op jit(solution)/shard_map/all_gather | solution.py:82
  15.9 32.5 %copy-start.2 = (s32[4,32]{1,0:T(4,128)S(1)}, s32[4,32]{1,0:T(4,128)}, u32[]{:S(2)}) copy-start(s32[4,32]{1,0:T(4,128)} %param.12) | copy-start | bytes 1540
  15.9 33.3 %copy-start.3 = (s32[4,32]{1,0:T(4,128)S(1)}, s32[4,32]{1,0:T(4,128)}, u32[]{:S(2)}) copy-start(s32[4,32]{1,0:T(4,128)} %param.13) | copy-start | bytes 1540
  23.4 43.9 %all-to-all-start = ((bf16[32,2,8192]{2,1,0:T(2,128)(2,1)}), bf16[32,2,8192]{2,1,0:T(2,128)(2,1)S(1)}, u32[]{:S(2)}, u32[]{:S(2)}) async-start(bf16[32,2,8192]{2,1,0:T(2,128)(2,1)} %reshape.659), calls=%async_computation | async-start | bytes 2097152 | tf_op jit(solution)/shard_map/all_to_all | solution.py:45
  75.0 1.9 copy-start
  128.2 10.0 %copy-start.1 = (bf16[512,256]{1,0:T(8,128)(2,1)S(1)}, bf16[512,256]{1,0:T(8,128)(2,1)}, u32[]{:S(2)}) copy-start(bf16[512,256]{1,0:T(8,128)(2,1)} %param.11) | copy-start | bytes 786436
  146.0 17.6 %collective-permute-start = (bf16[32,64]{1,0:T(8,128)(2,1)S(1)}, bf16[32,64]{1,0:T(8,128)(2,1)S(1)}, u32[]{:S(2)}, u32[]{:S(2)}) collective-permute-start(bf16[32,64]{1,0:T(8,128)(2,1)S(1)} %get-tuple-element.41), channel_id=1, source_target_pairs={{0,1},{1,2},{2,3},{3,4},{4,5},{5,6},{6,7},{7,8},{8,9},{9,10},{10,1... | collective-permute-start | bytes 12296 | tf_op jit(solution)/shard_map/ppermute | solution.py:24
  147.9 15.6 %collective-permute-start.1 = (bf16[32,64]{1,0:T(8,128)(2,1)S(1)}, bf16[32,64]{1,0:T(8,128)(2,1)S(1)}, u32[]{:S(2)}, u32[]{:S(2)}) collective-permute-start(bf16[32,64]{1,0:T(8,128)(2,1)S(1)} %get-tuple-element.42), channel_id=1, source_target_pairs={{1,0},{2,1},{3,2},{4,3},{5,4},{6,5},{7,6},{8,7},{9,8},{10,9},{11,1... | collective-permute-start | bytes 12296 | tf_op jit(solution)/shard_map/ppermute | solution.py:26
  156.4 15.2 %all-to-all-start.1 = ((f32[32,1,512]{2,1,0:T(1,128)}), f32[32,1,512]{2,1,0:T(1,128)S(1)}, u32[]{:S(2)}, u32[]{:S(2)}) async-start(f32[32,1,512]{2,1,0:T(1,128)} %mul.350), calls=%async_computation.1 | async-start | bytes 131072 | tf_op jit(solution)/shard_map/all_to_all | solution.py:45
  199.8 13.5 %all-to-all-start.3 = ((f32[32,1,128]{2,1,0:T(1,128)}), f32[32,1,128]{2,1,0:T(1,128)S(1)}, u32[]{:S(2)}, u32[]{:S(2)}) async-start(f32[32,1,128]{2,1,0:T(1,128)} %reshape.663), calls=%async_computation.3 | async-start | bytes 32768 | tf_op jit(solution)/shard_map/all_to_all | solution.py:37
  215.3 31.7 %all-to-all-start.4 = ((bf16[32,32,512]{2,1,0:T(8,128)(2,1)}), bf16[32,32,512]{2,1,0:T(8,128)(2,1)S(1)}, u32[]{:S(2)}, u32[]{:S(2)}) async-start(bf16[32,32,512]{2,1,0:T(8,128)(2,1)} %broadcast_in_dim.46), calls=%async_computation.4 | async-start | bytes 2097152 | tf_op jit(solution)/shard_map/all_to_all | solution.py:45
  221.3 19.4 %collective-permute-start.2 = (bf16[32,64]{1,0:T(8,128)(2,1)S(1)}, bf16[32,64]{1,0:T(8,128)(2,1)S(1)}, u32[]{:S(2)}, u32[]{:S(2)}) collective-permute-start(bf16[32,64]{1,0:T(8,128)(2,1)S(1)} %get-tuple-element.35), channel_id=1, source_target_pairs={{0,1},{1,2},{2,3},{3,4},{4,5},{5,6},{6,7},{7,8},{8,9},{9,10},{10,1... | collective-permute-start | bytes 12296 | tf_op jit(solution)/shard_map/ppermute | solution.py:24
  223.2 18.0 %collective-permute-start.3 = (bf16[32,64]{1,0:T(8,128)(2,1)S(1)}, bf16[32,64]{1,0:T(8,128)(2,1)S(1)}, u32[]{:S(2)}, u32[]{:S(2)}) collective-permute-start(bf16[32,64]{1,0:T(8,128)(2,1)S(1)} %get-tuple-element.36), channel_id=1, source_target_pairs={{1,0},{2,1},{3,2},{4,3},{5,4},{6,5},{7,6},{8,7},{9,8},{10,9},{11,1... | collective-permute-start | bytes 12296 | tf_op jit(solution)/shard_map/ppermute | solution.py:26
  263.8 16.0 %all-to-all-start.6 = ((f32[32,3,32]{2,1,0:T(4,128)}), f32[32,3,32]{2,1,0:T(4,128)S(1)}, u32[]{:S(2)}, u32[]{:S(2)}) async-start(f32[32,3,32]{2,1,0:T(4,128)} %broadcast_in_dim.48), calls=%async_computation.6 | async-start | bytes 131072 | tf_op jit(solution)/shard_map/all_to_all | solution.py:37
  281.1 31.6 %all-to-all-start.7 = ((bf16[32,32,512]{2,1,0:T(8,128)(2,1)}), bf16[32,32,512]{2,1,0:T(8,128)(2,1)S(1)}, u32[]{:S(2)}, u32[]{:S(2)}) async-start(bf16[32,32,512]{2,1,0:T(8,128)(2,1)} %broadcast_in_dim.50), calls=%async_computation.7 | async-start | bytes 2097152 | tf_op jit(solution)/shard_map/all_to_all | solution.py:45
  287.1 19.3 %collective-permute-start.4 = (bf16[32,64]{1,0:T(8,128)(2,1)S(1)}, bf16[32,64]{1,0:T(8,128)(2,1)S(1)}, u32[]{:S(2)}, u32[]{:S(2)}) collective-permute-start(bf16[32,64]{1,0:T(8,128)(2,1)S(1)} %get-tuple-element.29), channel_id=1, source_target_pairs={{0,1},{1,2},{2,3},{3,4},{4,5},{5,6},{6,7},{7,8},{8,9},{9,10},{10,1... | collective-permute-start | bytes 12296 | tf_op jit(solution)/shard_map/ppermute | solution.py:24
  289.0 18.0 %collective-permute-start.5 = (bf16[32,64]{1,0:T(8,128)(2,1)S(1)}, bf16[32,64]{1,0:T(8,128)(2,1)S(1)}, u32[]{:S(2)}, u32[]{:S(2)}) collective-permute-start(bf16[32,64]{1,0:T(8,128)(2,1)S(1)} %get-tuple-element.30), channel_id=1, source_target_pairs={{1,0},{2,1},{3,2},{4,3},{5,4},{6,5},{7,6},{8,7},{9,8},{10,9},{11,1... | collective-permute-start | bytes 12296 | tf_op jit(solution)/shard_map/ppermute | solution.py:26
Sparse Core Ops, SparseCore 0:
  10.5 117.6 all-gather.1

commit v7 on v3

--- a/solution.py
+++ b/solution.py
@@ -31,7 +31,7 @@
 
 
 def total_over_devices(values):
-    for axis in ("seq", "band"):
+    for axis in ("band", "seq"):
         count = lax.axis_size(axis)
         spread = jnp.broadcast_to(values[None], (count,) + values.shape)
         rows = lax.all_to_all(spread, axis, split_axis=0, concat_axis=0, tiled=True)

time: 343 us -> 345 us (level)
    ppermute x3, waiting for transfers between devices: 19 us -> 22.5 us  [with_halo(): lax.ppermute(tail, axis, [(i, (i + 1) % count) for i in range(ends)])]
  transfers between devices with their start and end apart: 12 -> 12, of which waited for: 10 -> 9; matrix products, arithmetic and copies ran while one was open for 8% -> 8% of each run, Pallas kernels for 0% -> 0%
where the time goes in v7:
time: 345 us; the launch traced here: 342 us
  waiting for transfers between devices  119 us (34%)
  blocking collectives  76.4 us (22%)
  starting transfers between devices  64.3 us (19%)
  local copies, waits for them, and re-layouts  40.7 us (12%)
  matrix products  18.2 us (5%)
  between operations  13.9 us (4%)
  other arithmetic  9.58 us (3%)
    all_to_all x6, blocking collectives, total_over_devices(): rows = lax.all_to_all(spread, axis, split_axis=0, concat_axis=0, tiled=True)  76.4 us
    all_gather x1, waiting for transfers between devices, on_device(): gathered = lax.all_gather(embeddings, 'band', axis=0, tiled=True)  54.2 us
    all_to_all x4, waiting for transfers between devices, band_gather(): lax.all_to_all(spread, 'band', split_axis=0, concat_axis=0, tiled=True)  33.8 us
    all_to_all x4, starting transfers between devices, band_gather(): lax.all_to_all(spread, 'band', split_axis=0, concat_axis=0, tiled=True)  24.5 us
    ppermute x3, starting transfers between devices, with_halo(): lax.ppermute(head, axis, [((i + 1) % count, i) for i in range(ends)])  23.8 us
    ppermute x3, waiting for transfers between devices, with_halo(): lax.ppermute(tail, axis, [(i, (i + 1) % count) for i in range(ends)])  22.5 us
    all_to_all x1, starting transfers between devices, on_device(): lax.all_to_all(ordered, 'band', split_axis=1, concat_axis=1, tiled=True)  10.2 us
    gather x1, local copies, waits for them, and re-layouts, on_device(): partner_rows = gathered.reshape(-1, 128, embed_width)[partners]  9.99 us
  transfers between devices with their start and end apart: 12, of which 9 were waited for; matrix products, arithmetic and copies ran while one was open for 8% of the time, Pallas kernels for 0%

profile of v7, /device:TPU:6, one launch (start us, length us, event | category | flops | bytes accessed | tf_op | source)
XLA Modules:
  0.0 341.7 jit_solution(13110666037540494985)
XLA Ops:
  6.5 0.7 all-gather.2.cloned.1.call-update
  7.9 0.8 broadcast_multiply_fusion
  9.4 1.3 reduce.14
  10.8 0.7 compare_select_fusion.1
  11.5 1.3 gather_fusion
  13.0 0.8 reshape.829
  13.7 10.2 %all-to-all-start = ((bf16[32,2,256]{2,1,0:T(2,128)(2,1)}), bf16[32,2,256]{2,1,0:T(2,128)(2,1)S(1)}, u32[]{:S(2)}, u32[]{:S(2)}) async-start(bf16[32,2,256]{2,1,0:T(2,128)(2,1)} %reshape.829), calls=%async_computation | async-start | bytes 65536 | tf_op jit(solution)/shard_map/all_to_all | solution.py:57
  24.0 1.0 reduce-window.9
  25.4 6.7 %all-to-all-done = bf16[32,2,256]{2,1,0:T(2,128)(2,1)S(1)} async-done(((bf16[32,2,256]{2,1,0:T(2,128)(2,1)}), bf16[32,2,256]{2,1,0:T(2,128)(2,1)S(1)}, u32[]{:S(2)}, u32[]{:S(2)}) %all-to-all-start) | async-done | bytes 32800 | tf_op jit(solution)/shard_map/all_to_all | solution.py:57
  32.2 1.2 broadcast_in_dim.40
  33.4 5.8 %all-to-all-start.1 = ((bf16[32,32,512]{2,1,0:T(8,128)(2,1)}), bf16[32,32,512]{2,1,0:T(8,128)(2,1)S(1)}, u32[]{:S(2)}, u32[]{:S(2)}) async-start(bf16[32,32,512]{2,1,0:T(8,128)(2,1)} %broadcast_in_dim.40), calls=%async_computation.1 | async-start | bytes 2097152 | tf_op jit(solution)/shard_map/all_to_all | solution.py:45
  39.5 4.5 %gather_fusion.1 = s32[1024]{0:T(1024)S(1)} fusion(s32[640]{0:T(1024)S(1)} %convert_reduce_fusion.1, s32[1024]{0:T(1024)S(1)} %broadcast_clamp_fusion), kind=kCustom, calls=%fused_computation.1 | custom fusion | bytes 12288 | tf_op jit(solution)/shard_map/gather | solution.py:73
  44.2 2.3 gather_fusion.2
  46.5 6.8 %gather_fusion.3 = pred[1024]{0:T(1024)(128)(4,1)S(1)} fusion(pred[640]{0:T(1024)(128)(4,1)S(1)} %compare_and_fusion.1, s32[1024]{0:T(1024)S(1)} %broadcast_clamp_fusion), kind=kCustom, calls=%fused_computation.3 | custom fusion | bytes 6144 | tf_op jit(solution)/shard_map/gather | solution.py:74
  54.2 17.5 %all-to-all-done.1 = bf16[32,32,512]{2,1,0:T(8,128)(2,1)S(1)} async-done(((bf16[32,32,512]{2,1,0:T(8,128)(2,1)}), bf16[32,32,512]{2,1,0:T(8,128)(2,1)S(1)}, u32[]{:S(2)}, u32[]{:S(2)}) %all-to-all-start.1) | async-done | bytes 1048608 | tf_op jit(solution)/shard_map/all_to_all | solution.py:45
  71.7 54.2 %all-gather.2.cloned.1.call-done = bf16[16384,256]{1,0:T(8,128)(2,1)} async-done(((bf16[512,256]{1,0:T(8,128)(2,1)}), bf16[16384,256]{1,0:T(8,128)(2,1)}) %all-gather.2.cloned.1.call-update) | async-done | bytes 8388624 | tf_op jit(solution)/shard_map/all_gather | solution.py:80
  125.8 10.0 %gather_fusion.4 = bf16[128,128,256]{2,1,0:T(8,128)(2,1)} fusion(bf16[128,128,256]{2,1,0:T(8,128)(2,1)} %bitcast.181, s32[1024]{0:T(1024)S(1)} %pad_clamp_fusion), kind=kCustom, calls=%fused_computation.4 | custom fusion | bytes 16777728 | tf_op jit(solution)/shard_map/gather | solution.py:84
  135.8 7.7 %convert_reduce_fusion = (f32[4,128]{1,0:T(4,128)S(1)}, bf16[4,32,128,128]{3,2,1,0:T(8,128)(2,1)}) fusion(f32[4,32]{1,0:T(4,128)S(1)} %convert_multiply_fusion.6, bf16[4,32,128,256]{3,2,1,0:T(8,128)(2,1)} %bitcast.182, bf16[4,128,256,1]{2,1,3,0:T(8,128)(2,1)S(1)} %bitcast.198), kind=kOutput, calls=%fused_computation.8 | convolution fusion | flops 1086324224 | bytes 12847616 | tf_op jit(solution)/shard_map/tkje,tie->tkji/dot_general | solution.py:86
  143.6 1.9 collective-permute-start
  145.5 7.9 %collective-permute-start.1 = (bf16[32,64]{1,0:T(8,128)(2,1)S(1)}, bf16[32,64]{1,0:T(8,128)(2,1)S(1)}, u32[]{:S(2)}, u32[]{:S(2)}) collective-permute-start(bf16[32,64]{1,0:T(8,128)(2,1)S(1)} %get-tuple-element.42), channel_id=1, source_target_pairs={{1,0},{2,1},{3,2},{4,3},{5,4},{6,5},{7,6},{8,7},{9,8},{10,9},{11,1... | collective-permute-start | bytes 12296 | tf_op jit(solution)/shard_map/ppermute | solution.py:26
  154.0 7.1 %all-to-all-start.2 = ((f32[32,1,512]{2,1,0:T(1,128)}), f32[32,1,512]{2,1,0:T(1,128)S(1)}, u32[]{:S(2)}, u32[]{:S(2)}) async-start(f32[32,1,512]{2,1,0:T(1,128)} %mul.397), calls=%async_computation.2 | async-start | bytes 131072 | tf_op jit(solution)/shard_map/all_to_all | solution.py:45
  161.9 7.3 %all-to-all-done.2 = f32[32,1,512]{2,1,0:T(1,128)S(1)} async-done(((f32[32,1,512]{2,1,0:T(1,128)}), f32[32,1,512]{2,1,0:T(1,128)S(1)}, u32[]{:S(2)}, u32[]{:S(2)}) %all-to-all-start.2) | async-done | bytes 65568 | tf_op jit(solution)/shard_map/all_to_all | solution.py:45
  171.5 0.8 gather_fusion.5
  172.2 2.9 fusion.3
  175.6 12.9 %all_to_all.56 = f32[32,1,128]{2,1,0:T(1,128)S(1)} all-to-all(f32[32,1,128]{2,1,0:T(1,128)S(1)} %reshape.831), channel_id=1, replica_groups=mesh['band'=32,'seq'=16] {'band'}, dimensions={0} | all-to-all | bytes 32768 | tf_op jit(solution)/shard_map/all_to_all | solution.py:37
  190.0 12.7 %all_to_all.57 = f32[16,1,128]{2,1,0:T(1,128)S(1)} all-to-all(f32[16,1,128]{2,1,0:T(1,128)S(1)} %reshape.833), channel_id=1, replica_groups=mesh['band'=32,'seq'=16] {'seq'}, dimensions={0} | all-to-all | bytes 16384 | tf_op jit(solution)/shard_map/all_to_all | solution.py:37
  203.6 1.1 broadcast_in_dim.44
  204.7 5.8 %all-to-all-start.5 = ((bf16[32,32,512]{2,1,0:T(8,128)(2,1)}), bf16[32,32,512]{2,1,0:T(8,128)(2,1)S(1)}, u32[]{:S(2)}, u32[]{:S(2)}) async-start(bf16[32,32,512]{2,1,0:T(8,128)(2,1)} %broadcast_in_dim.44), calls=%async_computation.5 | async-start | bytes 2097152 | tf_op jit(solution)/shard_map/all_to_all | solution.py:45
  210.6 1.9 collective-permute-start.2
  212.5 7.9 %collective-permute-start.3 = (bf16[32,64]{1,0:T(8,128)(2,1)S(1)}, bf16[32,64]{1,0:T(8,128)(2,1)S(1)}, u32[]{:S(2)}, u32[]{:S(2)}) collective-permute-start(bf16[32,64]{1,0:T(8,128)(2,1)S(1)} %get-tuple-element.36), channel_id=1, source_target_pairs={{1,0},{2,1},{3,2},{4,3},{5,4},{6,5},{7,6},{8,7},{9,8},{10,9},{11,1... | collective-permute-start | bytes 12296 | tf_op jit(solution)/shard_map/ppermute | solution.py:26
  220.4 10.5 %collective-permute-done.2 = bf16[32,64]{1,0:T(8,128)(2,1)S(1)} collective-permute-done((bf16[32,64]{1,0:T(8,128)(2,1)S(1)}, bf16[32,64]{1,0:T(8,128)(2,1)S(1)}, u32[]{:S(2)}, u32[]{:S(2)}) %collective-permute-start.2) | collective-permute-done | bytes 4128 | tf_op jit(solution)/shard_map/ppermute | solution.py:24
  230.9 0.7 collective-permute-done.3
  232.3 4.9 %all-to-all-done.5 = bf16[32,32,512]{2,1,0:T(8,128)(2,1)S(1)} async-done(((bf16[32,32,512]{2,1,0:T(8,128)(2,1)}), bf16[32,32,512]{2,1,0:T(8,128)(2,1)S(1)}, u32[]{:S(2)}, u32[]{:S(2)}) %all-to-all-start.5) | async-done | bytes 1048608 | tf_op jit(solution)/shard_map/all_to_all | solution.py:45
  239.2 0.8 gather_fusion.6
  239.9 2.9 fusion.2
  243.3 15.3 %all_to_all.58 = f32[32,3,32]{2,1,0:T(4,128)S(1)} all-to-all(f32[32,3,32]{2,1,0:T(4,128)S(1)} %broadcast_in_dim.45), channel_id=1, replica_groups=mesh['band'=32,'seq'=16] {'band'}, dimensions={0} | all-to-all | bytes 24576 | tf_op jit(solution)/shard_map/all_to_all | solution.py:37
  258.6 10.3 %all_to_all.59 = f32[16,3,32]{2,1,0:T(4,128)S(1)} all-to-all(f32[16,3,32]{2,1,0:T(4,128)S(1)} %broadcast_in_dim.46), channel_id=1, replica_groups=mesh['band'=32,'seq'=16] {'seq'}, dimensions={0} | all-to-all | bytes 12288 | tf_op jit(solution)/shard_map/all_to_all | solution.py:37
  269.0 1.1 broadcast_in_dim.47
  270.1 5.8 %all-to-all-start.8 = ((bf16[32,32,512]{2,1,0:T(8,128)(2,1)}), bf16[32,32,512]{2,1,0:T(8,128)(2,1)S(1)}, u32[]{:S(2)}, u32[]{:S(2)}) async-start(bf16[32,32,512]{2,1,0:T(8,128)(2,1)} %broadcast_in_dim.47), calls=%async_computation.8 | async-start | bytes 2097152 | tf_op jit(solution)/shard_map/all_to_all | solution.py:45
  276.0 1.9 collective-permute-start.4
  277.9 8.1 %collective-permute-start.5 = (bf16[32,64]{1,0:T(8,128)(2,1)S(1)}, bf16[32,64]{1,0:T(8,128)(2,1)S(1)}, u32[]{:S(2)}, u32[]{:S(2)}) collective-permute-start(bf16[32,64]{1,0:T(8,128)(2,1)S(1)} %get-tuple-element.30), channel_id=1, source_target_pairs={{1,0},{2,1},{3,2},{4,3},{5,4},{6,5},{7,6},{8,7},{9,8},{10,9},{11,1... | collective-permute-start | bytes 12296 | tf_op jit(solution)/shard_map/ppermute | solution.py:26
  286.0 12.0 %collective-permute-done.4 = bf16[32,64]{1,0:T(8,128)(2,1)S(1)} collective-permute-done((bf16[32,64]{1,0:T(8,128)(2,1)S(1)}, bf16[32,64]{1,0:T(8,128)(2,1)S(1)}, u32[]{:S(2)}, u32[]{:S(2)}) %collective-permute-start.4) | collective-permute-done | bytes 4128 | tf_op jit(solution)/shard_map/ppermute | solution.py:24
  298.7 4.1 %all-to-all-done.8 = bf16[32,32,512]{2,1,0:T(8,128)(2,1)S(1)} async-done(((bf16[32,32,512]{2,1,0:T(8,128)(2,1)}), bf16[32,32,512]{2,1,0:T(8,128)(2,1)S(1)}, u32[]{:S(2)}, u32[]{:S(2)}) %all-to-all-start.8) | async-done | bytes 1048608 | tf_op jit(solution)/shard_map/all_to_all | solution.py:45
  304.8 0.8 gather_fusion.7
  305.6 2.9 fusion.1
  308.9 15.1 %all_to_all.60 = f32[32,1,32]{2,1,0:T(1,128)S(1)} all-to-all(f32[32,1,32]{2,1,0:T(1,128)S(1)} %broadcast_in_dim.48), channel_id=1, replica_groups=mesh['band'=32,'seq'=16] {'band'}, dimensions={0} | all-to-all | bytes 8192 | tf_op jit(solution)/shard_map/all_to_all | solution.py:37
  324.0 10.1 %all_to_all.61 = f32[16,1,32]{2,1,0:T(1,128)S(1)} all-to-all(f32[16,1,32]{2,1,0:T(1,128)S(1)} %broadcast_in_dim.49), channel_id=1, replica_groups=mesh['band'=32,'seq'=16] {'seq'}, dimensions={0} | all-to-all | bytes 4096 | tf_op jit(solution)/shard_map/all_to_all | solution.py:37
  334.1 0.7 fusion.19
  (99 shorter events, 16.2 us)
Async XLA Ops:
  6.5 46.8 %copy-start.1 = (s32[4,32]{1,0:T(4,128)S(1)}, s32[4,32]{1,0:T(4,128)}, u32[]{:S(2)}) copy-start(s32[4,32]{1,0:T(4,128)} %param.12) | copy-start | bytes 1540
  6.5 47.6 %copy-start.2 = (s32[4,32]{1,0:T(4,128)S(1)}, s32[4,32]{1,0:T(4,128)}, u32[]{:S(2)}) copy-start(s32[4,32]{1,0:T(4,128)} %param.13) | copy-start | bytes 1540
  6.5 119.3 %all-gather.2.cloned.1.call-start = ((), (), s32[]{:S(2)}) async-start(), calls=%async_computation.11 | async-start | bytes 8650752 | tf_op jit(solution)/shard_map/all_gather | solution.py:80
  13.7 18.3 %all-to-all-start = ((bf16[32,2,256]{2,1,0:T(2,128)(2,1)}), bf16[32,2,256]{2,1,0:T(2,128)(2,1)S(1)}, u32[]{:S(2)}, u32[]{:S(2)}) async-start(bf16[32,2,256]{2,1,0:T(2,128)(2,1)} %reshape.829), calls=%async_computation | async-start | bytes 65536 | tf_op jit(solution)/shard_map/all_to_all | solution.py:57
  33.4 38.2 %all-to-all-start.1 = ((bf16[32,32,512]{2,1,0:T(8,128)(2,1)}), bf16[32,32,512]{2,1,0:T(8,128)(2,1)S(1)}, u32[]{:S(2)}, u32[]{:S(2)}) async-start(bf16[32,32,512]{2,1,0:T(8,128)(2,1)} %broadcast_in_dim.40), calls=%async_computation.1 | async-start | bytes 2097152 | tf_op jit(solution)/shard_map/all_to_all | solution.py:45
  125.8 10.0 %copy-start = (bf16[512,256]{1,0:T(8,128)(2,1)S(1)}, bf16[512,256]{1,0:T(8,128)(2,1)}, u32[]{:S(2)}) copy-start(bf16[512,256]{1,0:T(8,128)(2,1)} %param.11) | copy-start | bytes 786436
  143.6 17.6 %collective-permute-start = (bf16[32,64]{1,0:T(8,128)(2,1)S(1)}, bf16[32,64]{1,0:T(8,128)(2,1)S(1)}, u32[]{:S(2)}, u32[]{:S(2)}) collective-permute-start(bf16[32,64]{1,0:T(8,128)(2,1)S(1)} %get-tuple-element.41), channel_id=1, source_target_pairs={{0,1},{1,2},{2,3},{3,4},{4,5},{5,6},{6,7},{7,8},{8,9},{9,10},{10,1... | collective-permute-start | bytes 12296 | tf_op jit(solution)/shard_map/ppermute | solution.py:24
  145.5 15.7 %collective-permute-start.1 = (bf16[32,64]{1,0:T(8,128)(2,1)S(1)}, bf16[32,64]{1,0:T(8,128)(2,1)S(1)}, u32[]{:S(2)}, u32[]{:S(2)}) collective-permute-start(bf16[32,64]{1,0:T(8,128)(2,1)S(1)} %get-tuple-element.42), channel_id=1, source_target_pairs={{1,0},{2,1},{3,2},{4,3},{5,4},{6,5},{7,6},{8,7},{9,8},{10,9},{11,1... | collective-permute-start | bytes 12296 | tf_op jit(solution)/shard_map/ppermute | solution.py:26
  154.0 15.2 %all-to-all-start.2 = ((f32[32,1,512]{2,1,0:T(1,128)}), f32[32,1,512]{2,1,0:T(1,128)S(1)}, u32[]{:S(2)}, u32[]{:S(2)}) async-start(f32[32,1,512]{2,1,0:T(1,128)} %mul.397), calls=%async_computation.2 | async-start | bytes 131072 | tf_op jit(solution)/shard_map/all_to_all | solution.py:45
  204.7 32.5 %all-to-all-start.5 = ((bf16[32,32,512]{2,1,0:T(8,128)(2,1)}), bf16[32,32,512]{2,1,0:T(8,128)(2,1)S(1)}, u32[]{:S(2)}, u32[]{:S(2)}) async-start(bf16[32,32,512]{2,1,0:T(8,128)(2,1)} %broadcast_in_dim.44), calls=%async_computation.5 | async-start | bytes 2097152 | tf_op jit(solution)/shard_map/all_to_all | solution.py:45
  210.6 20.3 %collective-permute-start.2 = (bf16[32,64]{1,0:T(8,128)(2,1)S(1)}, bf16[32,64]{1,0:T(8,128)(2,1)S(1)}, u32[]{:S(2)}, u32[]{:S(2)}) collective-permute-start(bf16[32,64]{1,0:T(8,128)(2,1)S(1)} %get-tuple-element.35), channel_id=1, source_target_pairs={{0,1},{1,2},{2,3},{3,4},{4,5},{5,6},{6,7},{7,8},{8,9},{9,10},{10,1... | collective-permute-start | bytes 12296 | tf_op jit(solution)/shard_map/ppermute | solution.py:24
  212.5 19.1 %collective-permute-start.3 = (bf16[32,64]{1,0:T(8,128)(2,1)S(1)}, bf16[32,64]{1,0:T(8,128)(2,1)S(1)}, u32[]{:S(2)}, u32[]{:S(2)}) collective-permute-start(bf16[32,64]{1,0:T(8,128)(2,1)S(1)} %get-tuple-element.36), channel_id=1, source_target_pairs={{1,0},{2,1},{3,2},{4,3},{5,4},{6,5},{7,6},{8,7},{9,8},{10,9},{11,1... | collective-permute-start | bytes 12296 | tf_op jit(solution)/shard_map/ppermute | solution.py:26
  270.1 32.7 %all-to-all-start.8 = ((bf16[32,32,512]{2,1,0:T(8,128)(2,1)}), bf16[32,32,512]{2,1,0:T(8,128)(2,1)S(1)}, u32[]{:S(2)}, u32[]{:S(2)}) async-start(bf16[32,32,512]{2,1,0:T(8,128)(2,1)} %broadcast_in_dim.47), calls=%async_computation.8 | async-start | bytes 2097152 | tf_op jit(solution)/shard_map/all_to_all | solution.py:45
  276.0 22.0 %collective-permute-start.4 = (bf16[32,64]{1,0:T(8,128)(2,1)S(1)}, bf16[32,64]{1,0:T(8,128)(2,1)S(1)}, u32[]{:S(2)}, u32[]{:S(2)}) collective-permute-start(bf16[32,64]{1,0:T(8,128)(2,1)S(1)} %get-tuple-element.29), channel_id=1, source_target_pairs={{0,1},{1,2},{2,3},{3,4},{4,5},{5,6},{6,7},{7,8},{8,9},{9,10},{10,1... | collective-permute-start | bytes 12296 | tf_op jit(solution)/shard_map/ppermute | solution.py:24
  277.9 20.1 %collective-permute-start.5 = (bf16[32,64]{1,0:T(8,128)(2,1)S(1)}, bf16[32,64]{1,0:T(8,128)(2,1)S(1)}, u32[]{:S(2)}, u32[]{:S(2)}) collective-permute-start(bf16[32,64]{1,0:T(8,128)(2,1)S(1)} %get-tuple-element.30), channel_id=1, source_target_pairs={{1,0},{2,1},{3,2},{4,3},{5,4},{6,5},{7,6},{8,7},{9,8},{10,9},{11,1... | collective-permute-start | bytes 12296 | tf_op jit(solution)/shard_map/ppermute | solution.py:26
Sparse Core Ops, SparseCore 0:
  10.5 115.2 all-gather.1

commit v8 on v6

--- a/solution.py
+++ b/solution.py
@@ -54,8 +54,14 @@
     ordered = jnp.take(seeded, frame_perm[0], axis=1).reshape(
         channels, band_count, frames // band_count
     )
-    from_bands = band_gather(ordered)
-    labels_band = jnp.transpose(from_bands, (2, 1, 0, 3)).reshape(band_count, channels, frames)
+    embed_width = embeddings.shape[1]
+    carried = jnp.concatenate([embeddings, ordered.reshape(channels, frames).T], axis=1)
+    carried = lax.all_gather(carried, "band", axis=0, tiled=True)
+    gathered = carried[:, :embed_width]
+    labels_band = jnp.transpose(
+        carried[:, embed_width:].reshape(band_count, band_count, frames // band_count, channels),
+        (1, 3, 0, 2),
+    ).reshape(band_count, channels, frames)
     arrived = lax.dynamic_index_in_dim(labels_band, lax.axis_index("band"), axis=0, keepdims=False)
     labels = arrived.astype(jnp.float32)
     device = lax.axis_index("band") * groups + lax.axis_index("seq")
@@ -79,9 +85,6 @@
         linked, jnp.exp(-offset.astype(jnp.float32) / decay_len), jnp.float32(0.0)
     ).astype(jnp.bfloat16)
     near_degree = jnp.sum(band_tiles.astype(jnp.float32), axis=1).reshape(frames)
-    gathered = lax.all_gather(embeddings, "band", axis=0, tiled=True)
-    labels_band, gathered = lax.optimization_barrier((labels_band, gathered))
-    embed_width = embeddings.shape[1]
     partner_rows = gathered.reshape(-1, 128, embed_width)[partners]
     own_rows = embeddings.reshape(tile_count, 128, embed_width)
     inner_prod = jnp.einsum(

time: 354 us -> 379 us (1.071)
  waiting for transfers between devices: 123 us -> 164 us
  starting transfers between devices: 72.1 us -> 61.8 us
  local copies, waits for them, and re-layouts: 61.2 us -> 53.1 us
    all_gather x1, waiting for transfers between devices: 51.3 us -> 111 us  [on_device(): carried = lax.all_gather(carried, 'band', axis=0, tiled=True)]
    all_to_all x4 -> x3, waiting for transfers between devices: 35.5 us -> 17.4 us  [band_gather(): lax.all_to_all(spread, 'band', split_axis=0, concat_axis=0, tiled=True)]
    unnamed x21 -> x13, local copies, waits for them, and re-layouts: 17.5 us -> 3.04 us
    all_to_all x4 -> x3, starting transfers between devices: 29 us -> 18.9 us  [band_gather(): lax.all_to_all(spread, 'band', split_axis=0, concat_axis=0, tiled=True)]
    slice x1 -> x4, local copies, waits for them, and re-layouts: 0.07 us -> 9.29 us  [the longest x1 7.02 us: on_device(): gathered = carried[:, :embed_width]]
    transpose x2 -> x0, local copies, waits for them, and re-layouts: 4.08 us -> none  [on_device(): jnp.transpose(from_bands, (2, 1, 0, 3))]
  transfers between devices with their start and end apart: 13 -> 12, of which waited for: 11 -> 10; matrix products, arithmetic and copies ran while one was open for 12% -> 5% of each run, Pallas kernels for 0% -> 0%
where the time goes in v8:
time: 379 us; the launch traced here: 377 us
  waiting for transfers between devices  164 us (43%)
  starting transfers between devices  61.8 us (16%)
  local copies, waits for them, and re-layouts  53.1 us (14%)
  blocking collectives  48.8 us (13%)
  matrix products  18.3 us (5%)
  other arithmetic  17.1 us (5%)
  between operations  13.9 us (4%)
    all_gather x1, waiting for transfers between devices, on_device(): carried = lax.all_gather(carried, 'band', axis=0, tiled=True)  111 us
    all_to_all x4, blocking collectives, total_over_devices(): rows = lax.all_to_all(spread, axis, split_axis=0, concat_axis=0, tiled=True)  48.8 us
    ppermute x3, starting transfers between devices, with_halo(): lax.ppermute(head, axis, [((i + 1) % count, i) for i in range(ends)])  23.6 us
    ppermute x3, waiting for transfers between devices, with_halo(): lax.ppermute(tail, axis, [(i, (i + 1) % count) for i in range(ends)])  19.1 us
    all_to_all x3, starting transfers between devices, band_gather(): lax.all_to_all(spread, 'band', split_axis=0, concat_axis=0, tiled=True)  18.9 us
    all_to_all x3, waiting for transfers between devices, band_gather(): lax.all_to_all(spread, 'band', split_axis=0, concat_axis=0, tiled=True)  17.4 us
    all_to_all x2, waiting for transfers between devices, total_over_devices(): rows = lax.all_to_all(spread, axis, split_axis=0, concat_axis=0, tiled=True)  15.7 us
    all_to_all x2, starting transfers between devices, total_over_devices(): rows = lax.all_to_all(spread, axis, split_axis=0, concat_axis=0, tiled=True)  13.6 us
  transfers between devices with their start and end apart: 12, of which 10 were waited for; matrix products, arithmetic and copies ran while one was open for 5% of the time, Pallas kernels for 0%

profile of v8, /device:TPU:6, one launch (start us, length us, event | category | flops | bytes accessed | tf_op | source)
XLA Modules:
  0.0 377.0 jit_solution(4030182476258636887)
XLA Ops:
  8.6 0.8 broadcast_multiply_fusion
  9.5 1.3 gather_fusion
  11.0 1.8 pad_maximum_fusion
  12.8 1.0 reduce-window.9
  15.3 2.3 gather_fusion.2
  17.6 4.5 %gather_fusion.1 = s32[1024]{0:T(1024)S(1)} fusion(s32[640]{0:T(1024)S(1)} %convert_reduce_fusion.1, s32[1024]{0:T(1024)S(1)} %broadcast_clamp_fusion), kind=kCustom, calls=%fused_computation.1 | custom fusion | bytes 12288 | tf_op jit(solution)/shard_map/gather | solution.py:81
  22.2 6.8 %gather_fusion.3 = pred[1024]{0:T(1024)(128)(4,1)S(1)} fusion(pred[640]{0:T(1024)(128)(4,1)S(1)} %compare_and_fusion, s32[1024]{0:T(1024)S(1)} %broadcast_clamp_fusion), kind=kCustom, calls=%fused_computation.3 | custom fusion | bytes 6144 | tf_op jit(solution)/shard_map/gather | solution.py:82
  29.7 110.7 %all-gather.2.cloned.1.call-done = bf16[16384,288]{1,0:T(8,128)(2,1)} async-done(((bf16[512,288]{1,0:T(8,128)(2,1)}), bf16[16384,288]{1,0:T(8,128)(2,1)}) %all-gather.2.cloned.1.call-update) | async-done | bytes 9437200 | tf_op jit(solution)/shard_map/all_gather | solution.py:59
  140.4 2.2 slice-done
  142.6 1.2 copy.76
  143.8 2.0 copy-done
  145.8 7.0 %slice.140 = bf16[16384,256]{1,0:T(8,128)(2,1)} slice(bf16[16384,288]{1,0:T(8,128)(2,1)} %all-gather.2.cloned.1.call-done), slice={[0:16384], [0:256]} | slice | bytes 16777216 | tf_op jit(solution)/shard_map/slice | solution.py:60
  152.9 10.0 %gather_fusion.4 = bf16[128,128,256]{2,1,0:T(8,128)(2,1)} fusion(bf16[128,128,256]{2,1,0:T(8,128)(2,1)} %bitcast.265, s32[1024]{0:T(1024)S(1)} %pad_clamp_fusion), kind=kCustom, calls=%fused_computation.4 | custom fusion | bytes 16777728 | tf_op jit(solution)/shard_map/gather | solution.py:88
  162.9 7.7 %convert_reduce_fusion = (f32[4,128]{1,0:T(4,128)S(1)}, bf16[4,32,128,128]{3,2,1,0:T(8,128)(2,1)}) fusion(f32[4,32]{1,0:T(4,128)S(1)} %convert_multiply_fusion.1, bf16[4,32,128,256]{3,2,1,0:T(8,128)(2,1)} %bitcast.269, bf16[4,128,256,1]{2,1,3,0:T(8,128)(2,1)S(1)} %bitcast.278), kind=kOutput, calls=%fused_computation.9 | convolution fusion | flops 1086324224 | bytes 12847616 | tf_op jit(solution)/shard_map/tkje,tie->tkji/dot_general | solution.py:90
  170.7 1.9 collective-permute-start
  172.6 7.9 %collective-permute-start.1 = (bf16[32,64]{1,0:T(8,128)(2,1)S(1)}, bf16[32,64]{1,0:T(8,128)(2,1)S(1)}, u32[]{:S(2)}, u32[]{:S(2)}) collective-permute-start(bf16[32,64]{1,0:T(8,128)(2,1)S(1)} %get-tuple-element.38), channel_id=1, source_target_pairs={{1,0},{2,1},{3,2},{4,3},{5,4},{6,5},{7,6},{8,7},{9,8},{10,9},{11,1... | collective-permute-start | bytes 12296 | tf_op jit(solution)/shard_map/ppermute | solution.py:26
  181.1 7.1 %all-to-all-start = ((f32[32,1,512]{2,1,0:T(1,128)}), f32[32,1,512]{2,1,0:T(1,128)S(1)}, u32[]{:S(2)}, u32[]{:S(2)}) async-start(f32[32,1,512]{2,1,0:T(1,128)} %mul.350), calls=%async_computation | async-start | bytes 131072 | tf_op jit(solution)/shard_map/all_to_all | solution.py:45
  188.9 7.4 %all-to-all-done = f32[32,1,512]{2,1,0:T(1,128)S(1)} async-done(((f32[32,1,512]{2,1,0:T(1,128)}), f32[32,1,512]{2,1,0:T(1,128)S(1)}, u32[]{:S(2)}, u32[]{:S(2)}) %all-to-all-start) | async-done | bytes 65568 | tf_op jit(solution)/shard_map/all_to_all | solution.py:45
  196.4 5.8 %multiply_convert_fusion = bf16[32,32,512]{1,2,0:T(8,128)(2,1)} fusion(f32[32,512]{1,0:T(8,128)S(1)} %bitcast.277, bf16[32,32,16,32]{3,2,0,1:T(8,128)(2,1)} %copy-done), kind=kLoop, calls=%fused_computation.8 | loop fusion | flops 1572864 | bytes 2162688 | tf_op jit(solution)/shard_map/convert_element_type | solution.py:121
  202.2 3.6 copy.79
  205.7 0.8 gather_fusion.5
  206.5 2.9 fusion.3
  209.7 12.7 %all_to_all.46 = f32[16,1,128]{2,1,0:T(1,128)S(1)} all-to-all(f32[16,1,128]{2,1,0:T(1,128)S(1)} %reshape.643), channel_id=1, replica_groups=mesh['band'=32,'seq'=16] {'seq'}, dimensions={0} | all-to-all | bytes 16384 | tf_op jit(solution)/shard_map/all_to_all | solution.py:37
  224.6 5.7 %all-to-all-start.2 = ((f32[32,1,128]{2,1,0:T(1,128)}), f32[32,1,128]{2,1,0:T(1,128)S(1)}, u32[]{:S(2)}, u32[]{:S(2)}) async-start(f32[32,1,128]{2,1,0:T(1,128)} %reshape.645), calls=%async_computation.2 | async-start | bytes 32768 | tf_op jit(solution)/shard_map/all_to_all | solution.py:37
  230.4 7.7 %all-to-all-done.2 = f32[32,1,128]{2,1,0:T(1,128)S(1)} async-done(((f32[32,1,128]{2,1,0:T(1,128)}), f32[32,1,128]{2,1,0:T(1,128)S(1)}, u32[]{:S(2)}, u32[]{:S(2)}) %all-to-all-start.2) | async-done | bytes 16416 | tf_op jit(solution)/shard_map/all_to_all | solution.py:37
  238.1 0.7 reduce.5
  239.1 1.1 broadcast_in_dim.43
  240.2 6.0 %all-to-all-start.3 = ((bf16[32,32,512]{2,1,0:T(8,128)(2,1)}), bf16[32,32,512]{2,1,0:T(8,128)(2,1)S(1)}, u32[]{:S(2)}, u32[]{:S(2)}) async-start(bf16[32,32,512]{2,1,0:T(8,128)(2,1)} %broadcast_in_dim.43), calls=%async_computation.3 | async-start | bytes 2097152 | tf_op jit(solution)/shard_map/all_to_all | solution.py:45
  246.4 1.9 collective-permute-start.2
  248.3 7.9 %collective-permute-start.3 = (bf16[32,64]{1,0:T(8,128)(2,1)S(1)}, bf16[32,64]{1,0:T(8,128)(2,1)S(1)}, u32[]{:S(2)}, u32[]{:S(2)}) collective-permute-start(bf16[32,64]{1,0:T(8,128)(2,1)S(1)} %get-tuple-element.32), channel_id=1, source_target_pairs={{1,0},{2,1},{3,2},{4,3},{5,4},{6,5},{7,6},{8,7},{9,8},{10,9},{11,1... | collective-permute-start | bytes 12296 | tf_op jit(solution)/shard_map/ppermute | solution.py:26
  256.2 9.6 %collective-permute-done.2 = bf16[32,64]{1,0:T(8,128)(2,1)S(1)} collective-permute-done((bf16[32,64]{1,0:T(8,128)(2,1)S(1)}, bf16[32,64]{1,0:T(8,128)(2,1)S(1)}, u32[]{:S(2)}, u32[]{:S(2)}) %collective-permute-start.2) | collective-permute-done | bytes 4128 | tf_op jit(solution)/shard_map/ppermute | solution.py:24
  267.0 5.0 %all-to-all-done.3 = bf16[32,32,512]{2,1,0:T(8,128)(2,1)S(1)} async-done(((bf16[32,32,512]{2,1,0:T(8,128)(2,1)}), bf16[32,32,512]{2,1,0:T(8,128)(2,1)S(1)}, u32[]{:S(2)}, u32[]{:S(2)}) %all-to-all-start.3) | async-done | bytes 1048608 | tf_op jit(solution)/shard_map/all_to_all | solution.py:45
  274.0 0.8 gather_fusion.6
  274.8 2.9 fusion.2
  278.0 10.3 %all_to_all.47 = f32[16,3,32]{2,1,0:T(4,128)S(1)} all-to-all(f32[16,3,32]{2,1,0:T(4,128)S(1)} %broadcast_in_dim.44), channel_id=1, replica_groups=mesh['band'=32,'seq'=16] {'seq'}, dimensions={0} | all-to-all | bytes 12288 | tf_op jit(solution)/shard_map/all_to_all | solution.py:37
  288.9 7.9 %all-to-all-start.5 = ((f32[32,3,32]{2,1,0:T(4,128)}), f32[32,3,32]{2,1,0:T(4,128)S(1)}, u32[]{:S(2)}, u32[]{:S(2)}) async-start(f32[32,3,32]{2,1,0:T(4,128)} %broadcast_in_dim.45), calls=%async_computation.5 | async-start | bytes 131072 | tf_op jit(solution)/shard_map/all_to_all | solution.py:37
  296.9 8.0 %all-to-all-done.5 = f32[32,3,32]{2,1,0:T(4,128)S(1)} async-done(((f32[32,3,32]{2,1,0:T(4,128)}), f32[32,3,32]{2,1,0:T(4,128)S(1)}, u32[]{:S(2)}, u32[]{:S(2)}) %all-to-all-start.5) | async-done | bytes 12320 | tf_op jit(solution)/shard_map/all_to_all | solution.py:37
  305.1 1.1 broadcast_in_dim.47
  306.2 5.8 %all-to-all-start.6 = ((bf16[32,32,512]{2,1,0:T(8,128)(2,1)}), bf16[32,32,512]{2,1,0:T(8,128)(2,1)S(1)}, u32[]{:S(2)}, u32[]{:S(2)}) async-start(bf16[32,32,512]{2,1,0:T(8,128)(2,1)} %broadcast_in_dim.47), calls=%async_computation.6 | async-start | bytes 2097152 | tf_op jit(solution)/shard_map/all_to_all | solution.py:45
  312.2 1.9 collective-permute-start.4
  314.1 7.9 %collective-permute-start.5 = (bf16[32,64]{1,0:T(8,128)(2,1)S(1)}, bf16[32,64]{1,0:T(8,128)(2,1)S(1)}, u32[]{:S(2)}, u32[]{:S(2)}) collective-permute-start(bf16[32,64]{1,0:T(8,128)(2,1)S(1)} %get-tuple-element.26), channel_id=1, source_target_pairs={{1,0},{2,1},{3,2},{4,3},{5,4},{6,5},{7,6},{8,7},{9,8},{10,9},{11,1... | collective-permute-start | bytes 12296 | tf_op jit(solution)/shard_map/ppermute | solution.py:26
  322.0 9.5 %collective-permute-done.4 = bf16[32,64]{1,0:T(8,128)(2,1)S(1)} collective-permute-done((bf16[32,64]{1,0:T(8,128)(2,1)S(1)}, bf16[32,64]{1,0:T(8,128)(2,1)S(1)}, u32[]{:S(2)}, u32[]{:S(2)}) %collective-permute-start.4) | collective-permute-done | bytes 4128 | tf_op jit(solution)/shard_map/ppermute | solution.py:24
  332.8 5.0 %all-to-all-done.6 = bf16[32,32,512]{2,1,0:T(8,128)(2,1)S(1)} async-done(((bf16[32,32,512]{2,1,0:T(8,128)(2,1)}), bf16[32,32,512]{2,1,0:T(8,128)(2,1)S(1)}, u32[]{:S(2)}, u32[]{:S(2)}) %all-to-all-start.6) | async-done | bytes 1048608 | tf_op jit(solution)/shard_map/all_to_all | solution.py:45
  339.7 0.8 gather_fusion.7
  340.5 2.9 fusion.1
  343.6 10.1 %all_to_all.48 = f32[16,1,32]{2,1,0:T(1,128)S(1)} all-to-all(f32[16,1,32]{2,1,0:T(1,128)S(1)} %broadcast_in_dim.48), channel_id=1, replica_groups=mesh['band'=32,'seq'=16] {'seq'}, dimensions={0} | all-to-all | bytes 4096 | tf_op jit(solution)/shard_map/all_to_all | solution.py:37
  353.7 15.6 %all_to_all.49 = f32[32,1,32]{2,1,0:T(1,128)S(1)} all-to-all(f32[32,1,32]{2,1,0:T(1,128)S(1)} %broadcast_in_dim.49), channel_id=1, replica_groups=mesh['band'=32,'seq'=16] {'band'}, dimensions={0} | all-to-all | bytes 8192 | tf_op jit(solution)/shard_map/all_to_all | solution.py:37
  369.4 0.7 fusion.24
  (96 shorter events, 16.9 us)
Async XLA Ops:
  6.5 23.2 %copy-start.2 = (s32[4,32]{1,0:T(4,128)S(1)}, s32[4,32]{1,0:T(4,128)}, u32[]{:S(2)}) copy-start(s32[4,32]{1,0:T(4,128)} %param.13) | copy-start | bytes 1540
  6.5 133.9 %all-gather.2.cloned.1.call-start = ((), (), s32[]{:S(2)}) async-start(), calls=%async_computation.9 | async-start | bytes 12976128 | tf_op jit(solution)/shard_map/all_gather | solution.py:59
  140.4 2.2 slice-start
  143.8 2.0 copy-start
  152.9 10.0 %copy-start.1 = (bf16[512,256]{1,0:T(8,128)(2,1)S(1)}, bf16[512,256]{1,0:T(8,128)(2,1)}, u32[]{:S(2)}) copy-start(bf16[512,256]{1,0:T(8,128)(2,1)} %param.11) | copy-start | bytes 786436
  170.7 17.5 %collective-permute-start = (bf16[32,64]{1,0:T(8,128)(2,1)S(1)}, bf16[32,64]{1,0:T(8,128)(2,1)S(1)}, u32[]{:S(2)}, u32[]{:S(2)}) collective-permute-start(bf16[32,64]{1,0:T(8,128)(2,1)S(1)} %get-tuple-element.37), channel_id=1, source_target_pairs={{0,1},{1,2},{2,3},{3,4},{4,5},{5,6},{6,7},{7,8},{8,9},{9,10},{10,1... | collective-permute-start | bytes 12296 | tf_op jit(solution)/shard_map/ppermute | solution.py:24
  172.6 15.6 %collective-permute-start.1 = (bf16[32,64]{1,0:T(8,128)(2,1)S(1)}, bf16[32,64]{1,0:T(8,128)(2,1)S(1)}, u32[]{:S(2)}, u32[]{:S(2)}) collective-permute-start(bf16[32,64]{1,0:T(8,128)(2,1)S(1)} %get-tuple-element.38), channel_id=1, source_target_pairs={{1,0},{2,1},{3,2},{4,3},{5,4},{6,5},{7,6},{8,7},{9,8},{10,9},{11,1... | collective-permute-start | bytes 12296 | tf_op jit(solution)/shard_map/ppermute | solution.py:26
  181.1 15.2 %all-to-all-start = ((f32[32,1,512]{2,1,0:T(1,128)}), f32[32,1,512]{2,1,0:T(1,128)S(1)}, u32[]{:S(2)}, u32[]{:S(2)}) async-start(f32[32,1,512]{2,1,0:T(1,128)} %mul.350), calls=%async_computation | async-start | bytes 131072 | tf_op jit(solution)/shard_map/all_to_all | solution.py:45
  224.6 13.5 %all-to-all-start.2 = ((f32[32,1,128]{2,1,0:T(1,128)}), f32[32,1,128]{2,1,0:T(1,128)S(1)}, u32[]{:S(2)}, u32[]{:S(2)}) async-start(f32[32,1,128]{2,1,0:T(1,128)} %reshape.645), calls=%async_computation.2 | async-start | bytes 32768 | tf_op jit(solution)/shard_map/all_to_all | solution.py:37
  240.2 31.9 %all-to-all-start.3 = ((bf16[32,32,512]{2,1,0:T(8,128)(2,1)}), bf16[32,32,512]{2,1,0:T(8,128)(2,1)S(1)}, u32[]{:S(2)}, u32[]{:S(2)}) async-start(bf16[32,32,512]{2,1,0:T(8,128)(2,1)} %broadcast_in_dim.43), calls=%async_computation.3 | async-start | bytes 2097152 | tf_op jit(solution)/shard_map/all_to_all | solution.py:45
  246.4 19.4 %collective-permute-start.2 = (bf16[32,64]{1,0:T(8,128)(2,1)S(1)}, bf16[32,64]{1,0:T(8,128)(2,1)S(1)}, u32[]{:S(2)}, u32[]{:S(2)}) collective-permute-start(bf16[32,64]{1,0:T(8,128)(2,1)S(1)} %get-tuple-element.31), channel_id=1, source_target_pairs={{0,1},{1,2},{2,3},{3,4},{4,5},{5,6},{6,7},{7,8},{8,9},{9,10},{10,1... | collective-permute-start | bytes 12296 | tf_op jit(solution)/shard_map/ppermute | solution.py:24
  248.3 18.0 %collective-permute-start.3 = (bf16[32,64]{1,0:T(8,128)(2,1)S(1)}, bf16[32,64]{1,0:T(8,128)(2,1)S(1)}, u32[]{:S(2)}, u32[]{:S(2)}) collective-permute-start(bf16[32,64]{1,0:T(8,128)(2,1)S(1)} %get-tuple-element.32), channel_id=1, source_target_pairs={{1,0},{2,1},{3,2},{4,3},{5,4},{6,5},{7,6},{8,7},{9,8},{10,9},{11,1... | collective-permute-start | bytes 12296 | tf_op jit(solution)/shard_map/ppermute | solution.py:26
  288.9 16.0 %all-to-all-start.5 = ((f32[32,3,32]{2,1,0:T(4,128)}), f32[32,3,32]{2,1,0:T(4,128)S(1)}, u32[]{:S(2)}, u32[]{:S(2)}) async-start(f32[32,3,32]{2,1,0:T(4,128)} %broadcast_in_dim.45), calls=%async_computation.5 | async-start | bytes 131072 | tf_op jit(solution)/shard_map/all_to_all | solution.py:37
  306.2 31.6 %all-to-all-start.6 = ((bf16[32,32,512]{2,1,0:T(8,128)(2,1)}), bf16[32,32,512]{2,1,0:T(8,128)(2,1)S(1)}, u32[]{:S(2)}, u32[]{:S(2)}) async-start(bf16[32,32,512]{2,1,0:T(8,128)(2,1)} %broadcast_in_dim.47), calls=%async_computation.6 | async-start | bytes 2097152 | tf_op jit(solution)/shard_map/all_to_all | solution.py:45
  312.2 19.3 %collective-permute-start.4 = (bf16[32,64]{1,0:T(8,128)(2,1)S(1)}, bf16[32,64]{1,0:T(8,128)(2,1)S(1)}, u32[]{:S(2)}, u32[]{:S(2)}) collective-permute-start(bf16[32,64]{1,0:T(8,128)(2,1)S(1)} %get-tuple-element.25), channel_id=1, source_target_pairs={{0,1},{1,2},{2,3},{3,4},{4,5},{5,6},{6,7},{7,8},{8,9},{9,10},{10,1... | collective-permute-start | bytes 12296 | tf_op jit(solution)/shard_map/ppermute | solution.py:24
  314.1 18.0 %collective-permute-start.5 = (bf16[32,64]{1,0:T(8,128)(2,1)S(1)}, bf16[32,64]{1,0:T(8,128)(2,1)S(1)}, u32[]{:S(2)}, u32[]{:S(2)}) collective-permute-start(bf16[32,64]{1,0:T(8,128)(2,1)S(1)} %get-tuple-element.26), channel_id=1, source_target_pairs={{1,0},{2,1},{3,2},{4,3},{5,4},{6,5},{7,6},{8,7},{9,8},{10,9},{11,1... | collective-permute-start | bytes 12296 | tf_op jit(solution)/shard_map/ppermute | solution.py:26
Sparse Core Ops, SparseCore 0:
  12.9 127.4 all-gather.1

commit v9 on v5

--- a/solution.py
+++ b/solution.py
@@ -47,7 +47,7 @@
     return lax.all_to_all(spread, "band", split_axis=0, concat_axis=0, tiled=True)
 
 
-SLOT_BLOCK = 8
+SLOT_BLOCK = 32
 
 
 def affinity_kernel(part_ref, lev_ref, own_ref, *refs):

time: 343 us -> 340 us (level)
  Pallas kernels: 13.7 us -> 9.01 us
    pallas_call x1, Pallas kernels: 13.7 us -> 9.01 us  [affinity_blocks(): pl.pallas_call(affinity_kernel, grid_spec=grid_spec, out_shape=[jax.Shape...]
  transfers between devices with their start and end apart: 12 -> 12, of which waited for: 10 -> 10; matrix products, arithmetic and copies ran while one was open for 8% -> 9% of each run, Pallas kernels for 0% -> 0%
where the time goes in v9:
time: 340 us; the launch traced here: 337 us
  waiting for transfers between devices  113 us (33%)
  blocking collectives  79.3 us (23%)
  starting transfers between devices  64.3 us (19%)
  local copies, waits for them, and re-layouts  32 us (9%)
  between operations  14.3 us (4%)
  other arithmetic  12.6 us (4%)
  matrix products  12.3 us (4%)
  Pallas kernels  9.01 us (3%)
    all_to_all x6, blocking collectives, total_over_devices(): rows = lax.all_to_all(spread, axis, split_axis=0, concat_axis=0, tiled=True)  79.3 us
    all_gather x1, waiting for transfers between devices, on_device(): gathered = lax.all_gather(embeddings, 'band', axis=0, tiled=True)  54.3 us
    all_to_all x4, waiting for transfers between devices, band_gather(): lax.all_to_all(spread, 'band', split_axis=0, concat_axis=0, tiled=True)  30.4 us
    all_to_all x4, starting transfers between devices, band_gather(): lax.all_to_all(spread, 'band', split_axis=0, concat_axis=0, tiled=True)  24.5 us
    ppermute x3, starting transfers between devices, with_halo(): lax.ppermute(head, axis, [((i + 1) % count, i) for i in range(ends)])  23.8 us
    ppermute x3, waiting for transfers between devices, with_halo(): lax.ppermute(tail, axis, [(i, (i + 1) % count) for i in range(ends)])  19.1 us
    all_to_all x1, starting transfers between devices, on_device(): lax.all_to_all(ordered, 'band', split_axis=1, concat_axis=1, tiled=True)  10.2 us
    pallas_call x1, Pallas kernels, affinity_blocks(): pl.pallas_call(affinity_kernel, grid_spec=grid_spec, out_shape=[jax.Shape...  9.01 us
  transfers between devices with their start and end apart: 12, of which 10 were waited for; matrix products, arithmetic and copies ran while one was open for 9% of the time, Pallas kernels for 0%

profile of v9, /device:TPU:6, one launch (start us, length us, event | category | flops | bytes accessed | tf_op | source)
XLA Modules:
  0.0 337.2 jit_solution(15338861169963367352)
XLA Ops:
  6.5 0.7 all-gather.2.cloned.1.call-update
  7.9 0.8 broadcast_multiply_fusion
  9.3 1.3 reduce.17
  11.5 1.3 gather_fusion
  13.0 0.8 reshape.836
  13.7 10.2 %all-to-all-start = ((bf16[32,2,256]{2,1,0:T(2,128)(2,1)}), bf16[32,2,256]{2,1,0:T(2,128)(2,1)S(1)}, u32[]{:S(2)}, u32[]{:S(2)}) async-start(bf16[32,2,256]{2,1,0:T(2,128)(2,1)} %reshape.836), calls=%async_computation | async-start | bytes 65536 | tf_op jit(solution)/shard_map/all_to_all | solution.py:114
  24.1 7.9 %all-to-all-done = bf16[32,2,256]{2,1,0:T(2,128)(2,1)S(1)} async-done(((bf16[32,2,256]{2,1,0:T(2,128)(2,1)}), bf16[32,2,256]{2,1,0:T(2,128)(2,1)S(1)}, u32[]{:S(2)}, u32[]{:S(2)}) %all-to-all-start) | async-done | bytes 32800 | tf_op jit(solution)/shard_map/all_to_all | solution.py:114
  32.3 1.2 broadcast_in_dim.40
  33.4 5.8 %all-to-all-start.1 = ((bf16[32,32,512]{2,1,0:T(8,128)(2,1)}), bf16[32,32,512]{2,1,0:T(8,128)(2,1)S(1)}, u32[]{:S(2)}, u32[]{:S(2)}) async-start(bf16[32,32,512]{2,1,0:T(8,128)(2,1)} %broadcast_in_dim.40), calls=%async_computation.1 | async-start | bytes 2097152 | tf_op jit(solution)/shard_map/all_to_all | solution.py:47
  39.3 6.8 %gather_fusion.3 = pred[1024]{0:T(1024)(128)(4,1)S(1)} fusion(pred[640]{0:T(1024)(128)(4,1)S(1)} %compare_and_fusion.1, s32[1024]{0:T(1024)S(1)} %broadcast_clamp_fusion), kind=kCustom, calls=%fused_computation.3 | custom fusion | bytes 6144 | tf_op jit(solution)/shard_map/gather | solution.py:131
  47.0 4.5 %gather_fusion.1 = s32[1024]{0:T(1024)S(1)} fusion(s32[640]{0:T(1024)S(1)} %convert_reduce_fusion, s32[1024]{0:T(1024)S(1)} %broadcast_clamp_fusion), kind=kCustom, calls=%fused_computation.1 | custom fusion | bytes 12288 | tf_op jit(solution)/shard_map/gather | solution.py:130
  51.6 2.3 gather_fusion.2
  54.9 16.7 %all-to-all-done.1 = bf16[32,32,512]{2,1,0:T(8,128)(2,1)S(1)} async-done(((bf16[32,32,512]{2,1,0:T(8,128)(2,1)}), bf16[32,32,512]{2,1,0:T(8,128)(2,1)S(1)}, u32[]{:S(2)}, u32[]{:S(2)}) %all-to-all-start.1) | async-done | bytes 1048608 | tf_op jit(solution)/shard_map/all_to_all | solution.py:47
  71.6 54.3 %all-gather.2.cloned.1.call-done = bf16[16384,256]{1,0:T(8,128)(2,1)} async-done(((bf16[512,256]{1,0:T(8,128)(2,1)}), bf16[16384,256]{1,0:T(8,128)(2,1)}) %all-gather.2.cloned.1.call-update) | async-done | bytes 8388624 | tf_op jit(solution)/shard_map/all_gather | solution.py:137
  125.9 9.0 %shard_map.73 = (bf16[4,32,128,128]{3,2,1,0:T(8,128)(2,1)}, f32[4,1,1,128]{3,2,1,0:T(1,128)}) custom-call(s32[4,32]{1,0:T(4,128)} %part_ref.1, s32[4,32]{1,0:T(4,128)} %lev_ref.1, bf16[4,128,256]{2,1,0:T(8,128)(2,1)} %bitcast.222, bf16[128,128,256]{2,1,0:T(8,128)(2,1)} %bitcast.192, bf16[128,128,256]{2,1,0:T(8,128)(2,1)} %bitcast.208, ...), custom_call_target="tpu_custom_call" | custom-call | tf_op jit(solution)/shard_map/pallas_call | solution.py:94
  135.7 1.9 collective-permute-start
  137.6 7.9 %collective-permute-start.1 = (bf16[32,64]{1,0:T(8,128)(2,1)S(1)}, bf16[32,64]{1,0:T(8,128)(2,1)S(1)}, u32[]{:S(2)}, u32[]{:S(2)}) collective-permute-start(bf16[32,64]{1,0:T(8,128)(2,1)S(1)} %get-tuple-element.46), channel_id=1, source_target_pairs={{1,0},{2,1},{3,2},{4,3},{5,4},{6,5},{7,6},{8,7},{9,8},{10,9},{11,1... | collective-permute-start | bytes 12296 | tf_op jit(solution)/shard_map/ppermute | solution.py:28
  146.1 7.1 %all-to-all-start.2 = ((f32[32,1,512]{2,1,0:T(1,128)}), f32[32,1,512]{2,1,0:T(1,128)S(1)}, u32[]{:S(2)}, u32[]{:S(2)}) async-start(f32[32,1,512]{2,1,0:T(1,128)} %mul.375), calls=%async_computation.2 | async-start | bytes 131072 | tf_op jit(solution)/shard_map/all_to_all | solution.py:47
  153.8 1.3 reduce.18
  155.9 5.4 %all-to-all-done.2 = f32[32,1,512]{2,1,0:T(1,128)S(1)} async-done(((f32[32,1,512]{2,1,0:T(1,128)}), f32[32,1,512]{2,1,0:T(1,128)S(1)}, u32[]{:S(2)}, u32[]{:S(2)}) %all-to-all-start.2) | async-done | bytes 65568 | tf_op jit(solution)/shard_map/all_to_all | solution.py:47
  163.6 0.8 gather_fusion.4
  164.4 2.9 fusion.3
  167.8 12.8 %all_to_all.56 = f32[16,1,128]{2,1,0:T(1,128)S(1)} all-to-all(f32[16,1,128]{2,1,0:T(1,128)S(1)} %reshape.838), channel_id=1, replica_groups=mesh['band'=32,'seq'=16] {'seq'}, dimensions={0} | all-to-all | bytes 16384 | tf_op jit(solution)/shard_map/all_to_all | solution.py:39
  181.9 12.9 %all_to_all.57 = f32[32,1,128]{2,1,0:T(1,128)S(1)} all-to-all(f32[32,1,128]{2,1,0:T(1,128)S(1)} %reshape.840), channel_id=1, replica_groups=mesh['band'=32,'seq'=16] {'band'}, dimensions={0} | all-to-all | bytes 32768 | tf_op jit(solution)/shard_map/all_to_all | solution.py:39
  196.4 1.1 broadcast_in_dim.44
  197.5 5.8 %all-to-all-start.5 = ((bf16[32,32,512]{2,1,0:T(8,128)(2,1)}), bf16[32,32,512]{2,1,0:T(8,128)(2,1)S(1)}, u32[]{:S(2)}, u32[]{:S(2)}) async-start(bf16[32,32,512]{2,1,0:T(8,128)(2,1)} %broadcast_in_dim.44), calls=%async_computation.5 | async-start | bytes 2097152 | tf_op jit(solution)/shard_map/all_to_all | solution.py:47
  203.3 1.9 collective-permute-start.2
  205.3 8.0 %collective-permute-start.3 = (bf16[32,64]{1,0:T(8,128)(2,1)S(1)}, bf16[32,64]{1,0:T(8,128)(2,1)S(1)}, u32[]{:S(2)}, u32[]{:S(2)}) collective-permute-start(bf16[32,64]{1,0:T(8,128)(2,1)S(1)} %get-tuple-element.40), channel_id=1, source_target_pairs={{1,0},{2,1},{3,2},{4,3},{5,4},{6,5},{7,6},{8,7},{9,8},{10,9},{11,1... | collective-permute-start | bytes 12296 | tf_op jit(solution)/shard_map/ppermute | solution.py:28
  213.3 9.4 %collective-permute-done.2 = bf16[32,64]{1,0:T(8,128)(2,1)S(1)} collective-permute-done((bf16[32,64]{1,0:T(8,128)(2,1)S(1)}, bf16[32,64]{1,0:T(8,128)(2,1)S(1)}, u32[]{:S(2)}, u32[]{:S(2)}) %collective-permute-start.2) | collective-permute-done | bytes 4128 | tf_op jit(solution)/shard_map/ppermute | solution.py:26
  223.4 1.4 fusion.15
  224.8 4.1 %all-to-all-done.5 = bf16[32,32,512]{2,1,0:T(8,128)(2,1)S(1)} async-done(((bf16[32,32,512]{2,1,0:T(8,128)(2,1)}), bf16[32,32,512]{2,1,0:T(8,128)(2,1)S(1)}, u32[]{:S(2)}, u32[]{:S(2)}) %all-to-all-start.5) | async-done | bytes 1048608 | tf_op jit(solution)/shard_map/all_to_all | solution.py:47
  230.9 1.0 gather_fusion.5
  232.0 2.9 fusion.2
  235.4 10.6 %all_to_all.58 = f32[16,3,32]{2,1,0:T(4,128)S(1)} all-to-all(f32[16,3,32]{2,1,0:T(4,128)S(1)} %broadcast_in_dim.45), channel_id=1, replica_groups=mesh['band'=32,'seq'=16] {'seq'}, dimensions={0} | all-to-all | bytes 12288 | tf_op jit(solution)/shard_map/all_to_all | solution.py:39
  246.0 16.5 %all_to_all.59 = f32[32,3,32]{2,1,0:T(4,128)S(1)} all-to-all(f32[32,3,32]{2,1,0:T(4,128)S(1)} %broadcast_in_dim.46), channel_id=1, replica_groups=mesh['band'=32,'seq'=16] {'band'}, dimensions={0} | all-to-all | bytes 24576 | tf_op jit(solution)/shard_map/all_to_all | solution.py:39
  263.1 0.7 multiply_convert_fusion.1
  263.8 1.1 broadcast_in_dim.47
  264.9 5.8 %all-to-all-start.8 = ((bf16[32,32,512]{2,1,0:T(8,128)(2,1)}), bf16[32,32,512]{2,1,0:T(8,128)(2,1)S(1)}, u32[]{:S(2)}, u32[]{:S(2)}) async-start(bf16[32,32,512]{2,1,0:T(8,128)(2,1)} %broadcast_in_dim.47), calls=%async_computation.8 | async-start | bytes 2097152 | tf_op jit(solution)/shard_map/all_to_all | solution.py:47
  270.8 1.9 collective-permute-start.4
  272.7 7.9 %collective-permute-start.5 = (bf16[32,64]{1,0:T(8,128)(2,1)S(1)}, bf16[32,64]{1,0:T(8,128)(2,1)S(1)}, u32[]{:S(2)}, u32[]{:S(2)}) collective-permute-start(bf16[32,64]{1,0:T(8,128)(2,1)S(1)} %get-tuple-element.34), channel_id=1, source_target_pairs={{1,0},{2,1},{3,2},{4,3},{5,4},{6,5},{7,6},{8,7},{9,8},{10,9},{11,1... | collective-permute-start | bytes 12296 | tf_op jit(solution)/shard_map/ppermute | solution.py:28
  280.6 9.6 %collective-permute-done.4 = bf16[32,64]{1,0:T(8,128)(2,1)S(1)} collective-permute-done((bf16[32,64]{1,0:T(8,128)(2,1)S(1)}, bf16[32,64]{1,0:T(8,128)(2,1)S(1)}, u32[]{:S(2)}, u32[]{:S(2)}) %collective-permute-start.4) | collective-permute-done | bytes 4128 | tf_op jit(solution)/shard_map/ppermute | solution.py:26
  290.9 1.4 fusion.16
  292.4 4.1 %all-to-all-done.8 = bf16[32,32,512]{2,1,0:T(8,128)(2,1)S(1)} async-done(((bf16[32,32,512]{2,1,0:T(8,128)(2,1)}), bf16[32,32,512]{2,1,0:T(8,128)(2,1)S(1)}, u32[]{:S(2)}, u32[]{:S(2)}) %all-to-all-start.8) | async-done | bytes 1048608 | tf_op jit(solution)/shard_map/all_to_all | solution.py:47
  298.5 1.0 gather_fusion.6
  299.5 2.9 fusion.1
  302.9 10.4 %all_to_all.60 = f32[16,1,32]{2,1,0:T(1,128)S(1)} all-to-all(f32[16,1,32]{2,1,0:T(1,128)S(1)} %broadcast_in_dim.48), channel_id=1, replica_groups=mesh['band'=32,'seq'=16] {'seq'}, dimensions={0} | all-to-all | bytes 4096 | tf_op jit(solution)/shard_map/all_to_all | solution.py:39
  313.3 16.2 %all_to_all.61 = f32[32,1,32]{2,1,0:T(1,128)S(1)} all-to-all(f32[32,1,32]{2,1,0:T(1,128)S(1)} %broadcast_in_dim.49), channel_id=1, replica_groups=mesh['band'=32,'seq'=16] {'band'}, dimensions={0} | all-to-all | bytes 8192 | tf_op jit(solution)/shard_map/all_to_all | solution.py:39
  329.7 0.7 fusion.19
  (172 shorter events, 19.6 us)
Async XLA Ops:
  6.5 39.6 %copy-start.35 = (s32[256]{0:T(256)S(1)}, s32[256]{0:T(256)}, u32[]{:S(2)}) copy-start(s32[256]{0:T(256)} %param.10) | copy-start | bytes 3076
  6.5 119.4 %all-gather.2.cloned.1.call-start = ((), (), s32[]{:S(2)}) async-start(), calls=%async_computation.11 | async-start | bytes 8650752 | tf_op jit(solution)/shard_map/all_gather | solution.py:137
  13.7 18.3 %all-to-all-start = ((bf16[32,2,256]{2,1,0:T(2,128)(2,1)}), bf16[32,2,256]{2,1,0:T(2,128)(2,1)S(1)}, u32[]{:S(2)}, u32[]{:S(2)}) async-start(bf16[32,2,256]{2,1,0:T(2,128)(2,1)} %reshape.836), calls=%async_computation | async-start | bytes 65536 | tf_op jit(solution)/shard_map/all_to_all | solution.py:114
  32.2 164.0 %copy-start.5 = (bf16[32,512]{1,0:T(8,128)(2,1)}, bf16[32,512]{1,0:T(8,128)(2,1)S(1)}, u32[]{:S(2)}) copy-start(bf16[32,512]{1,0:T(8,128)(2,1)S(1)} %copy.72) | copy-start | bytes 98308
  33.4 38.2 %all-to-all-start.1 = ((bf16[32,32,512]{2,1,0:T(8,128)(2,1)}), bf16[32,32,512]{2,1,0:T(8,128)(2,1)S(1)}, u32[]{:S(2)}, u32[]{:S(2)}) async-start(bf16[32,32,512]{2,1,0:T(8,128)(2,1)} %broadcast_in_dim.40), calls=%async_computation.1 | async-start | bytes 2097152 | tf_op jit(solution)/shard_map/all_to_all | solution.py:47
  39.2 14.7 %copy-start.23 = (s32[4,32]{1,0:T(4,128)S(1)}, s32[4,32]{1,0:T(4,128)}, u32[]{:S(2)}) copy-start(s32[4,32]{1,0:T(4,128)} %part_ref.1) | copy-start | bytes 1540
  46.1 177.3 %copy-start.36 = (pred[4,256]{1,0:T(4,128)(4,1)}, pred[4,256]{1,0:T(4,128)(4,1)S(1)}, u32[]{:S(2)}) copy-start(pred[4,256]{1,0:T(4,128)(4,1)S(1)} %and.33) | copy-start | bytes 3076
  53.9 169.4 %copy-start.33 = (s32[512]{0:T(512)}, s32[512]{0:T(512)S(1)}, u32[]{:S(2)}) copy-start(s32[512]{0:T(512)S(1)} %gather_fusion.2) | copy-start | bytes 6148
  53.9 169.4 %copy-start.28 = (s32[4,256]{1,0:T(4,128)}, s32[4,256]{1,0:T(4,128)S(1)}, u32[]{:S(2)}) copy-start(s32[4,256]{1,0:T(4,128)S(1)} %eq.17) | copy-start | bytes 12292
  54.1 169.2 %copy-start.31 = (s32[4,128]{1,0:T(4,128)}, s32[4,128]{1,0:T(4,128)S(1)}, u32[]{:S(2)}) copy-start(s32[4,128]{1,0:T(4,128)S(1)} %iota_add_fusion.2) | copy-start | bytes 6148
  54.2 169.2 %copy-start.26 = (s32[4,256]{1,0:T(4,128)}, s32[4,256]{1,0:T(4,128)S(1)}, u32[]{:S(2)}) copy-start(s32[4,256]{1,0:T(4,128)S(1)} %iota_add_fusion.1) | copy-start | bytes 12292
  54.9 108.7 %copy-start.14 = (s32[1024]{0:T(1024)}, s32[1024]{0:T(1024)S(1)}, u32[]{:S(2)}) copy-start(s32[1024]{0:T(1024)S(1)} %pad_clamp_fusion) | copy-start | bytes 12292
  135.6 60.7 %copy-start.9 = (f32[512]{0:T(512)}, f32[512]{0:T(512)S(1)}, u32[]{:S(2)}) copy-start(f32[512]{0:T(512)S(1)} %get-tuple-element.25) | copy-start | bytes 6148
  135.6 60.7 %copy-start.11 = (f32[512]{0:T(512)}, f32[512]{0:T(512)S(1)}, u32[]{:S(2)}) copy-start(f32[512]{0:T(512)S(1)} %get-tuple-element.24) | copy-start | bytes 6148
  135.7 19.5 %collective-permute-start = (bf16[32,64]{1,0:T(8,128)(2,1)S(1)}, bf16[32,64]{1,0:T(8,128)(2,1)S(1)}, u32[]{:S(2)}, u32[]{:S(2)}) collective-permute-start(bf16[32,64]{1,0:T(8,128)(2,1)S(1)} %get-tuple-element.45), channel_id=1, source_target_pairs={{0,1},{1,2},{2,3},{3,4},{4,5},{5,6},{6,7},{7,8},{8,9},{9,10},{10,1... | collective-permute-start | bytes 12296 | tf_op jit(solution)/shard_map/ppermute | solution.py:26
  137.6 17.6 %collective-permute-start.1 = (bf16[32,64]{1,0:T(8,128)(2,1)S(1)}, bf16[32,64]{1,0:T(8,128)(2,1)S(1)}, u32[]{:S(2)}, u32[]{:S(2)}) collective-permute-start(bf16[32,64]{1,0:T(8,128)(2,1)S(1)} %get-tuple-element.46), channel_id=1, source_target_pairs={{1,0},{2,1},{3,2},{4,3},{5,4},{6,5},{7,6},{8,7},{9,8},{10,9},{11,1... | collective-permute-start | bytes 12296 | tf_op jit(solution)/shard_map/ppermute | solution.py:28
  146.1 15.2 %all-to-all-start.2 = ((f32[32,1,512]{2,1,0:T(1,128)}), f32[32,1,512]{2,1,0:T(1,128)S(1)}, u32[]{:S(2)}, u32[]{:S(2)}) async-start(f32[32,1,512]{2,1,0:T(1,128)} %mul.375), calls=%async_computation.2 | async-start | bytes 131072 | tf_op jit(solution)/shard_map/all_to_all | solution.py:47
  167.3 30.1 %copy-start.2 = (f32[4,128,32]{1,2,0:T(8,128)}, f32[4,128,32]{1,2,0:T(8,128)S(1)}, u32[]{:S(2)}) copy-start(f32[4,128,32]{1,2,0:T(8,128)S(1)} %fusion.3) | copy-start | bytes 196612
  196.2 32.6 %copy-start.15 = (f32[32]{0:T(128)}, f32[32]{0:T(128)S(1)}, u32[]{:S(2)}) copy-start(f32[32]{0:T(128)S(1)} %get-tuple-element.26) | copy-start | bytes 388
  196.2 32.6 %copy-start.18 = (f32[32]{0:T(128)}, f32[32]{0:T(128)S(1)}, u32[]{:S(2)}) copy-start(f32[32]{0:T(128)S(1)} %get-tuple-element.28) | copy-start | bytes 388
  197.5 31.4 %all-to-all-start.5 = ((bf16[32,32,512]{2,1,0:T(8,128)(2,1)}), bf16[32,32,512]{2,1,0:T(8,128)(2,1)S(1)}, u32[]{:S(2)}, u32[]{:S(2)}) async-start(bf16[32,32,512]{2,1,0:T(8,128)(2,1)} %broadcast_in_dim.44), calls=%async_computation.5 | async-start | bytes 2097152 | tf_op jit(solution)/shard_map/all_to_all | solution.py:47
  203.3 19.4 %collective-permute-start.2 = (bf16[32,64]{1,0:T(8,128)(2,1)S(1)}, bf16[32,64]{1,0:T(8,128)(2,1)S(1)}, u32[]{:S(2)}, u32[]{:S(2)}) collective-permute-start(bf16[32,64]{1,0:T(8,128)(2,1)S(1)} %get-tuple-element.39), channel_id=1, source_target_pairs={{0,1},{1,2},{2,3},{3,4},{4,5},{5,6},{6,7},{7,8},{8,9},{9,10},{10,1... | collective-permute-start | bytes 12296 | tf_op jit(solution)/shard_map/ppermute | solution.py:26
  205.3 18.0 %collective-permute-start.3 = (bf16[32,64]{1,0:T(8,128)(2,1)S(1)}, bf16[32,64]{1,0:T(8,128)(2,1)S(1)}, u32[]{:S(2)}, u32[]{:S(2)}) collective-permute-start(bf16[32,64]{1,0:T(8,128)(2,1)S(1)} %get-tuple-element.40), channel_id=1, source_target_pairs={{1,0},{2,1},{3,2},{4,3},{5,4},{6,5},{7,6},{8,7},{9,8},{10,9},{11,1... | collective-permute-start | bytes 12296 | tf_op jit(solution)/shard_map/ppermute | solution.py:28
  230.8 4.2 %copy-start.16 = (f32[32]{0:T(128)S(1)}, f32[32]{0:T(128)}, u32[]{:S(2)}) copy-start(f32[32]{0:T(128)} %copy-done.15) | copy-start | bytes 388
  230.9 4.2 %copy-start.19 = (f32[32]{0:T(128)S(1)}, f32[32]{0:T(128)}, u32[]{:S(2)}) copy-start(f32[32]{0:T(128)} %copy-done.18) | copy-start | bytes 388
  230.9 31.6 %copy-start.30 = (f32[32]{0:T(128)S(1)}, f32[32]{0:T(128)}, u32[]{:S(2)}) copy-start(f32[32]{0:T(128)} %get-tuple-element.27) | copy-start | bytes 388
  230.9 32.2 %copy-start.3 = (f32[4,128,32]{1,2,0:T(8,128)S(1)}, f32[4,128,32]{1,2,0:T(8,128)}, u32[]{:S(2)}) copy-start(f32[4,128,32]{1,2,0:T(8,128)} %copy-done.2) | copy-start | bytes 196612
  230.9 32.2 %copy-start.6 = (bf16[32,512]{1,0:T(8,128)(2,1)S(1)}, bf16[32,512]{1,0:T(8,128)(2,1)}, u32[]{:S(2)}) copy-start(bf16[32,512]{1,0:T(8,128)(2,1)} %copy-done.5) | copy-start | bytes 98308
  230.9 32.2 %copy-start.10 = (f32[512]{0:T(512)S(1)}, f32[512]{0:T(512)}, u32[]{:S(2)}) copy-start(f32[512]{0:T(512)} %copy-done.9) | copy-start | bytes 6148
  230.9 32.2 %copy-start.12 = (f32[512]{0:T(512)S(1)}, f32[512]{0:T(512)}, u32[]{:S(2)}) copy-start(f32[512]{0:T(512)} %copy-done.11) | copy-start | bytes 6148
  231.9 59.0 %copy-start.27 = (s32[4,256]{1,0:T(4,128)S(1)}, s32[4,256]{1,0:T(4,128)}, u32[]{:S(2)}) copy-start(s32[4,256]{1,0:T(4,128)} %copy-done.26) | copy-start | bytes 12292
  231.9 59.0 %copy-start.29 = (s32[4,256]{1,0:T(4,128)S(1)}, s32[4,256]{1,0:T(4,128)}, u32[]{:S(2)}) copy-start(s32[4,256]{1,0:T(4,128)} %copy-done.28) | copy-start | bytes 12292
  231.9 59.0 %copy-start.32 = (s32[4,128]{1,0:T(4,128)S(1)}, s32[4,128]{1,0:T(4,128)}, u32[]{:S(2)}) copy-start(s32[4,128]{1,0:T(4,128)} %copy-done.31) | copy-start | bytes 6148
  232.0 59.0 %copy-start.34 = (s32[512]{0:T(512)S(1)}, s32[512]{0:T(512)}, u32[]{:S(2)}) copy-start(s32[512]{0:T(512)} %copy-done.33) | copy-start | bytes 6148
  232.0 59.0 %copy-start.37 = (pred[4,256]{1,0:T(4,128)(4,1)S(1)}, pred[4,256]{1,0:T(4,128)(4,1)}, u32[]{:S(2)}) copy-start(pred[4,256]{1,0:T(4,128)(4,1)} %copy-done.36) | copy-start | bytes 3076
  235.1 29.8 %copy-start = (f32[32,4,128]{0,2,1:T(8,128)}, f32[32,4,128]{0,2,1:T(8,128)S(1)}, u32[]{:S(2)}) copy-start(f32[32,4,128]{0,2,1:T(8,128)S(1)} %copy.82) | copy-start | bytes 196612
  263.0 27.2 %copy-start.21 = (f32[32]{0:T(128)}, f32[32]{0:T(128)S(1)}, u32[]{:S(2)}) copy-start(f32[32]{0:T(128)S(1)} %get-tuple-element.23) | copy-start | bytes 388
  264.9 31.6 %all-to-all-start.8 = ((bf16[32,32,512]{2,1,0:T(8,128)(2,1)}), bf16[32,32,512]{2,1,0:T(8,128)(2,1)S(1)}, u32[]{:S(2)}, u32[]{:S(2)}) async-start(bf16[32,32,512]{2,1,0:T(8,128)(2,1)} %broadcast_in_dim.47), calls=%async_computation.8 | async-start | bytes 2097152 | tf_op jit(solution)/shard_map/all_to_all | solution.py:47
  270.8 19.4 %collective-permute-start.4 = (bf16[32,64]{1,0:T(8,128)(2,1)S(1)}, bf16[32,64]{1,0:T(8,128)(2,1)S(1)}, u32[]{:S(2)}, u32[]{:S(2)}) collective-permute-start(bf16[32,64]{1,0:T(8,128)(2,1)S(1)} %get-tuple-element.33), channel_id=1, source_target_pairs={{0,1},{1,2},{2,3},{3,4},{4,5},{5,6},{6,7},{7,8},{8,9},{9,10},{10,1... | collective-permute-start | bytes 12296 | tf_op jit(solution)/shard_map/ppermute | solution.py:26
  272.7 18.1 %collective-permute-start.5 = (bf16[32,64]{1,0:T(8,128)(2,1)S(1)}, bf16[32,64]{1,0:T(8,128)(2,1)S(1)}, u32[]{:S(2)}, u32[]{:S(2)}) collective-permute-start(bf16[32,64]{1,0:T(8,128)(2,1)S(1)} %get-tuple-element.34), channel_id=1, source_target_pairs={{1,0},{2,1},{3,2},{4,3},{5,4},{6,5},{7,6},{8,7},{9,8},{10,9},{11,1... | collective-permute-start | bytes 12296 | tf_op jit(solution)/shard_map/ppermute | solution.py:28
  298.4 4.2 %copy-start.1 = (f32[32,4,128]{0,2,1:T(8,128)S(1)}, f32[32,4,128]{0,2,1:T(8,128)}, u32[]{:S(2)}) copy-start(f32[32,4,128]{0,2,1:T(8,128)} %copy-done) | copy-start | bytes 196612
  298.4 4.2 %copy-start.17 = (f32[32]{0:T(128)S(1)}, f32[32]{0:T(128)}, u32[]{:S(2)}) copy-start(f32[32]{0:T(128)} %copy-done.15) | copy-start | bytes 388
  298.4 4.2 %copy-start.20 = (f32[32]{0:T(128)S(1)}, f32[32]{0:T(128)}, u32[]{:S(2)}) copy-start(f32[32]{0:T(128)} %copy-done.18) | copy-start | bytes 388
  298.5 31.1 %copy-start.38 = (f32[32]{0:T(128)S(1)}, f32[32]{0:T(128)}, u32[]{:S(2)}) copy-start(f32[32]{0:T(128)} %get-tuple-element.22) | copy-start | bytes 388
  298.5 31.1 %copy-start.4 = (f32[4,128,32]{1,2,0:T(8,128)S(1)}, f32[4,128,32]{1,2,0:T(8,128)}, u32[]{:S(2)}) copy-start(f32[4,128,32]{1,2,0:T(8,128)} %copy-done.2) | copy-start | bytes 196612
  298.5 31.1 %copy-start.7 = (bf16[32,512]{1,0:T(8,128)(2,1)S(1)}, bf16[32,512]{1,0:T(8,128)(2,1)}, u32[]{:S(2)}) copy-start(bf16[32,512]{1,0:T(8,128)(2,1)} %copy-done.5) | copy-start | bytes 98308
  298.5 31.1 %copy-start.8 = (f32[32,512]{1,0:T(8,128)S(1)}, f32[32,512]{1,0:T(8,128)}, u32[]{:S(2)}) copy-start(f32[32,512]{1,0:T(8,128)} %get-tuple-element.20) | copy-start | bytes 196612
  298.5 31.1 %copy-start.13 = (f32[512]{0:T(512)S(1)}, f32[512]{0:T(512)}, u32[]{:S(2)}) copy-start(f32[512]{0:T(512)} %copy-done.11) | copy-start | bytes 6148
  (3 other events, 10.3 us)
Sparse Core Ops, SparseCore 0:
  10.5 115.3 all-gather.1
